TPU v7x, 256 devices: a whole 4x4x8 slice. The times are simulated.
256 devices in a mesh: ctx: 32 (over z_hi, x, y), head: 8 (over z_lo, core).
Axes of the slice: x: 4, y: 4, z: 8 (z_hi: 2, z_lo: 4; z = z_hi * 4 + z_lo), core: 2. Of those that a mesh axis runs over, the one named last changes fastest.
Arguments:
- queries: bfloat16 [12288, 4096], P('ctx', 'head'), may hold values from -200 to 200
- key_matrix: bfloat16 [12288, 1024], P('ctx', 'head'), may hold values from -6 to 6
- value_matrix: bfloat16 [12288, 1024], P('ctx', 'head'), may hold values from -6 to 6
- doc_ids: int32 [12288], P('ctx'), may hold values from 0 to 15, never falling along the last dimension, each value on 1 to 6528 neighbouring positions
- out_weight: bfloat16 [4096, 4096], P('head'), may hold values from -0.09375 to 0.09375
Outputs:
- projected: bfloat16 [12288, 4096], P(('ctx', 'head'))
Inputs may be any that keep to these rules, and one draw needn't show every extreme that they name: `doc_ids`: document ids never fall along the tokens; each document has 1 to 6528 tokens and one has exactly 6528.
All inputs are finite; a program needn't handle non-finite values.
Results may differ from a plain program's by a relative error of at most 0.019.
Values may be sent and summed in bfloat16 or wider, within the bound.
No kernel may reach another device: no remote copies, remote signals or barrier semaphores. Data moves between devices by JAX's collectives and lax.ppermute only.
A program may use at most 256 MiB of HBM per device.

v0:
```python
import functools

import jax
import jax.numpy as jnp
import numpy as np
from jax import lax
from jax.experimental import pallas as pl
from jax.experimental.pallas import tpu as pltpu
from jax.sharding import Mesh, PartitionSpec as P

HEAD_WIDTH = 128
LANES = 128
MOST = 6528
DOCS = 16
NEG = -1e30
CHUNKS = 2


def attn_kernel(
    steps, shard_rows, heads, scale, sc_ref, q_ref, k_ref, v_ref, qs_ref, qp_ref, after_ref, o_ref, m_sc, l_sc, acc_sc
):
    j = pl.program_id(0)
    me = sc_ref[0]
    first = sc_ref[1]
    q_last_start = sc_ref[2]
    shard = me - (steps - 1) + j
    rows = q_ref.shape[0]

    @pl.when(j == 0)
    def _init():
        m_sc[...] = jnp.full(m_sc.shape, NEG, jnp.float32)
        l_sc[...] = jnp.zeros(l_sc.shape, jnp.float32)
        acc_sc[...] = jnp.zeros(acc_sc.shape, jnp.float32)

    def block(masked):
        cols = shard_rows // LANES
        if masked:
            lane = lax.broadcasted_iota(jnp.int32, (rows, LANES), 1)
            allowed = []
            for c in range(cols):
                k_pos = shard * shard_rows + c * LANES + lane
                allowed.append((k_pos >= qs_ref[:, 0:1]) & (k_pos <= qp_ref[:, 0:1]))
        for h in range(heads):
            qh = q_ref[:, h * HEAD_WIDTH:(h + 1) * HEAD_WIDTH]
            s = []
            for c in range(cols):
                s_c = jnp.dot(qh, k_ref[c * LANES:(c + 1) * LANES, :], preferred_element_type=jnp.float32)
                if masked:
                    s_c = jnp.where(allowed[c], s_c, NEG)
                s.append(s_c)
            top = s[0]
            for c in range(1, cols):
                top = jnp.maximum(top, s[c])
            m_prev = m_sc[h]
            m_next = jnp.maximum(m_prev, jnp.max(top, axis=1, keepdims=True))
            m_b = m_next[:, 0:1]
            part = None
            pv = None
            for c in range(cols):
                p = jnp.exp((s[c] - m_b) * scale)
                if masked:
                    p = jnp.where(allowed[c], p, 0.0)
                part = p if part is None else part + p
                term = jnp.dot(
                    p.astype(jnp.bfloat16), v_ref[c * LANES:(c + 1) * LANES, :], preferred_element_type=jnp.float32
                )
                pv = term if pv is None else pv + term
            alpha = jnp.exp((m_prev - m_next) * scale)
            l_sc[h] = alpha * l_sc[h] + part
            acc_sc[h] = alpha[:, 0:1] * acc_sc[h] + pv
            m_sc[h] = m_next

    live = shard >= first
    full = (shard < me) & (shard * shard_rows >= q_last_start)

    @pl.when(live & full)
    def _full():
        block(False)

    @pl.when(live & jnp.logical_not(full))
    def _masked():
        block(True)

    @pl.when(j == steps - 1)
    def _finish():
        for h in range(heads):
            denominator = jnp.sum(l_sc[h], axis=1, keepdims=True)
            o_ref[:, h * HEAD_WIDTH:(h + 1) * HEAD_WIDTH] = (acc_sc[h] / denominator).astype(o_ref.dtype)


def attention(scalars, queries, kv, q_start, q_pos, after, n_xy, shard_rows):
    rows, width = queries.shape
    heads = width // HEAD_WIDTH
    steps = -(-(MOST - 1) // shard_rows) + 1
    scale = HEAD_WIDTH ** (-0.5)

    def index(j, sc, half):
        s = jnp.maximum(sc[0] - (steps - 1) + j, sc[1])
        slot = jnp.where(s // n_xy == sc[3], 0, 1)
        return (s % n_xy, slot, 0, half)

    kernel = functools.partial(attn_kernel, steps, shard_rows, heads, scale)
    return pl.pallas_call(
        kernel,
        out_shape=jax.ShapeDtypeStruct((rows, width), jnp.bfloat16),
        grid_spec=pltpu.PrefetchScalarGridSpec(
            num_scalar_prefetch=1,
            grid=(steps,),
            in_specs=[
                pl.BlockSpec((rows, width), lambda j, sc: (0, 0)),
                pl.BlockSpec((None, None, shard_rows, HEAD_WIDTH), lambda j, sc: index(j, sc, 0)),
                pl.BlockSpec((None, None, shard_rows, HEAD_WIDTH), lambda j, sc: index(j, sc, 1)),
                pl.BlockSpec((rows, LANES), lambda j, sc: (0, 0)),
                pl.BlockSpec((rows, LANES), lambda j, sc: (0, 0)),
                pl.BlockSpec(memory_space=pl.ANY),
            ],
            out_specs=pl.BlockSpec((rows, width), lambda j, sc: (0, 0)),
            scratch_shapes=[
                pltpu.VMEM((heads, rows, LANES), jnp.float32),
                pltpu.VMEM((heads, rows, LANES), jnp.float32),
                pltpu.VMEM((heads, rows, HEAD_WIDTH), jnp.float32),
            ],
        ),
        compiler_params=pltpu.CompilerParams(dimension_semantics=("arbitrary",)),
        cost_estimate=pl.CostEstimate(
            flops=4 * steps * heads * rows * shard_rows * HEAD_WIDTH,
            transcendentals=steps * heads * rows * shard_rows,
            bytes_accessed=steps * shard_rows * 2 * HEAD_WIDTH * 2 + 2 * rows * width * 2,
        ),
    )(scalars, queries, kv, kv, q_start, q_pos, after)


def sum_over_heads(projected, n_head, piece):
    me_head = lax.axis_index("head")
    held = projected.reshape((n_head // 2, 2, piece) + projected.shape[1:]).astype(jnp.float32)
    core = me_head % 2
    keep = lax.dynamic_index_in_dim(held, core, axis=1, keepdims=False)
    send = lax.dynamic_index_in_dim(held, 1 - core, axis=1, keepdims=False)
    got = lax.ppermute(send.astype(jnp.bfloat16), "head", perm=[(i, i ^ 1) for i in range(n_head)])
    held = keep + got.astype(jnp.float32)
    chip = me_head // 2
    total = lax.dynamic_index_in_dim(held, chip, axis=0, keepdims=False)
    for k in range(1, n_head // 2):
        send = lax.dynamic_index_in_dim(held, chip ^ k, axis=0, keepdims=False)
        got = lax.ppermute(send.astype(jnp.bfloat16), "head", perm=[(i, i ^ (2 * k)) for i in range(n_head)])
        total = total + got.astype(jnp.float32)
    return total.astype(jnp.bfloat16)


def per_device(n_xy, n_head, queries, key_matrix, value_matrix, doc_ids, out_weight):
    rows = queries.shape[0]
    zh = lax.axis_index("zh")
    me = zh * n_xy + lax.axis_index("xy")

    width = key_matrix.shape[1]
    k_t = key_matrix.T.reshape(width, rows // LANES, LANES).transpose(1, 0, 2).reshape(rows, width)
    kv = jnp.concatenate([k_t, value_matrix], axis=1)
    lanes = kv.shape[1]
    tile = 8
    ids = jnp.full((tile * lanes,), -1.0, jnp.float32).at[:rows].set(doc_ids.astype(jnp.float32))
    block = jnp.concatenate([kv, ids.reshape(tile, lanes).astype(kv.dtype)], axis=0)

    partner = lax.ppermute(block, "zh", perm=[(0, 1), (1, 0)])
    pair = jnp.stack([block, partner])
    gathered = lax.all_gather(pair, "xy")

    id_rows = gathered[:, :, rows:, :].astype(jnp.float32)
    docs = jnp.arange(DOCS, dtype=jnp.float32)
    counts = jnp.sum((id_rows[..., None] == docs).astype(jnp.float32), axis=(0, 1, 2, 3))
    below = (jnp.arange(DOCS, dtype=jnp.int32)[None, :] < doc_ids[:, None]).astype(jnp.float32)
    q_start = jnp.sum(below * counts[None, :], axis=1).astype(jnp.int32)
    q_pos = me * rows + jnp.arange(rows, dtype=jnp.int32)

    per_head = rows // n_head
    piece = per_head // CHUNKS

    def chunk_of(x, c):
        x = x.reshape((n_head, CHUNKS, piece) + x.shape[1:])[:, c]
        return x.reshape((n_head * piece,) + x.shape[2:])

    outs = []
    after = jnp.zeros((8, LANES), jnp.bfloat16)
    for c in range(CHUNKS):
        qs_c = chunk_of(q_start, c)
        qp_c = chunk_of(q_pos, c)
        first = jnp.maximum(qs_c[0] // rows, 0)
        scalars = jnp.stack([me, first, qs_c[-1], zh]).astype(jnp.int32)
        attended = attention(
            scalars,
            chunk_of(queries, c),
            gathered,
            jnp.broadcast_to(qs_c[:, None], (qs_c.shape[0], LANES)),
            jnp.broadcast_to(qp_c[:, None], (qp_c.shape[0], LANES)),
            after,
            n_xy,
            rows,
        )
        projected = jnp.dot(attended, out_weight, preferred_element_type=jnp.float32).astype(jnp.bfloat16)
        after = projected
        outs.append(sum_over_heads(projected, n_head, piece))
    return jnp.concatenate(outs, axis=0)


def solution(mesh):
    n_ctx = mesh.shape["ctx"]
    n_head = mesh.shape["head"]
    n_zh = 2
    n_xy = n_ctx // n_zh
    devices = np.asarray(mesh.devices).reshape(n_zh, n_xy, n_head)
    inner = Mesh(devices, ("zh", "xy", "head"))
    ctx = ("zh", "xy")
    placed = (P(ctx, "head"), P(ctx, "head"), P(ctx, "head"), P(ctx), P("head", None))
    return jax.shard_map(
        functools.partial(per_device, n_xy, n_head),
        mesh=inner,
        in_specs=placed,
        out_specs=P(("zh", "xy", "head"), None),
        check_vma=False,
    )
```

profile of v0, /device:TPU:148, one launch (start us, length us, event | category | flops | bytes accessed | tf_op | source)
XLA Modules:
  0.0 207.8 jit_solution(5830922342795083461)
XLA Ops:
  6.5 0.0 all-gather.3.cloned.1.call-start
  6.5 0.8 convert_convert_fusion
  7.3 1.0 copy.16
  8.3 0.9 fusion.14
  9.3 0.1 collective-permute-start
  9.4 14.2 %collective-permute-done = bf16[392,256]{1,0:T(8,128)(2,1)S(1)} collective-permute-done((bf16[392,256]{1,0:T(8,128)(2,1)S(1)}, bf16[392,256]{1,0:T(8,128)(2,1)S(1)}, u32[]{:S(2)}, u32[]{:S(2)}) %collective-permute-start) | collective-permute-done | bytes 200736 | tf_op jit(solution)/shard_map/ppermute | solution.py:163
  23.6 0.8 pad_maximum_fusion
  24.4 0.0 all-gather.3.cloned.1.call-update
  24.5 1.8 fusion.15
  26.3 65.2 %all-gather.3.cloned.1.call-done = bf16[32,392,256]{2,1,0:T(8,128)(2,1)} async-done(((bf16[2,392,256]{2,1,0:T(8,128)(2,1)}), bf16[32,392,256]{2,1,0:T(8,128)(2,1)}) %all-gather.3.cloned.1.call-update) | async-done | bytes 6422544 | tf_op jit(solution)/shard_map/all_gather | solution.py:165
  91.4 0.9 slice_convert_fusion
  92.4 0.7 convert_reduce_fusion
  93.0 0.0 copy-done.3
  93.0 0.1 select_reduce_fusion
  93.1 0.1 convert_element_type.122
  93.3 0.1 reshape_squeeze.14
  93.4 0.6 fusion.17
  95.9 0.1 reshape_squeeze.12
  95.9 0.6 fusion.16
  98.3 0.1 broadcast_in_dim.38
  98.4 0.1 broadcast_in_dim.15
  98.5 1.3 add_add_fusion.2.sc_ref
  99.7 1.3 add_add_fusion.1.sc_ref
  101.0 0.7 broadcast_in_dim.14.qs_ref
  101.7 0.7 broadcast_in_dim.16.qp_ref
  102.5 0.6 broadcast_in_dim.17.after_ref
  103.1 23.2 %shard_map.55 = bf16[192,512]{1,0:T(8,128)(2,1)} custom-call(s32[4]{0:T(128)} %add_add_fusion.1.sc_ref, bf16[192,512]{1,0:T(8,128)(2,1)} %bitcast.85, bf16[16,2,392,256]{3,2,1,0:T(8,128)(2,1)} %bitcast.78, bf16[16,2,392,256]{3,2,1,0:T(8,128)(2,1)} %bitcast.79, s32[192,128]{1,0:T(8,128)} %broadcast_in_dim.14.qs_ref, s32[192,128]{1,0:T(8,128)} %broadcast_in_dim.16.qp_ref, ...), custom_call_target="tpu_custom_call" | custom-call | flops 2717908992 | bytes 3932160 | tf_op jit(solution)/shard_map/pallas_call | solution.py:103
  126.3 4.4 %convolution_convert_fusion.1.after_ref = bf16[192,4096]{1,0:T(8,128)(2,1)} fusion(bf16[192,512]{1,0:T(8,128)(2,1)} %shard_map.55, bf16[512,4096]{1,0:T(8,128)(2,1)} %param.11), kind=kOutput, calls=%fused_computation.1 | convolution fusion | flops 806092800 | bytes 5963776 | tf_op jit(solution)/shard_map/dot_general | solution.py:198
  130.7 0.7 broadcast_in_dim.18.qs_ref
  131.4 0.7 broadcast_in_dim.39.qp_ref
  132.2 23.2 %shard_map.56 = bf16[192,512]{1,0:T(8,128)(2,1)} custom-call(s32[4]{0:T(128)} %add_add_fusion.2.sc_ref, bf16[192,512]{1,0:T(8,128)(2,1)} %bitcast.84, bf16[16,2,392,256]{3,2,1,0:T(8,128)(2,1)} %bitcast.80, bf16[16,2,392,256]{3,2,1,0:T(8,128)(2,1)} %bitcast.81, s32[192,128]{1,0:T(8,128)} %broadcast_in_dim.18.qs_ref, s32[192,128]{1,0:T(8,128)} %broadcast_in_dim.39.qp_ref, ...), custom_call_target="tpu_custom_call" | custom-call | flops 2717908992 | bytes 3932160 | tf_op jit(solution)/shard_map/pallas_call | solution.py:103
  155.3 3.3 %convolution_convert_fusion = bf16[192,4096]{1,0:T(8,128)(2,1)S(1)} fusion(bf16[192,512]{1,0:T(8,128)(2,1)} %shard_map.56, bf16[512,4096]{1,0:T(8,128)(2,1)} %param.11), kind=kOutput, calls=%fused_computation | convolution fusion | flops 806092800 | bytes 5963776 | tf_op jit(solution)/shard_map/dot_general | solution.py:198
  158.6 0.0 copy-start
  158.6 0.3 convert.8
  159.0 0.0 copy-start.1
  159.0 1.6 copy-done.1
  160.7 0.1 fusion.1
  160.8 0.1 collective-permute-start.5
  160.9 0.0 copy-done
  160.9 0.0 copy-start.2
  160.9 0.3 convert.7
  161.3 0.1 fusion
  161.4 0.5 collective-permute-start.1
  161.9 1.2 collective-permute-done.5
  163.1 0.2 bitcast_add_fusion
  163.3 0.1 fusion.11
  163.4 0.9 collective-permute-start.8
  164.3 1.3 collective-permute-start.7
  165.6 2.3 %collective-permute-start.6 = (bf16[24,4096]{1,0:T(8,128)(2,1)S(1)}, bf16[24,4096]{1,0:T(8,128)(2,1)S(1)}, u32[]{:S(2)}, u32[]{:S(2)}) collective-permute-start(bf16[24,4096]{1,0:T(8,128)(2,1)S(1)} %get-tuple-element.24), channel_id=1, source_target_pairs={{0,2},{1,3},{2,0},{3,1},{4,6},{5,7},{6,4},{7,5},{8,10},{9,11},{10,... | collective-permute-start | bytes 589832 | tf_op jit(solution)/shard_map/ppermute | solution.py:145
  167.9 0.0 collective-permute-done.1
  167.9 0.1 bitcast_add_fusion.1
  168.0 0.1 fusion.8
  168.1 0.9 collective-permute-start.4
  169.0 0.6 collective-permute-start.3
  169.7 3.5 %collective-permute-done.8 = bf16[24,4096]{1,0:T(8,128)(2,1)S(1)} collective-permute-done((bf16[24,4096]{1,0:T(8,128)(2,1)S(1)}, bf16[24,4096]{1,0:T(8,128)(2,1)S(1)}, u32[]{:S(2)}, u32[]{:S(2)}) %collective-permute-start.8) | collective-permute-done | bytes 196640 | tf_op jit(solution)/shard_map/ppermute | solution.py:145
  173.2 7.1 %collective-permute-start.2 = (bf16[24,4096]{1,0:T(8,128)(2,1)S(1)}, bf16[24,4096]{1,0:T(8,128)(2,1)S(1)}, u32[]{:S(2)}, u32[]{:S(2)}) collective-permute-start(bf16[24,4096]{1,0:T(8,128)(2,1)S(1)} %get-tuple-element.21), channel_id=1, source_target_pairs={{0,2},{1,3},{2,0},{3,1},{4,6},{5,7},{6,4},{7,5},{8,10},{9,11},{10,... | collective-permute-start | bytes 589832 | tf_op jit(solution)/shard_map/ppermute | solution.py:145
  180.3 12.1 %collective-permute-done.7 = bf16[24,4096]{1,0:T(8,128)(2,1)S(1)} collective-permute-done((bf16[24,4096]{1,0:T(8,128)(2,1)S(1)}, bf16[24,4096]{1,0:T(8,128)(2,1)S(1)}, u32[]{:S(2)}, u32[]{:S(2)}) %collective-permute-start.7) | collective-permute-done | bytes 196640 | tf_op jit(solution)/shard_map/ppermute | solution.py:145
  192.4 0.0 collective-permute-done.6
  192.4 0.1 fusion.4
  192.5 0.0 collective-permute-done.4
  192.5 7.5 %collective-permute-done.3 = bf16[24,4096]{1,0:T(8,128)(2,1)S(1)} collective-permute-done((bf16[24,4096]{1,0:T(8,128)(2,1)S(1)}, bf16[24,4096]{1,0:T(8,128)(2,1)S(1)}, u32[]{:S(2)}, u32[]{:S(2)}) %collective-permute-start.3) | collective-permute-done | bytes 196640 | tf_op jit(solution)/shard_map/ppermute | solution.py:145
  200.1 0.0 collective-permute-done.2
  200.1 0.1 fusion.7
  200.2 0.8 pad_maximum_fusion.1
  (7 shorter events, 0.1 us)
Async XLA Ops:
  6.5 86.5 %copy-start.3 = (s32[384]{0:T(512)S(1)}, s32[384]{0:T(512)}, u32[]{:S(2)}) copy-start(s32[384]{0:T(512)} %param.10) | copy-start | bytes 4612
  6.5 84.9 %all-gather.3.cloned.1.call-start = ((), (), s32[]{:S(2)}) async-start(), calls=%async_computation | async-start | bytes 6823936 | tf_op jit(solution)/shard_map/all_gather | solution.py:165
  9.3 14.3 %collective-permute-start = (bf16[392,256]{1,0:T(8,128)(2,1)S(1)}, bf16[392,256]{1,0:T(8,128)(2,1)S(1)}, u32[]{:S(2)}, u32[]{:S(2)}) collective-permute-start(bf16[392,256]{1,0:T(8,128)(2,1)S(1)} %get-tuple-element.30), channel_id=1, source_target_pairs={{0,128},{128,0},{1,129},{129,1},{2,130},{130,2},{3,131},{131,3},{4... | collective-permute-start | bytes 602120 | tf_op jit(solution)/shard_map/ppermute | solution.py:163
  158.6 2.3 %copy-start = (bf16[192,4096]{1,0:T(8,128)(2,1)S(1)}, bf16[192,4096]{1,0:T(8,128)(2,1)}, u32[]{:S(2)}) copy-start(bf16[192,4096]{1,0:T(8,128)(2,1)} %convolution_convert_fusion.1.after_ref) | copy-start | bytes 4718596
  159.0 1.7 copy-start.1
  160.8 2.4 %collective-permute-start.5 = (bf16[4,24,4096]{2,1,0:T(8,128)(2,1)S(1)}, bf16[4,24,4096]{2,1,0:T(8,128)(2,1)S(1)}, u32[]{:S(2)}, u32[]{:S(2)}) collective-permute-start(bf16[4,24,4096]{2,1,0:T(8,128)(2,1)S(1)} %fusion.1), channel_id=1, source_target_pairs={{0,1},{1,0},{2,3},{3,2},{4,5},{5,4},{6,7},{7,6},{8,9},{9,8},{10,11... | collective-permute-start | bytes 2359304 | tf_op jit(solution)/shard_map/ppermute | solution.py:139
  160.9 2.2 %copy-start.2 = (f32[4,2,24,4096]{3,2,1,0:T(8,128)S(1)}, f32[4,2,24,4096]{3,2,1,0:T(8,128)}, u32[]{:S(2)}) copy-start(f32[4,2,24,4096]{3,2,1,0:T(8,128)} %copy-done.1) | copy-start | bytes 9437188
  161.4 6.5 %collective-permute-start.1 = (bf16[4,24,4096]{2,1,0:T(8,128)(2,1)S(1)}, bf16[4,24,4096]{2,1,0:T(8,128)(2,1)S(1)}, u32[]{:S(2)}, u32[]{:S(2)}) collective-permute-start(bf16[4,24,4096]{2,1,0:T(8,128)(2,1)S(1)} %fusion), channel_id=1, source_target_pairs={{0,1},{1,0},{2,3},{3,2},{4,5},{5,4},{6,7},{7,6},{8,9},{9,8},{10,11... | collective-permute-start | bytes 2359304 | tf_op jit(solution)/shard_map/ppermute | solution.py:139
  163.4 9.8 %collective-permute-start.8 = (bf16[24,4096]{1,0:T(8,128)(2,1)S(1)}, bf16[24,4096]{1,0:T(8,128)(2,1)S(1)}, u32[]{:S(2)}, u32[]{:S(2)}) collective-permute-start(bf16[24,4096]{1,0:T(8,128)(2,1)S(1)} %get-tuple-element.25), channel_id=1, source_target_pairs={{0,6},{1,7},{2,4},{3,5},{4,2},{5,3},{6,0},{7,1},{8,14},{9,15},{10,... | collective-permute-start | bytes 589832 | tf_op jit(solution)/shard_map/ppermute | solution.py:145
  164.3 28.1 %collective-permute-start.7 = (bf16[24,4096]{1,0:T(8,128)(2,1)S(1)}, bf16[24,4096]{1,0:T(8,128)(2,1)S(1)}, u32[]{:S(2)}, u32[]{:S(2)}) collective-permute-start(bf16[24,4096]{1,0:T(8,128)(2,1)S(1)} %get-tuple-element.26), channel_id=1, source_target_pairs={{0,4},{1,5},{2,6},{3,7},{4,0},{5,1},{6,2},{7,3},{8,12},{9,13},{10,... | collective-permute-start | bytes 589832 | tf_op jit(solution)/shard_map/ppermute | solution.py:145
  165.6 26.8 %collective-permute-start.6 = (bf16[24,4096]{1,0:T(8,128)(2,1)S(1)}, bf16[24,4096]{1,0:T(8,128)(2,1)S(1)}, u32[]{:S(2)}, u32[]{:S(2)}) collective-permute-start(bf16[24,4096]{1,0:T(8,128)(2,1)S(1)} %get-tuple-element.24), channel_id=1, source_target_pairs={{0,2},{1,3},{2,0},{3,1},{4,6},{5,7},{6,4},{7,5},{8,10},{9,11},{10,... | collective-permute-start | bytes 589832 | tf_op jit(solution)/shard_map/ppermute | solution.py:145
  168.1 24.4 %collective-permute-start.4 = (bf16[24,4096]{1,0:T(8,128)(2,1)S(1)}, bf16[24,4096]{1,0:T(8,128)(2,1)S(1)}, u32[]{:S(2)}, u32[]{:S(2)}) collective-permute-start(bf16[24,4096]{1,0:T(8,128)(2,1)S(1)} %get-tuple-element.22), channel_id=1, source_target_pairs={{0,6},{1,7},{2,4},{3,5},{4,2},{5,3},{6,0},{7,1},{8,14},{9,15},{10,... | collective-permute-start | bytes 589832 | tf_op jit(solution)/shard_map/ppermute | solution.py:145
  169.0 31.0 %collective-permute-start.3 = (bf16[24,4096]{1,0:T(8,128)(2,1)S(1)}, bf16[24,4096]{1,0:T(8,128)(2,1)S(1)}, u32[]{:S(2)}, u32[]{:S(2)}) collective-permute-start(bf16[24,4096]{1,0:T(8,128)(2,1)S(1)} %get-tuple-element.23), channel_id=1, source_target_pairs={{0,4},{1,5},{2,6},{3,7},{4,0},{5,1},{6,2},{7,3},{8,12},{9,13},{10,... | collective-permute-start | bytes 589832 | tf_op jit(solution)/shard_map/ppermute | solution.py:145
  173.2 26.9 %collective-permute-start.2 = (bf16[24,4096]{1,0:T(8,128)(2,1)S(1)}, bf16[24,4096]{1,0:T(8,128)(2,1)S(1)}, u32[]{:S(2)}, u32[]{:S(2)}) collective-permute-start(bf16[24,4096]{1,0:T(8,128)(2,1)S(1)} %get-tuple-element.21), channel_id=1, source_target_pairs={{0,2},{1,3},{2,0},{3,1},{4,6},{5,7},{6,4},{7,5},{8,10},{9,11},{10,... | collective-permute-start | bytes 589832 | tf_op jit(solution)/shard_map/ppermute | solution.py:145
Sparse Core Ops, SparseCore 0:
  24.6 66.8 all-gather.2
where the time goes:
time: 211 us; the launch traced here: 208 us
  waiting for transfers between devices  104 us (49%)
  Pallas kernels  46.4 us (22%)
  between operations  17.2 us (8%)
  starting transfers between devices  13.9 us (7%)
  local copies, waits for them, and re-layouts  10 us (5%)
  other arithmetic  8.72 us (4%)
  matrix products  7.73 us (4%)
    all_gather x1, waiting for transfers between devices, per_device(): gathered = lax.all_gather(pair, 'xy')  65.2 us
    pallas_call x2, Pallas kernels, attention(): pl.pallas_call(kernel, out_shape=jax.ShapeDtypeStruct((rows, width), jnp....  46.4 us
    ppermute x6, waiting for transfers between devices, sum_over_heads(): lax.ppermute(send.astype(jnp.bfloat16), 'head', perm=[(i, i ^ 2 * k) for...  23.2 us
    ppermute x1, waiting for transfers between devices, per_device(): partner = lax.ppermute(block, 'zh', perm=[(0, 1), (1, 0)])  14.2 us
    ppermute x6, starting transfers between devices, sum_over_heads(): lax.ppermute(send.astype(jnp.bfloat16), 'head', perm=[(i, i ^ 2 * k) for...  13.2 us
    dot_general x2, matrix products, per_device(): jnp.dot(attended, out_weight, preferred_element_type=jnp.float32)  7.73 us
  transfers between devices with their start and end apart: 10, of which 6 were waited for; matrix products, arithmetic and copies ran while one was open for 1% of the time, Pallas kernels for 0%

commit v1 on v0

--- a/solution.py
+++ b/solution.py
@@ -130,18 +130,21 @@
     )(scalars, queries, kv, kv, q_start, q_pos, after)
 
 
-def sum_over_heads(projected, n_head, piece):
+def core_step(projected, n_head, piece):
     me_head = lax.axis_index("head")
     held = projected.reshape((n_head // 2, 2, piece) + projected.shape[1:]).astype(jnp.float32)
     core = me_head % 2
     keep = lax.dynamic_index_in_dim(held, core, axis=1, keepdims=False)
     send = lax.dynamic_index_in_dim(held, 1 - core, axis=1, keepdims=False)
     got = lax.ppermute(send.astype(jnp.bfloat16), "head", perm=[(i, i ^ 1) for i in range(n_head)])
-    held = keep + got.astype(jnp.float32)
-    chip = me_head // 2
-    total = lax.dynamic_index_in_dim(held, chip, axis=0, keepdims=False)
+    return keep + got.astype(jnp.float32)
+
+
+def chip_step(held, n_head):
+    chip = lax.axis_index("head") // 2
+    total = lax.dynamic_index_in_dim(held, chip, axis=1, keepdims=False)
     for k in range(1, n_head // 2):
-        send = lax.dynamic_index_in_dim(held, chip ^ k, axis=0, keepdims=False)
+        send = lax.dynamic_index_in_dim(held, chip ^ k, axis=1, keepdims=False)
         got = lax.ppermute(send.astype(jnp.bfloat16), "head", perm=[(i, i ^ (2 * k)) for i in range(n_head)])
         total = total + got.astype(jnp.float32)
     return total.astype(jnp.bfloat16)
@@ -196,9 +199,11 @@
             rows,
         )
         projected = jnp.dot(attended, out_weight, preferred_element_type=jnp.float32).astype(jnp.bfloat16)
-        after = projected
-        outs.append(sum_over_heads(projected, n_head, piece))
-    return jnp.concatenate(outs, axis=0)
+        held = core_step(projected, n_head, piece)
+        after = held
+        outs.append(held)
+    summed = chip_step(jnp.stack(outs), n_head)
+    return summed.reshape((-1,) + summed.shape[2:])
 
 
 def solution(mesh):

time: 211 us -> 220 us (1.043)
  the two profiles are of different devices: /device:TPU:148 before, /device:TPU:132 now
where the time goes in v1:
time: 220 us
  waiting for transfers between devices  116 us (53%)
  Pallas kernels  48.9 us (22%)
  between operations  17.5 us (8%)
  other arithmetic  14.8 us (7%)
  local copies, waits for them, and re-layouts  10.8 us (5%)
  matrix products  6.59 us (3%)
  starting transfers between devices  5.09 us (2%)
    all_gather x1, waiting for transfers between devices, per_device(): gathered = lax.all_gather(pair, 'xy')  66.9 us
    pallas_call x2, Pallas kernels, attention(): pl.pallas_call(kernel, out_shape=jax.ShapeDtypeStruct((rows, width), jnp....  48.9 us
    ppermute x3, waiting for transfers between devices, chip_step(): lax.ppermute(send.astype(jnp.bfloat16), 'head', perm=[(i, i ^ 2 * k) for...  32.7 us
    ppermute x1, waiting for transfers between devices, per_device(): partner = lax.ppermute(block, 'zh', perm=[(0, 1), (1, 0)])  14.2 us
    dot_general x2, matrix products, per_device(): jnp.dot(attended, out_weight, preferred_element_type=jnp.float32)  6.59 us
    ppermute x3, starting transfers between devices, chip_step(): lax.ppermute(send.astype(jnp.bfloat16), 'head', perm=[(i, i ^ 2 * k) for...  4.4 us
  transfers between devices with their start and end apart: 7, of which 5 were waited for; matrix products, arithmetic and copies ran while one was open for 2% of the time, Pallas kernels for 0%

profile of v1, /device:TPU:132, one launch (start us, length us, event | category | flops | bytes accessed | tf_op | source)
XLA Modules:
  0.0 219.5 jit_solution(5318840814267399143)
XLA Ops:
  6.5 0.0 copy-start.2
  6.5 0.0 all-gather.3.cloned.1.call-start
  6.5 0.8 convert_convert_fusion
  7.3 1.0 copy.25
  8.3 0.9 fusion.20
  9.3 0.1 collective-permute-start
  9.4 14.2 %collective-permute-done = bf16[392,256]{1,0:T(8,128)(2,1)S(1)} collective-permute-done((bf16[392,256]{1,0:T(8,128)(2,1)S(1)}, bf16[392,256]{1,0:T(8,128)(2,1)S(1)}, u32[]{:S(2)}, u32[]{:S(2)}) %collective-permute-start) | collective-permute-done | bytes 200736 | tf_op jit(solution)/shard_map/ppermute | solution.py:166
  23.6 0.8 pad_maximum_fusion
  24.4 0.0 all-gather.3.cloned.1.call-update
  24.4 1.8 fusion.21
  26.2 66.9 %all-gather.3.cloned.1.call-done = bf16[32,392,256]{2,1,0:T(8,128)(2,1)} async-done(((bf16[2,392,256]{2,1,0:T(8,128)(2,1)}), bf16[32,392,256]{2,1,0:T(8,128)(2,1)}) %all-gather.3.cloned.1.call-update) | async-done | bytes 6422544 | tf_op jit(solution)/shard_map/all_gather | solution.py:168
  93.1 0.9 slice_convert_fusion
  94.1 0.7 convert_reduce_fusion
  94.7 0.0 copy-done.2
  94.7 0.1 select_reduce_fusion
  94.8 0.1 convert_element_type.92
  95.0 0.1 reshape_squeeze.12
  95.1 0.6 fusion.23
  97.8 0.1 broadcast_in_dim.15
  97.9 1.3 add_add_fusion.1.sc_ref
  99.2 0.7 broadcast_in_dim.14.qs_ref
  99.9 0.7 broadcast_in_dim.16.qp_ref
  100.7 0.6 broadcast_in_dim.17.after_ref
  101.2 24.3 %shard_map.55 = bf16[192,512]{1,0:T(8,128)(2,1)} custom-call(s32[4]{0:T(128)} %add_add_fusion.1.sc_ref, bf16[192,512]{1,0:T(8,128)(2,1)} %bitcast.93, bf16[16,2,392,256]{3,2,1,0:T(8,128)(2,1)} %bitcast.84, bf16[16,2,392,256]{3,2,1,0:T(8,128)(2,1)} %bitcast.85, s32[192,128]{1,0:T(8,128)} %broadcast_in_dim.14.qs_ref, s32[192,128]{1,0:T(8,128)} %broadcast_in_dim.16.qp_ref, ...), custom_call_target="tpu_custom_call" | custom-call | flops 2717908992 | bytes 3932160 | tf_op jit(solution)/shard_map/pallas_call | solution.py:103
  125.5 3.3 %convolution_convert_fusion.1 = bf16[192,4096]{1,0:T(8,128)(2,1)S(1)} fusion(bf16[192,512]{1,0:T(8,128)(2,1)} %shard_map.55, bf16[512,4096]{1,0:T(8,128)(2,1)} %param.11), kind=kOutput, calls=%fused_computation.1 | convolution fusion | flops 806092800 | bytes 5963776 | tf_op jit(solution)/shard_map/dot_general | solution.py:201
  128.8 0.3 convert.7
  129.2 1.0 fusion.1
  130.2 0.0 collective-permute-start.1
  130.2 0.1 reshape_squeeze.14
  130.2 0.6 fusion.22
  132.7 0.1 broadcast_in_dim.38
  132.8 1.2 add_add_fusion.2.sc_ref
  134.0 0.0 collective-permute-done.1
  134.0 2.4 %bitcast_add_fusion.1.after_ref = f32[4,24,4096]{2,1,0:T(8,128)} fusion(bf16[4,24,4096]{2,1,0:T(8,128)(2,1)} %collective-permute-done.1, f32[4,2,24,4096]{3,2,1,0:T(8,128)S(1)} %convert.7, s32[]{:T(128)S(6)} %select_n.43), kind=kLoop, calls=%fused_computation.16 | loop fusion | flops 786432 | bytes 3932164 | tf_op jit(solution)/shard_map/add | solution.py:140
  136.4 0.7 broadcast_in_dim.18.qs_ref
  137.2 0.7 broadcast_in_dim.39.qp_ref
  137.9 24.6 %shard_map.56 = bf16[192,512]{1,0:T(8,128)(2,1)} custom-call(s32[4]{0:T(128)} %add_add_fusion.2.sc_ref, bf16[192,512]{1,0:T(8,128)(2,1)} %bitcast.92, bf16[16,2,392,256]{3,2,1,0:T(8,128)(2,1)} %bitcast.86, bf16[16,2,392,256]{3,2,1,0:T(8,128)(2,1)} %bitcast.87, s32[192,128]{1,0:T(8,128)} %broadcast_in_dim.18.qs_ref, s32[192,128]{1,0:T(8,128)} %broadcast_in_dim.39.qp_ref, ...), custom_call_target="tpu_custom_call" | custom-call | flops 2717908992 | bytes 3932160 | tf_op jit(solution)/shard_map/pallas_call | solution.py:103
  162.5 3.3 %convolution_convert_fusion = bf16[192,4096]{1,0:T(8,128)(2,1)S(1)} fusion(bf16[192,512]{1,0:T(8,128)(2,1)} %shard_map.56, bf16[512,4096]{1,0:T(8,128)(2,1)} %param.11), kind=kOutput, calls=%fused_computation | convolution fusion | flops 806092800 | bytes 5963776 | tf_op jit(solution)/shard_map/dot_general | solution.py:201
  165.8 0.3 convert.8
  166.2 0.0 copy-start.1
  166.2 1.7 copy-done.1
  167.9 0.0 copy-start
  167.9 0.1 fusion.2
  168.0 0.6 collective-permute-start.2
  168.6 2.0 collective-permute-done.2
  170.6 1.8 fusion
  172.4 0.0 copy-done
  172.4 1.0 fusion.18
  173.5 0.8 collective-permute-start.5
  174.3 1.3 collective-permute-start.4
  175.6 2.3 %collective-permute-start.3 = (bf16[2,24,4096]{2,1,0:T(8,128)(2,1)S(1)}, bf16[2,24,4096]{2,1,0:T(8,128)(2,1)}, u32[]{:S(2)}, u32[]{:S(2)}) collective-permute-start(bf16[2,24,4096]{2,1,0:T(8,128)(2,1)S(1)} %get-tuple-element.21), channel_id=1, source_target_pairs={{0,2},{1,3},{2,0},{3,1},{4,6},{5,7},{6,4},{7,5},{8,10},{9,11},{10,... | collective-permute-start | bytes 1179656 | tf_op jit(solution)/shard_map/ppermute | solution.py:148
  177.9 9.8 %collective-permute-done.5 = bf16[2,24,4096]{2,1,0:T(8,128)(2,1)} collective-permute-done((bf16[2,24,4096]{2,1,0:T(8,128)(2,1)}, bf16[2,24,4096]{2,1,0:T(8,128)(2,1)}, u32[]{:S(2)}, u32[]{:S(2)}) %collective-permute-start.5) | collective-permute-done | bytes 393248 | tf_op jit(solution)/shard_map/ppermute | solution.py:148
  187.7 22.9 %collective-permute-done.4 = bf16[2,24,4096]{2,1,0:T(8,128)(2,1)} collective-permute-done((bf16[2,24,4096]{2,1,0:T(8,128)(2,1)}, bf16[2,24,4096]{2,1,0:T(8,128)(2,1)}, u32[]{:S(2)}, u32[]{:S(2)}) %collective-permute-start.4) | collective-permute-done | bytes 393248 | tf_op jit(solution)/shard_map/ppermute | solution.py:148
  210.5 0.0 collective-permute-done.3
  210.5 2.1 fusion.10
  (5 shorter events, 0.1 us)
Async XLA Ops:
  6.5 88.2 %copy-start.2 = (s32[384]{0:T(512)S(1)}, s32[384]{0:T(512)}, u32[]{:S(2)}) copy-start(s32[384]{0:T(512)} %param.10) | copy-start | bytes 4612
  6.5 86.6 %all-gather.3.cloned.1.call-start = ((), (), s32[]{:S(2)}) async-start(), calls=%async_computation | async-start | bytes 6823936 | tf_op jit(solution)/shard_map/all_gather | solution.py:168
  9.3 14.3 %collective-permute-start = (bf16[392,256]{1,0:T(8,128)(2,1)S(1)}, bf16[392,256]{1,0:T(8,128)(2,1)S(1)}, u32[]{:S(2)}, u32[]{:S(2)}) collective-permute-start(bf16[392,256]{1,0:T(8,128)(2,1)S(1)} %get-tuple-element.27), channel_id=1, source_target_pairs={{0,128},{128,0},{1,129},{129,1},{2,130},{130,2},{3,131},{131,3},{4... | collective-permute-start | bytes 602120 | tf_op jit(solution)/shard_map/ppermute | solution.py:166
  130.2 3.9 %collective-permute-start.1 = (bf16[4,24,4096]{2,1,0:T(8,128)(2,1)}, bf16[4,24,4096]{2,1,0:T(8,128)(2,1)}, u32[]{:S(2)}, u32[]{:S(2)}) collective-permute-start(bf16[4,24,4096]{2,1,0:T(8,128)(2,1)} %fusion.1), channel_id=1, source_target_pairs={{0,1},{1,0},{2,3},{3,2},{4,5},{5,4},{6,7},{7,6},{8,9},{9,8},{10,11... | collective-permute-start | bytes 2359304 | tf_op jit(solution)/shard_map/ppermute | solution.py:139
  166.2 1.7 copy-start.1
  167.9 4.5 %copy-start = (f32[4,24,4096]{2,1,0:T(8,128)S(1)}, f32[4,24,4096]{2,1,0:T(8,128)}, u32[]{:S(2)}) copy-start(f32[4,24,4096]{2,1,0:T(8,128)} %bitcast_add_fusion.1.after_ref) | copy-start | bytes 4718596
  168.0 2.6 %collective-permute-start.2 = (bf16[4,24,4096]{2,1,0:T(8,128)(2,1)S(1)}, bf16[4,24,4096]{2,1,0:T(8,128)(2,1)}, u32[]{:S(2)}, u32[]{:S(2)}) collective-permute-start(bf16[4,24,4096]{2,1,0:T(8,128)(2,1)S(1)} %fusion.2), channel_id=1, source_target_pairs={{0,1},{1,0},{2,3},{3,2},{4,5},{5,4},{6,7},{7,6},{8,9},{9,8},{10,11... | collective-permute-start | bytes 2359304 | tf_op jit(solution)/shard_map/ppermute | solution.py:139
  173.5 14.2 %collective-permute-start.5 = (bf16[2,24,4096]{2,1,0:T(8,128)(2,1)}, bf16[2,24,4096]{2,1,0:T(8,128)(2,1)}, u32[]{:S(2)}, u32[]{:S(2)}) collective-permute-start(bf16[2,24,4096]{2,1,0:T(8,128)(2,1)} %get-tuple-element.23), channel_id=1, source_target_pairs={{0,6},{1,7},{2,4},{3,5},{4,2},{5,3},{6,0},{7,1},{8,14},{9,15},{10,... | collective-permute-start | bytes 1179656 | tf_op jit(solution)/shard_map/ppermute | solution.py:148
  174.3 36.2 %collective-permute-start.4 = (bf16[2,24,4096]{2,1,0:T(8,128)(2,1)}, bf16[2,24,4096]{2,1,0:T(8,128)(2,1)}, u32[]{:S(2)}, u32[]{:S(2)}) collective-permute-start(bf16[2,24,4096]{2,1,0:T(8,128)(2,1)} %get-tuple-element.22), channel_id=1, source_target_pairs={{0,4},{1,5},{2,6},{3,7},{4,0},{5,1},{6,2},{7,3},{8,12},{9,13},{10,... | collective-permute-start | bytes 1179656 | tf_op jit(solution)/shard_map/ppermute | solution.py:148
  175.6 35.0 %collective-permute-start.3 = (bf16[2,24,4096]{2,1,0:T(8,128)(2,1)S(1)}, bf16[2,24,4096]{2,1,0:T(8,128)(2,1)}, u32[]{:S(2)}, u32[]{:S(2)}) collective-permute-start(bf16[2,24,4096]{2,1,0:T(8,128)(2,1)S(1)} %get-tuple-element.21), channel_id=1, source_target_pairs={{0,2},{1,3},{2,0},{3,1},{4,6},{5,7},{6,4},{7,5},{8,10},{9,11},{10,... | collective-permute-start | bytes 1179656 | tf_op jit(solution)/shard_map/ppermute | solution.py:148
Sparse Core Ops, SparseCore 0:
  24.5 68.5 all-gather.2

commit v2 on v0

--- a/solution.py
+++ b/solution.py
@@ -197,7 +197,11 @@
         )
         projected = jnp.dot(attended, out_weight, preferred_element_type=jnp.float32).astype(jnp.bfloat16)
         after = projected
-        outs.append(sum_over_heads(projected, n_head, piece))
+        if c < CHUNKS - 1:
+            outs.append(lax.psum_scatter(projected, "head", scatter_dimension=0, tiled=True))
+        else:
+            *outs, projected = lax.optimization_barrier((*outs, projected))
+            outs.append(sum_over_heads(projected, n_head, piece))
     return jnp.concatenate(outs, axis=0)
 
 

time: 211 us -> 206 us (0.976)
  the two profiles are of different devices: /device:TPU:148 before, /device:TPU:2 now
where the time goes in v2:
time: 206 us; the launch traced here: 202 us
  waiting for transfers between devices  123 us (60%)
  Pallas kernels  19.5 us (9%)
  between operations  17.1 us (8%)
  starting transfers between devices  11.8 us (6%)
  other arithmetic  11.3 us (5%)
  local copies, waits for them, and re-layouts  10.1 us (5%)
  matrix products  8.89 us (4%)
    all_gather x1, waiting for transfers between devices, per_device(): gathered = lax.all_gather(pair, 'xy')  69.4 us
    reduce_scatter x1, waiting for transfers between devices, per_device(): lax.psum_scatter(projected, 'head', scatter_dimension=0, tiled=True)  32.2 us
    pallas_call x2, Pallas kernels, attention(): pl.pallas_call(kernel, out_shape=jax.ShapeDtypeStruct((rows, width), jnp....  19.5 us
    ppermute x3, waiting for transfers between devices, sum_over_heads(): lax.ppermute(send.astype(jnp.bfloat16), 'head', perm=[(i, i ^ 2 * k) for...  12.8 us
    dot_general x2, matrix products, per_device(): jnp.dot(attended, out_weight, preferred_element_type=jnp.float32)  8.89 us
    ppermute x1, starting transfers between devices, per_device(): partner = lax.ppermute(block, 'zh', perm=[(0, 1), (1, 0)])  7.28 us
    ppermute x1, waiting for transfers between devices, per_device(): partner = lax.ppermute(block, 'zh', perm=[(0, 1), (1, 0)])  6.02 us
    ppermute x3, starting transfers between devices, sum_over_heads(): lax.ppermute(send.astype(jnp.bfloat16), 'head', perm=[(i, i ^ 2 * k) for...  4.47 us
  transfers between devices with their start and end apart: 7, of which 6 were waited for; matrix products, arithmetic and copies ran while one was open for 5% of the time, Pallas kernels for 5%

profile of v2, /device:TPU:2, one launch (start us, length us, event | category | flops | bytes accessed | tf_op | source)
XLA Modules:
  0.0 201.7 jit_solution(15335269002894976974)
XLA Ops:
  6.5 0.0 copy-start.2
  6.5 0.0 all-gather.3.cloned.1.call-start
  6.5 1.0 copy.17
  7.6 0.7 convert_convert_fusion
  8.3 0.9 fusion.7
  9.2 7.3 %collective-permute-start = (bf16[392,256]{1,0:T(8,128)(2,1)S(1)}, bf16[392,256]{1,0:T(8,128)(2,1)S(1)}, u32[]{:S(2)}, u32[]{:S(2)}) collective-permute-start(bf16[392,256]{1,0:T(8,128)(2,1)S(1)} %get-tuple-element.31), channel_id=1, source_target_pairs={{0,128},{128,0},{1,129},{129,1},{2,130},{130,2},{3,131},{131,3},{4... | collective-permute-start | bytes 602120 | tf_op jit(solution)/shard_map/ppermute | solution.py:163
  16.5 6.0 %collective-permute-done = bf16[392,256]{1,0:T(8,128)(2,1)S(1)} collective-permute-done((bf16[392,256]{1,0:T(8,128)(2,1)S(1)}, bf16[392,256]{1,0:T(8,128)(2,1)S(1)}, u32[]{:S(2)}, u32[]{:S(2)}) %collective-permute-start) | collective-permute-done | bytes 200736 | tf_op jit(solution)/shard_map/ppermute | solution.py:163
  22.5 0.8 pad_maximum_fusion
  23.3 0.0 all-gather.3.cloned.1.call-update
  23.3 0.0 reduce-scatter.2.cloned.1.call-start
  23.4 1.8 fusion.8
  25.2 69.4 %all-gather.3.cloned.1.call-done = bf16[32,392,256]{2,1,0:T(8,128)(2,1)} async-done(((bf16[2,392,256]{2,1,0:T(8,128)(2,1)}), bf16[32,392,256]{2,1,0:T(8,128)(2,1)}) %all-gather.3.cloned.1.call-update) | async-done | bytes 6422544 | tf_op jit(solution)/shard_map/all_gather | solution.py:165
  94.5 0.9 slice_convert_fusion
  95.5 0.7 convert_reduce_fusion
  96.2 0.0 copy-done.2
  96.2 0.1 select_reduce_fusion
  96.3 0.1 convert_element_type.77
  96.4 0.1 reshape_squeeze.12
  96.5 0.6 fusion.10
  98.9 0.1 broadcast_in_dim.15
  99.0 1.2 add_add_fusion.1.sc_ref
  100.2 0.7 broadcast_in_dim.14.qs_ref
  100.9 0.7 broadcast_in_dim.16.qp_ref
  101.6 0.6 broadcast_in_dim.17.after_ref
  102.2 9.7 %shard_map.55 = bf16[192,512]{1,0:T(8,128)(2,1)} custom-call(s32[4]{0:T(128)} %add_add_fusion.1.sc_ref, bf16[192,512]{1,0:T(8,128)(2,1)} %bitcast.60, bf16[16,2,392,256]{3,2,1,0:T(8,128)(2,1)} %bitcast.54, bf16[16,2,392,256]{3,2,1,0:T(8,128)(2,1)} %bitcast.55, s32[192,128]{1,0:T(8,128)} %broadcast_in_dim.14.qs_ref, s32[192,128]{1,0:T(8,128)} %broadcast_in_dim.16.qp_ref, ...), custom_call_target="tpu_custom_call" | custom-call | flops 2717908992 | bytes 3932160 | tf_op jit(solution)/shard_map/pallas_call | solution.py:103
  111.9 4.4 %convolution_convert_fusion.1.after_ref = bf16[192,4096]{1,0:T(8,128)(2,1)} fusion(bf16[192,512]{1,0:T(8,128)(2,1)} %shard_map.55, bf16[512,4096]{1,0:T(8,128)(2,1)} %param.11), kind=kOutput, calls=%fused_computation.1 | convolution fusion | flops 806092800 | bytes 5963776 | tf_op jit(solution)/shard_map/dot_general | solution.py:198
  116.3 0.0 reduce-scatter.2.cloned.1.call-update
  116.4 0.1 reshape_squeeze.14
  116.5 0.6 fusion.9
  118.7 0.1 broadcast_in_dim.38
  118.8 1.2 add_add_fusion.2.sc_ref
  120.0 0.7 broadcast_in_dim.18.qs_ref
  120.7 0.7 broadcast_in_dim.39.qp_ref
  121.4 9.7 %shard_map.56 = bf16[192,512]{1,0:T(8,128)(2,1)} custom-call(s32[4]{0:T(128)} %add_add_fusion.2.sc_ref, bf16[192,512]{1,0:T(8,128)(2,1)} %bitcast.59, bf16[16,2,392,256]{3,2,1,0:T(8,128)(2,1)} %bitcast.56, bf16[16,2,392,256]{3,2,1,0:T(8,128)(2,1)} %bitcast.57, s32[192,128]{1,0:T(8,128)} %broadcast_in_dim.18.qs_ref, s32[192,128]{1,0:T(8,128)} %broadcast_in_dim.39.qp_ref, ...), custom_call_target="tpu_custom_call" | custom-call | flops 2717908992 | bytes 3932160 | tf_op jit(solution)/shard_map/pallas_call | solution.py:103
  131.2 4.5 %convolution_convert_fusion = bf16[192,4096]{1,0:T(8,128)(2,1)} fusion(bf16[192,512]{1,0:T(8,128)(2,1)} %shard_map.56, bf16[512,4096]{1,0:T(8,128)(2,1)} %param.11), kind=kOutput, calls=%fused_computation | convolution fusion | flops 806092800 | bytes 5963776 | tf_op jit(solution)/shard_map/dot_general | solution.py:198
  135.6 32.2 %reduce-scatter.2.cloned.1.call-done = bf16[24,4096]{1,0:T(8,128)(2,1)} async-done(((bf16[192,4096]{1,0:T(8,128)(2,1)}), bf16[24,4096]{1,0:T(8,128)(2,1)}) %reduce-scatter.2.cloned.1.call-update) | async-done | bytes 196624 | tf_op jit(solution)/shard_map/reduce_scatter | solution.py:201
  167.8 1.7 convert.6
  169.6 1.0 fusion
  170.6 0.0 collective-permute-start.1
  170.6 0.0 copy-start.1
  170.6 2.6 %collective-permute-done.1 = bf16[4,24,4096]{2,1,0:T(8,128)(2,1)} collective-permute-done((bf16[4,24,4096]{2,1,0:T(8,128)(2,1)}, bf16[4,24,4096]{2,1,0:T(8,128)(2,1)}, u32[]{:S(2)}, u32[]{:S(2)}) %collective-permute-start.1) | collective-permute-done | bytes 786464 | tf_op jit(solution)/shard_map/ppermute | solution.py:139
  173.2 1.3 bitcast_add_fusion
  174.5 0.0 copy-start
  174.5 1.1 copy-done
  175.6 0.1 fusion.4
  175.7 0.1 collective-permute-start.2
  175.8 1.2 collective-permute-start.3
  177.0 3.1 %collective-permute-start.4 = (bf16[24,4096]{1,0:T(8,128)(2,1)S(1)}, bf16[24,4096]{1,0:T(8,128)(2,1)S(1)}, u32[]{:S(2)}, u32[]{:S(2)}) collective-permute-start(bf16[24,4096]{1,0:T(8,128)(2,1)S(1)} %get-tuple-element.26), channel_id=1, source_target_pairs={{0,6},{1,7},{2,4},{3,5},{4,2},{5,3},{6,0},{7,1},{8,14},{9,15},{10,... | collective-permute-start | bytes 589832 | tf_op jit(solution)/shard_map/ppermute | solution.py:145
  180.2 5.0 %collective-permute-done.2 = bf16[24,4096]{1,0:T(8,128)(2,1)S(1)} collective-permute-done((bf16[24,4096]{1,0:T(8,128)(2,1)S(1)}, bf16[24,4096]{1,0:T(8,128)(2,1)S(1)}, u32[]{:S(2)}, u32[]{:S(2)}) %collective-permute-start.2) | collective-permute-done | bytes 196640 | tf_op jit(solution)/shard_map/ppermute | solution.py:145
  185.2 7.8 %collective-permute-done.3 = bf16[24,4096]{1,0:T(8,128)(2,1)S(1)} collective-permute-done((bf16[24,4096]{1,0:T(8,128)(2,1)S(1)}, bf16[24,4096]{1,0:T(8,128)(2,1)S(1)}, u32[]{:S(2)}, u32[]{:S(2)}) %collective-permute-start.3) | collective-permute-done | bytes 196640 | tf_op jit(solution)/shard_map/ppermute | solution.py:145
  193.0 0.0 collective-permute-done.4
  193.0 1.1 fusion.3
  194.1 0.0 copy-done.1
  194.1 0.8 pad_maximum_fusion.1
  (5 shorter events, 0.1 us)
Async XLA Ops:
  6.5 89.6 %copy-start.2 = (s32[384]{0:T(512)S(1)}, s32[384]{0:T(512)}, u32[]{:S(2)}) copy-start(s32[384]{0:T(512)} %param.10) | copy-start | bytes 4612
  6.5 88.0 %all-gather.3.cloned.1.call-start = ((), (), s32[]{:S(2)}) async-start(), calls=%async_computation.2 | async-start | bytes 6823936 | tf_op jit(solution)/shard_map/all_gather | solution.py:165
  9.2 13.3 %collective-permute-start = (bf16[392,256]{1,0:T(8,128)(2,1)S(1)}, bf16[392,256]{1,0:T(8,128)(2,1)S(1)}, u32[]{:S(2)}, u32[]{:S(2)}) collective-permute-start(bf16[392,256]{1,0:T(8,128)(2,1)S(1)} %get-tuple-element.31), channel_id=1, source_target_pairs={{0,128},{128,0},{1,129},{129,1},{2,130},{130,2},{3,131},{131,3},{4... | collective-permute-start | bytes 602120 | tf_op jit(solution)/shard_map/ppermute | solution.py:163
  23.3 144.5 %reduce-scatter.2.cloned.1.call-start = ((), (), s32[]{:S(2)}) async-start(), calls=%async_computation.1 | async-start | bytes 1769472 | tf_op jit(solution)/shard_map/reduce_scatter | solution.py:201
  170.6 2.6 %collective-permute-start.1 = (bf16[4,24,4096]{2,1,0:T(8,128)(2,1)}, bf16[4,24,4096]{2,1,0:T(8,128)(2,1)}, u32[]{:S(2)}, u32[]{:S(2)}) collective-permute-start(bf16[4,24,4096]{2,1,0:T(8,128)(2,1)} %fusion), channel_id=1, source_target_pairs={{0,1},{1,0},{2,3},{3,2},{4,5},{5,4},{6,7},{7,6},{8,9},{9,8},{10,11... | collective-permute-start | bytes 2359304 | tf_op jit(solution)/shard_map/ppermute | solution.py:139
  170.6 23.5 %copy-start.1 = (bf16[24,4096]{1,0:T(8,128)(2,1)S(1)}, bf16[24,4096]{1,0:T(8,128)(2,1)}, u32[]{:S(2)}) copy-start(bf16[24,4096]{1,0:T(8,128)(2,1)} %reduce-scatter.2.cloned.1.call-done) | copy-start | bytes 589828
  174.5 1.2 copy-start
  175.7 9.5 %collective-permute-start.2 = (bf16[24,4096]{1,0:T(8,128)(2,1)S(1)}, bf16[24,4096]{1,0:T(8,128)(2,1)S(1)}, u32[]{:S(2)}, u32[]{:S(2)}) collective-permute-start(bf16[24,4096]{1,0:T(8,128)(2,1)S(1)} %get-tuple-element.25), channel_id=1, source_target_pairs={{0,2},{1,3},{2,0},{3,1},{4,6},{5,7},{6,4},{7,5},{8,10},{9,11},{10,... | collective-permute-start | bytes 589832 | tf_op jit(solution)/shard_map/ppermute | solution.py:145
  175.8 17.2 %collective-permute-start.3 = (bf16[24,4096]{1,0:T(8,128)(2,1)S(1)}, bf16[24,4096]{1,0:T(8,128)(2,1)S(1)}, u32[]{:S(2)}, u32[]{:S(2)}) collective-permute-start(bf16[24,4096]{1,0:T(8,128)(2,1)S(1)} %get-tuple-element.27), channel_id=1, source_target_pairs={{0,4},{1,5},{2,6},{3,7},{4,0},{5,1},{6,2},{7,3},{8,12},{9,13},{10,... | collective-permute-start | bytes 589832 | tf_op jit(solution)/shard_map/ppermute | solution.py:145
  177.0 16.0 %collective-permute-start.4 = (bf16[24,4096]{1,0:T(8,128)(2,1)S(1)}, bf16[24,4096]{1,0:T(8,128)(2,1)S(1)}, u32[]{:S(2)}, u32[]{:S(2)}) collective-permute-start(bf16[24,4096]{1,0:T(8,128)(2,1)S(1)} %get-tuple-element.26), channel_id=1, source_target_pairs={{0,6},{1,7},{2,4},{3,5},{4,2},{5,3},{6,0},{7,1},{8,14},{9,15},{10,... | collective-permute-start | bytes 589832 | tf_op jit(solution)/shard_map/ppermute | solution.py:145
Sparse Core Ops, SparseCore 0:
  23.4 71.0 all-gather.2
  116.5 51.2 reduce-scatter.1

commit v3 on v2

--- a/solution.py
+++ b/solution.py
@@ -17,12 +17,12 @@
 
 
 def attn_kernel(
-    steps, shard_rows, heads, scale, sc_ref, q_ref, k_ref, v_ref, qs_ref, qp_ref, after_ref, o_ref, m_sc, l_sc, acc_sc
+    steps, shard_rows, heads, scale, at, sc_ref, q_ref, k_ref, v_ref, qs_ref, qp_ref, after_ref, o_ref, m_sc, l_sc, acc_sc
 ):
     j = pl.program_id(0)
-    me = sc_ref[0]
-    first = sc_ref[1]
-    q_last_start = sc_ref[2]
+    me = sc_ref[at]
+    first = sc_ref[at + 1]
+    q_last_start = sc_ref[at + 2]
     shard = me - (steps - 1) + j
     rows = q_ref.shape[0]
 
@@ -36,10 +36,12 @@
         cols = shard_rows // LANES
         if masked:
             lane = lax.broadcasted_iota(jnp.int32, (rows, LANES), 1)
+            q_start = qs_ref[...].reshape(rows, LANES)[:, 0:1]
+            q_pos = qp_ref[...].reshape(rows, LANES)[:, 0:1]
             allowed = []
             for c in range(cols):
                 k_pos = shard * shard_rows + c * LANES + lane
-                allowed.append((k_pos >= qs_ref[:, 0:1]) & (k_pos <= qp_ref[:, 0:1]))
+                allowed.append((k_pos >= q_start) & (k_pos <= q_pos))
         for h in range(heads):
             qh = q_ref[:, h * HEAD_WIDTH:(h + 1) * HEAD_WIDTH]
             s = []
@@ -88,18 +90,21 @@
             o_ref[:, h * HEAD_WIDTH:(h + 1) * HEAD_WIDTH] = (acc_sc[h] / denominator).astype(o_ref.dtype)
 
 
-def attention(scalars, queries, kv, q_start, q_pos, after, n_xy, shard_rows):
+def attention(scalars, chunk, queries, kv, q_start, q_pos, after, n_xy, shard_rows):
     rows, width = queries.shape
     heads = width // HEAD_WIDTH
     steps = -(-(MOST - 1) // shard_rows) + 1
     scale = HEAD_WIDTH ** (-0.5)
 
+    at = 4 * chunk
+
     def index(j, sc, half):
-        s = jnp.maximum(sc[0] - (steps - 1) + j, sc[1])
-        slot = jnp.where(s // n_xy == sc[3], 0, 1)
+        s = jnp.maximum(sc[at] - (steps - 1) + j, sc[at + 1])
+        slot = jnp.where(s // n_xy == sc[at + 3], 0, 1)
         return (s % n_xy, slot, 0, half)
 
-    kernel = functools.partial(attn_kernel, steps, shard_rows, heads, scale)
+    groups, _, piece, _ = q_start.shape
+    kernel = functools.partial(attn_kernel, steps, shard_rows, heads, scale, at)
     return pl.pallas_call(
         kernel,
         out_shape=jax.ShapeDtypeStruct((rows, width), jnp.bfloat16),
@@ -110,8 +115,8 @@
                 pl.BlockSpec((rows, width), lambda j, sc: (0, 0)),
                 pl.BlockSpec((None, None, shard_rows, HEAD_WIDTH), lambda j, sc: index(j, sc, 0)),
                 pl.BlockSpec((None, None, shard_rows, HEAD_WIDTH), lambda j, sc: index(j, sc, 1)),
-                pl.BlockSpec((rows, LANES), lambda j, sc: (0, 0)),
-                pl.BlockSpec((rows, LANES), lambda j, sc: (0, 0)),
+                pl.BlockSpec((groups, None, piece, LANES), lambda j, sc: (0, chunk, 0, 0)),
+                pl.BlockSpec((groups, None, piece, LANES), lambda j, sc: (0, chunk, 0, 0)),
                 pl.BlockSpec(memory_space=pl.ANY),
             ],
             out_specs=pl.BlockSpec((rows, width), lambda j, sc: (0, 0)),
@@ -178,23 +183,22 @@
         x = x.reshape((n_head, CHUNKS, piece) + x.shape[1:])[:, c]
         return x.reshape((n_head * piece,) + x.shape[2:])
 
+    def rows_view(x):
+        return jnp.broadcast_to(x[:, None], (rows, LANES)).reshape(n_head, CHUNKS, piece, LANES)
+
+    q_start_b = rows_view(q_start)
+    q_pos_b = rows_view(q_pos)
+    q_start_c = q_start.reshape(n_head, CHUNKS, piece)
+    firsts = jnp.maximum(q_start_c[0, :, 0] // rows, 0)
+    lasts = q_start_c[n_head - 1, :, piece - 1]
+    scalars = jnp.stack(
+        [jnp.full((CHUNKS,), me), firsts, lasts, jnp.full((CHUNKS,), zh)], axis=1
+    ).reshape(-1).astype(jnp.int32)
+
     outs = []
-    after = jnp.zeros((8, LANES), jnp.bfloat16)
+    after = gathered
     for c in range(CHUNKS):
-        qs_c = chunk_of(q_start, c)
-        qp_c = chunk_of(q_pos, c)
-        first = jnp.maximum(qs_c[0] // rows, 0)
-        scalars = jnp.stack([me, first, qs_c[-1], zh]).astype(jnp.int32)
-        attended = attention(
-            scalars,
-            chunk_of(queries, c),
-            gathered,
-            jnp.broadcast_to(qs_c[:, None], (qs_c.shape[0], LANES)),
-            jnp.broadcast_to(qp_c[:, None], (qp_c.shape[0], LANES)),
-            after,
-            n_xy,
-            rows,
-        )
+        attended = attention(scalars, c, chunk_of(queries, c), gathered, q_start_b, q_pos_b, after, n_xy, rows)
         projected = jnp.dot(attended, out_weight, preferred_element_type=jnp.float32).astype(jnp.bfloat16)
         after = projected
         if c < CHUNKS - 1:

time: 206 us -> 201 us (0.976)
  the two profiles are of different devices: /device:TPU:2 before, /device:TPU:32 now
where the time goes in v3:
time: 201 us; the launch traced here: 199 us
  waiting for transfers between devices  136 us (68%)
  between operations  13.5 us (7%)
  starting transfers between devices  12.3 us (6%)
  Pallas kernels  11.2 us (6%)
  other arithmetic  9.38 us (5%)
  matrix products  8.89 us (4%)
  local copies, waits for them, and re-layouts  7.52 us (4%)
    all_gather x1, waiting for transfers between devices, per_device(): gathered = lax.all_gather(pair, 'xy')  66.5 us
    reduce_scatter x1, waiting for transfers between devices, per_device(): lax.psum_scatter(projected, 'head', scatter_dimension=0, tiled=True)  40 us
    ppermute x3, waiting for transfers between devices, sum_over_heads(): lax.ppermute(send.astype(jnp.bfloat16), 'head', perm=[(i, i ^ 2 * k) for...  17.6 us
    pallas_call x2, Pallas kernels, attention(): pl.pallas_call(kernel, out_shape=jax.ShapeDtypeStruct((rows, width), jnp....  11.2 us
    ppermute x1, waiting for transfers between devices, per_device(): partner = lax.ppermute(block, 'zh', perm=[(0, 1), (1, 0)])  9.38 us
    dot_general x2, matrix products, per_device(): jnp.dot(attended, out_weight, preferred_element_type=jnp.float32)  8.89 us
    ppermute x1, starting transfers between devices, per_device(): partner = lax.ppermute(block, 'zh', perm=[(0, 1), (1, 0)])  6.38 us
    ppermute x3, starting transfers between devices, sum_over_heads(): lax.ppermute(send.astype(jnp.bfloat16), 'head', perm=[(i, i ^ 2 * k) for...  5.87 us
  transfers between devices with their start and end apart: 7, of which 7 were waited for; matrix products, arithmetic and copies ran while one was open for 3% of the time, Pallas kernels for 3%

profile of v3, /device:TPU:32, one launch (start us, length us, event | category | flops | bytes accessed | tf_op | source)
XLA Modules:
  0.0 198.9 jit_solution(12569310327050758448)
XLA Ops:
  6.5 0.0 copy-start.2
  6.5 0.0 all-gather.3.cloned.1.call-start
  6.5 1.0 copy.26
  7.6 0.7 convert_convert_fusion
  8.3 0.9 fusion.8
  9.2 6.4 %collective-permute-start = (bf16[392,256]{1,0:T(8,128)(2,1)S(1)}, bf16[392,256]{1,0:T(8,128)(2,1)S(1)}, u32[]{:S(2)}, u32[]{:S(2)}) collective-permute-start(bf16[392,256]{1,0:T(8,128)(2,1)S(1)} %get-tuple-element.29), channel_id=1, source_target_pairs={{0,128},{128,0},{1,129},{129,1},{2,130},{130,2},{3,131},{131,3},{4... | collective-permute-start | bytes 602120 | tf_op jit(solution)/shard_map/ppermute | solution.py:168
  15.6 9.4 %collective-permute-done = bf16[392,256]{1,0:T(8,128)(2,1)S(1)} collective-permute-done((bf16[392,256]{1,0:T(8,128)(2,1)S(1)}, bf16[392,256]{1,0:T(8,128)(2,1)S(1)}, u32[]{:S(2)}, u32[]{:S(2)}) %collective-permute-start) | collective-permute-done | bytes 200736 | tf_op jit(solution)/shard_map/ppermute | solution.py:168
  25.0 0.8 pad_maximum_fusion
  25.7 0.0 all-gather.3.cloned.1.call-update
  25.8 0.0 reduce-scatter.2.cloned.1.call-start
  25.8 0.1 pad.9.clone
  25.9 1.8 fusion.9
  27.7 66.5 %all-gather.3.cloned.1.call-done = bf16[32,392,256]{2,1,0:T(8,128)(2,1)} async-done(((bf16[2,392,256]{2,1,0:T(8,128)(2,1)}), bf16[32,392,256]{2,1,0:T(8,128)(2,1)}) %all-gather.3.cloned.1.call-update) | async-done | bytes 6422544 | tf_op jit(solution)/shard_map/all_gather | solution.py:170
  94.2 0.9 slice_convert_fusion
  95.1 0.7 convert_reduce_fusion
  95.8 0.0 copy-done.2
  95.8 0.1 select_reduce_fusion
  95.9 0.1 convert_element_type.81
  96.0 0.2 divide_reduce_fusion
  96.2 0.1 and_reduce_fusion
  96.3 0.1 add_add_fusion.1
  96.4 0.1 copy.27
  96.5 0.6 reshape.128.sc_ref
  97.1 0.8 broadcast_in_dim.4.qs_ref
  97.9 0.8 broadcast_in_dim.5.qp_ref
  98.7 5.6 %shard_map.55 = bf16[192,512]{1,0:T(8,128)(2,1)} custom-call(s32[8]{0:T(128)} %reshape.128.sc_ref, bf16[192,512]{1,0:T(8,128)(2,1)} %bitcast.62, bf16[16,2,392,256]{3,2,1,0:T(8,128)(2,1)} %bitcast.55, bf16[16,2,392,256]{3,2,1,0:T(8,128)(2,1)} %bitcast.56, s32[8,2,24,128]{3,2,1,0:T(8,128)} %broadcast_in_dim.4.qs_ref, ...), custom_call_target="tpu_custom_call" | custom-call | flops 2717908992 | bytes 3932160 | tf_op jit(solution)/shard_map/pallas_call | solution.py:108
  104.3 4.4 %convolution_convert_fusion.1.after_ref = bf16[192,4096]{1,0:T(8,128)(2,1)} fusion(bf16[192,512]{1,0:T(8,128)(2,1)} %shard_map.55, bf16[512,4096]{1,0:T(8,128)(2,1)} %param.11), kind=kOutput, calls=%fused_computation.1 | convolution fusion | flops 806092800 | bytes 5963776 | tf_op jit(solution)/shard_map/dot_general | solution.py:202
  108.7 0.0 reduce-scatter.2.cloned.1.call-update
  108.8 5.6 %shard_map.56 = bf16[192,512]{1,0:T(8,128)(2,1)} custom-call(s32[8]{0:T(128)} %reshape.128.sc_ref, bf16[192,512]{1,0:T(8,128)(2,1)} %bitcast.61, bf16[16,2,392,256]{3,2,1,0:T(8,128)(2,1)} %bitcast.58, bf16[16,2,392,256]{3,2,1,0:T(8,128)(2,1)} %bitcast.59, s32[8,2,24,128]{3,2,1,0:T(8,128)} %broadcast_in_dim.4.qs_ref, ...), custom_call_target="tpu_custom_call" | custom-call | flops 2717908992 | bytes 3932160 | tf_op jit(solution)/shard_map/pallas_call | solution.py:108
  114.4 4.5 %convolution_convert_fusion = bf16[192,4096]{1,0:T(8,128)(2,1)} fusion(bf16[192,512]{1,0:T(8,128)(2,1)} %shard_map.56, bf16[512,4096]{1,0:T(8,128)(2,1)} %param.11), kind=kOutput, calls=%fused_computation | convolution fusion | flops 806092800 | bytes 5963776 | tf_op jit(solution)/shard_map/dot_general | solution.py:202
  118.8 40.0 %reduce-scatter.2.cloned.1.call-done = bf16[24,4096]{1,0:T(8,128)(2,1)} async-done(((bf16[192,4096]{1,0:T(8,128)(2,1)}), bf16[24,4096]{1,0:T(8,128)(2,1)}) %reduce-scatter.2.cloned.1.call-update) | async-done | bytes 196624 | tf_op jit(solution)/shard_map/reduce_scatter | solution.py:205
  158.8 1.7 convert.6
  160.6 1.0 fusion
  161.6 0.0 collective-permute-start.1
  161.6 0.0 copy-start.1
  161.6 2.6 %collective-permute-done.1 = bf16[4,24,4096]{2,1,0:T(8,128)(2,1)} collective-permute-done((bf16[4,24,4096]{2,1,0:T(8,128)(2,1)}, bf16[4,24,4096]{2,1,0:T(8,128)(2,1)}, u32[]{:S(2)}, u32[]{:S(2)}) %collective-permute-start.1) | collective-permute-done | bytes 786464 | tf_op jit(solution)/shard_map/ppermute | solution.py:144
  164.2 1.3 bitcast_add_fusion
  165.5 0.0 copy-start
  165.5 1.1 copy-done
  166.7 0.1 fusion.4
  166.7 4.3 %collective-permute-start.2 = (bf16[24,4096]{1,0:T(8,128)(2,1)S(1)}, bf16[24,4096]{1,0:T(8,128)(2,1)S(1)}, u32[]{:S(2)}, u32[]{:S(2)}) collective-permute-start(bf16[24,4096]{1,0:T(8,128)(2,1)S(1)} %get-tuple-element.23), channel_id=1, source_target_pairs={{0,2},{1,3},{2,0},{3,1},{4,6},{5,7},{6,4},{7,5},{8,10},{9,11},{10,... | collective-permute-start | bytes 589832 | tf_op jit(solution)/shard_map/ppermute | solution.py:150
  171.0 0.0 collective-permute-start.3
  171.0 1.6 collective-permute-start.4
  172.6 5.2 %collective-permute-done.2 = bf16[24,4096]{1,0:T(8,128)(2,1)S(1)} collective-permute-done((bf16[24,4096]{1,0:T(8,128)(2,1)S(1)}, bf16[24,4096]{1,0:T(8,128)(2,1)S(1)}, u32[]{:S(2)}, u32[]{:S(2)}) %collective-permute-start.2) | collective-permute-done | bytes 196640 | tf_op jit(solution)/shard_map/ppermute | solution.py:150
  177.8 7.0 %collective-permute-done.3 = bf16[24,4096]{1,0:T(8,128)(2,1)S(1)} collective-permute-done((bf16[24,4096]{1,0:T(8,128)(2,1)S(1)}, bf16[24,4096]{1,0:T(8,128)(2,1)S(1)}, u32[]{:S(2)}, u32[]{:S(2)}) %collective-permute-start.3) | collective-permute-done | bytes 196640 | tf_op jit(solution)/shard_map/ppermute | solution.py:150
  184.8 5.4 %collective-permute-done.4 = bf16[24,4096]{1,0:T(8,128)(2,1)S(1)} collective-permute-done((bf16[24,4096]{1,0:T(8,128)(2,1)S(1)}, bf16[24,4096]{1,0:T(8,128)(2,1)S(1)}, u32[]{:S(2)}, u32[]{:S(2)}) %collective-permute-start.4) | collective-permute-done | bytes 196640 | tf_op jit(solution)/shard_map/ppermute | solution.py:150
  190.2 1.1 fusion.3
  191.3 0.0 copy-done.1
  191.3 0.8 pad_maximum_fusion.1
  (6 shorter events, 0.0 us)
Async XLA Ops:
  6.5 89.3 %copy-start.2 = (s32[384]{0:T(512)S(1)}, s32[384]{0:T(512)}, u32[]{:S(2)}) copy-start(s32[384]{0:T(512)} %param.10) | copy-start | bytes 4612
  6.5 87.7 %all-gather.3.cloned.1.call-start = ((), (), s32[]{:S(2)}) async-start(), calls=%async_computation.2 | async-start | bytes 6823936 | tf_op jit(solution)/shard_map/all_gather | solution.py:170
  9.2 15.8 %collective-permute-start = (bf16[392,256]{1,0:T(8,128)(2,1)S(1)}, bf16[392,256]{1,0:T(8,128)(2,1)S(1)}, u32[]{:S(2)}, u32[]{:S(2)}) collective-permute-start(bf16[392,256]{1,0:T(8,128)(2,1)S(1)} %get-tuple-element.29), channel_id=1, source_target_pairs={{0,128},{128,0},{1,129},{129,1},{2,130},{130,2},{3,131},{131,3},{4... | collective-permute-start | bytes 602120 | tf_op jit(solution)/shard_map/ppermute | solution.py:168
  25.8 133.1 %reduce-scatter.2.cloned.1.call-start = ((), (), s32[]{:S(2)}) async-start(), calls=%async_computation.1 | async-start | bytes 1769472 | tf_op jit(solution)/shard_map/reduce_scatter | solution.py:205
  161.6 2.6 %collective-permute-start.1 = (bf16[4,24,4096]{2,1,0:T(8,128)(2,1)}, bf16[4,24,4096]{2,1,0:T(8,128)(2,1)}, u32[]{:S(2)}, u32[]{:S(2)}) collective-permute-start(bf16[4,24,4096]{2,1,0:T(8,128)(2,1)} %fusion), channel_id=1, source_target_pairs={{0,1},{1,0},{2,3},{3,2},{4,5},{5,4},{6,7},{7,6},{8,9},{9,8},{10,11... | collective-permute-start | bytes 2359304 | tf_op jit(solution)/shard_map/ppermute | solution.py:144
  161.6 29.7 %copy-start.1 = (bf16[24,4096]{1,0:T(8,128)(2,1)S(1)}, bf16[24,4096]{1,0:T(8,128)(2,1)}, u32[]{:S(2)}) copy-start(bf16[24,4096]{1,0:T(8,128)(2,1)} %reduce-scatter.2.cloned.1.call-done) | copy-start | bytes 589828
  165.5 1.2 copy-start
  166.7 11.1 %collective-permute-start.2 = (bf16[24,4096]{1,0:T(8,128)(2,1)S(1)}, bf16[24,4096]{1,0:T(8,128)(2,1)S(1)}, u32[]{:S(2)}, u32[]{:S(2)}) collective-permute-start(bf16[24,4096]{1,0:T(8,128)(2,1)S(1)} %get-tuple-element.23), channel_id=1, source_target_pairs={{0,2},{1,3},{2,0},{3,1},{4,6},{5,7},{6,4},{7,5},{8,10},{9,11},{10,... | collective-permute-start | bytes 589832 | tf_op jit(solution)/shard_map/ppermute | solution.py:150
  171.0 13.7 %collective-permute-start.3 = (bf16[24,4096]{1,0:T(8,128)(2,1)S(1)}, bf16[24,4096]{1,0:T(8,128)(2,1)S(1)}, u32[]{:S(2)}, u32[]{:S(2)}) collective-permute-start(bf16[24,4096]{1,0:T(8,128)(2,1)S(1)} %get-tuple-element.25), channel_id=1, source_target_pairs={{0,4},{1,5},{2,6},{3,7},{4,0},{5,1},{6,2},{7,3},{8,12},{9,13},{10,... | collective-permute-start | bytes 589832 | tf_op jit(solution)/shard_map/ppermute | solution.py:150
  171.0 19.2 %collective-permute-start.4 = (bf16[24,4096]{1,0:T(8,128)(2,1)S(1)}, bf16[24,4096]{1,0:T(8,128)(2,1)S(1)}, u32[]{:S(2)}, u32[]{:S(2)}) collective-permute-start(bf16[24,4096]{1,0:T(8,128)(2,1)S(1)} %get-tuple-element.24), channel_id=1, source_target_pairs={{0,6},{1,7},{2,4},{3,5},{4,2},{5,3},{6,0},{7,1},{8,14},{9,15},{10,... | collective-permute-start | bytes 589832 | tf_op jit(solution)/shard_map/ppermute | solution.py:150
Sparse Core Ops, SparseCore 0:
  25.9 68.2 all-gather.2
  108.9 49.9 reduce-scatter.1

commit v4 on v3

--- a/solution.py
+++ b/solution.py
@@ -135,15 +135,18 @@
     )(scalars, queries, kv, kv, q_start, q_pos, after)
 
 
-def sum_over_heads(projected, n_head, piece):
+def core_step(projected, n_head, piece):
     me_head = lax.axis_index("head")
-    held = projected.reshape((n_head // 2, 2, piece) + projected.shape[1:]).astype(jnp.float32)
+    held = projected.reshape((n_head // 2, 2, piece) + projected.shape[1:])
     core = me_head % 2
     keep = lax.dynamic_index_in_dim(held, core, axis=1, keepdims=False)
     send = lax.dynamic_index_in_dim(held, 1 - core, axis=1, keepdims=False)
-    got = lax.ppermute(send.astype(jnp.bfloat16), "head", perm=[(i, i ^ 1) for i in range(n_head)])
-    held = keep + got.astype(jnp.float32)
-    chip = me_head // 2
+    got = lax.ppermute(send, "head", perm=[(i, i ^ 1) for i in range(n_head)])
+    return keep.astype(jnp.float32) + got.astype(jnp.float32)
+
+
+def chip_step(held, n_head):
+    chip = lax.axis_index("head") // 2
     total = lax.dynamic_index_in_dim(held, chip, axis=0, keepdims=False)
     for k in range(1, n_head // 2):
         send = lax.dynamic_index_in_dim(held, chip ^ k, axis=0, keepdims=False)
@@ -204,8 +207,9 @@
         if c < CHUNKS - 1:
             outs.append(lax.psum_scatter(projected, "head", scatter_dimension=0, tiled=True))
         else:
-            *outs, projected = lax.optimization_barrier((*outs, projected))
-            outs.append(sum_over_heads(projected, n_head, piece))
+            held = core_step(projected, n_head, piece)
+            *outs, held = lax.optimization_barrier((*outs, held))
+            outs.append(chip_step(held, n_head))
     return jnp.concatenate(outs, axis=0)
 
 

time: 201 us -> 195 us (0.970)
  the two profiles are of different devices: /device:TPU:32 before, /device:TPU:2 now
where the time goes in v4:
time: 195 us
  waiting for transfers between devices  133 us (68%)
  Pallas kernels  15.8 us (8%)
  between operations  13.6 us (7%)
  starting transfers between devices  11 us (6%)
  matrix products  7.74 us (4%)
  other arithmetic  7.65 us (4%)
  local copies, waits for them, and re-layouts  5.44 us (3%)
    all_gather x1, waiting for transfers between devices, per_device(): gathered = lax.all_gather(pair, 'xy')  69.3 us
    reduce_scatter x1, waiting for transfers between devices, per_device(): lax.psum_scatter(projected, 'head', scatter_dimension=0, tiled=True)  40.4 us
    pallas_call x2, Pallas kernels, attention(): pl.pallas_call(kernel, out_shape=jax.ShapeDtypeStruct((rows, width), jnp....  15.8 us
    ppermute x3, waiting for transfers between devices, chip_step(): lax.ppermute(send.astype(jnp.bfloat16), 'head', perm=[(i, i ^ 2 * k) for...  15.4 us
    dot_general x2, matrix products, per_device(): jnp.dot(attended, out_weight, preferred_element_type=jnp.float32)  7.74 us
    ppermute x1, starting transfers between devices, per_device(): partner = lax.ppermute(block, 'zh', perm=[(0, 1), (1, 0)])  7.28 us
    ppermute x1, waiting for transfers between devices, per_device(): partner = lax.ppermute(block, 'zh', perm=[(0, 1), (1, 0)])  6.02 us
  transfers between devices with their start and end apart: 7, of which 6 were waited for; matrix products, arithmetic and copies ran while one was open for 3% of the time, Pallas kernels for 4%

profile of v4, /device:TPU:2, one launch (start us, length us, event | category | flops | bytes accessed | tf_op | source)
XLA Modules:
  0.0 194.6 jit_solution(9564934561067435003)
XLA Ops:
  6.5 0.0 copy-start
  6.5 0.0 all-gather.3.cloned.1.call-start
  6.5 0.8 convert_convert_fusion
  7.3 1.0 copy.26
  8.3 0.9 fusion.7
  9.3 7.3 %collective-permute-start = (bf16[392,256]{1,0:T(8,128)(2,1)S(1)}, bf16[392,256]{1,0:T(8,128)(2,1)S(1)}, u32[]{:S(2)}, u32[]{:S(2)}) collective-permute-start(bf16[392,256]{1,0:T(8,128)(2,1)S(1)} %get-tuple-element.29), channel_id=1, source_target_pairs={{0,128},{128,0},{1,129},{129,1},{2,130},{130,2},{3,131},{131,3},{4... | collective-permute-start | bytes 602120 | tf_op jit(solution)/shard_map/ppermute | solution.py:171
  16.5 6.0 %collective-permute-done = bf16[392,256]{1,0:T(8,128)(2,1)S(1)} collective-permute-done((bf16[392,256]{1,0:T(8,128)(2,1)S(1)}, bf16[392,256]{1,0:T(8,128)(2,1)S(1)}, u32[]{:S(2)}, u32[]{:S(2)}) %collective-permute-start) | collective-permute-done | bytes 200736 | tf_op jit(solution)/shard_map/ppermute | solution.py:171
  22.6 0.8 pad_maximum_fusion
  23.3 0.0 all-gather.3.cloned.1.call-update
  23.4 0.0 reduce-scatter.2.cloned.1.call-start
  23.4 0.1 pad.9.clone
  23.5 1.8 fusion.8
  25.3 69.3 %all-gather.3.cloned.1.call-done = bf16[32,392,256]{2,1,0:T(8,128)(2,1)} async-done(((bf16[2,392,256]{2,1,0:T(8,128)(2,1)}), bf16[32,392,256]{2,1,0:T(8,128)(2,1)}) %all-gather.3.cloned.1.call-update) | async-done | bytes 6422544 | tf_op jit(solution)/shard_map/all_gather | solution.py:173
  94.6 0.9 slice_convert_fusion
  95.5 0.7 convert_reduce_fusion
  96.2 0.0 copy-done
  96.2 0.1 select_reduce_fusion
  96.3 0.1 convert_element_type.75
  96.4 0.1 and_reduce_fusion
  96.5 0.2 divide_reduce_fusion
  96.7 0.1 add_add_fusion.1
  96.8 0.1 copy.27
  96.9 0.6 reshape.129.sc_ref
  97.5 0.8 broadcast_in_dim.5.qp_ref
  98.3 0.8 broadcast_in_dim.4.qs_ref
  99.1 7.9 %shard_map.55 = bf16[192,512]{1,0:T(8,128)(2,1)} custom-call(s32[8]{0:T(128)} %reshape.129.sc_ref, bf16[192,512]{1,0:T(8,128)(2,1)} %bitcast.61, bf16[16,2,392,256]{3,2,1,0:T(8,128)(2,1)} %bitcast.53, bf16[16,2,392,256]{3,2,1,0:T(8,128)(2,1)} %bitcast.54, s32[8,2,24,128]{3,2,1,0:T(8,128)} %broadcast_in_dim.4.qs_ref, ...), custom_call_target="tpu_custom_call" | custom-call | flops 2717908992 | bytes 3932160 | tf_op jit(solution)/shard_map/pallas_call | solution.py:108
  107.0 4.4 %convolution_convert_fusion.1.after_ref = bf16[192,4096]{1,0:T(8,128)(2,1)} fusion(bf16[192,512]{1,0:T(8,128)(2,1)} %shard_map.55, bf16[512,4096]{1,0:T(8,128)(2,1)} %param.11), kind=kOutput, calls=%fused_computation.1 | convolution fusion | flops 806092800 | bytes 5963776 | tf_op jit(solution)/shard_map/dot_general | solution.py:205
  111.4 0.0 reduce-scatter.2.cloned.1.call-update
  111.5 7.9 %shard_map.56 = bf16[192,512]{1,0:T(8,128)(2,1)} custom-call(s32[8]{0:T(128)} %reshape.129.sc_ref, bf16[192,512]{1,0:T(8,128)(2,1)} %bitcast.60, bf16[16,2,392,256]{3,2,1,0:T(8,128)(2,1)} %bitcast.56, bf16[16,2,392,256]{3,2,1,0:T(8,128)(2,1)} %bitcast.57, s32[8,2,24,128]{3,2,1,0:T(8,128)} %broadcast_in_dim.4.qs_ref, ...), custom_call_target="tpu_custom_call" | custom-call | flops 2717908992 | bytes 3932160 | tf_op jit(solution)/shard_map/pallas_call | solution.py:108
  119.4 3.3 %convolution_convert_fusion = bf16[192,4096]{1,0:T(8,128)(2,1)S(1)} fusion(bf16[192,512]{1,0:T(8,128)(2,1)} %shard_map.56, bf16[512,4096]{1,0:T(8,128)(2,1)} %param.11), kind=kOutput, calls=%fused_computation | convolution fusion | flops 806092800 | bytes 5963776 | tf_op jit(solution)/shard_map/dot_general | solution.py:205
  122.7 0.1 dynamic-slice_bitcast_fusion
  122.7 0.1 collective-permute-start.1
  122.9 2.4 %collective-permute-done.1 = bf16[4,24,4096]{2,1,0:T(8,128)(2,1)} collective-permute-done((bf16[4,24,4096]{2,1,0:T(8,128)(2,1)S(1)}, bf16[4,24,4096]{2,1,0:T(8,128)(2,1)}, u32[]{:S(2)}, u32[]{:S(2)}) %collective-permute-start.1) | collective-permute-done | bytes 786464 | tf_op jit(solution)/shard_map/ppermute | solution.py:144
  125.3 1.3 convert_add_fusion
  126.6 40.4 %reduce-scatter.2.cloned.1.call-done = bf16[24,4096]{1,0:T(8,128)(2,1)} async-done(((bf16[192,4096]{1,0:T(8,128)(2,1)}), bf16[24,4096]{1,0:T(8,128)(2,1)}) %reduce-scatter.2.cloned.1.call-update) | async-done | bytes 196624 | tf_op jit(solution)/shard_map/reduce_scatter | solution.py:208
  167.0 0.1 fusion.3
  167.0 0.1 collective-permute-start.2
  167.1 0.1 collective-permute-start.4
  167.2 3.4 %collective-permute-start.3 = (bf16[24,4096]{1,0:T(8,128)(2,1)S(1)}, bf16[24,4096]{1,0:T(8,128)(2,1)S(1)}, u32[]{:S(2)}, u32[]{:S(2)}) collective-permute-start(bf16[24,4096]{1,0:T(8,128)(2,1)S(1)} %get-tuple-element.25), channel_id=1, source_target_pairs={{0,4},{1,5},{2,6},{3,7},{4,0},{5,1},{6,2},{7,3},{8,12},{9,13},{10,... | collective-permute-start | bytes 589832 | tf_op jit(solution)/shard_map/ppermute | solution.py:153
  170.6 7.5 %collective-permute-done.2 = bf16[24,4096]{1,0:T(8,128)(2,1)S(1)} collective-permute-done((bf16[24,4096]{1,0:T(8,128)(2,1)S(1)}, bf16[24,4096]{1,0:T(8,128)(2,1)S(1)}, u32[]{:S(2)}, u32[]{:S(2)}) %collective-permute-start.2) | collective-permute-done | bytes 196640 | tf_op jit(solution)/shard_map/ppermute | solution.py:153
  178.1 0.0 collective-permute-done.4
  178.1 7.9 %collective-permute-done.3 = bf16[24,4096]{1,0:T(8,128)(2,1)S(1)} collective-permute-done((bf16[24,4096]{1,0:T(8,128)(2,1)S(1)}, bf16[24,4096]{1,0:T(8,128)(2,1)S(1)}, u32[]{:S(2)}, u32[]{:S(2)}) %collective-permute-start.3) | collective-permute-done | bytes 196640 | tf_op jit(solution)/shard_map/ppermute | solution.py:153
  185.9 0.1 fusion.2
  186.0 1.7 pad_maximum_fusion.1
  (6 shorter events, 0.0 us)
Async XLA Ops:
  6.5 89.7 %copy-start = (s32[384]{0:T(512)S(1)}, s32[384]{0:T(512)}, u32[]{:S(2)}) copy-start(s32[384]{0:T(512)} %param.10) | copy-start | bytes 4612
  6.5 88.1 %all-gather.3.cloned.1.call-start = ((), (), s32[]{:S(2)}) async-start(), calls=%async_computation.2 | async-start | bytes 6823936 | tf_op jit(solution)/shard_map/all_gather | solution.py:173
  9.3 13.3 %collective-permute-start = (bf16[392,256]{1,0:T(8,128)(2,1)S(1)}, bf16[392,256]{1,0:T(8,128)(2,1)S(1)}, u32[]{:S(2)}, u32[]{:S(2)}) collective-permute-start(bf16[392,256]{1,0:T(8,128)(2,1)S(1)} %get-tuple-element.29), channel_id=1, source_target_pairs={{0,128},{128,0},{1,129},{129,1},{2,130},{130,2},{3,131},{131,3},{4... | collective-permute-start | bytes 602120 | tf_op jit(solution)/shard_map/ppermute | solution.py:171
  23.4 143.6 %reduce-scatter.2.cloned.1.call-start = ((), (), s32[]{:S(2)}) async-start(), calls=%async_computation.1 | async-start | bytes 1769472 | tf_op jit(solution)/shard_map/reduce_scatter | solution.py:208
  122.7 2.5 %collective-permute-start.1 = (bf16[4,24,4096]{2,1,0:T(8,128)(2,1)S(1)}, bf16[4,24,4096]{2,1,0:T(8,128)(2,1)}, u32[]{:S(2)}, u32[]{:S(2)}) collective-permute-start(bf16[4,24,4096]{2,1,0:T(8,128)(2,1)S(1)} %dynamic-slice_bitcast_fusion), channel_id=1, source_target_pairs={{0,1},{1,0},{2,3},{3,2},{4,5},{5,4},{6,7},{7,6},{8,9},{9,8},{10,11... | collective-permute-start | bytes 2359304 | tf_op jit(solution)/shard_map/ppermute | solution.py:144
  167.0 11.1 %collective-permute-start.2 = (bf16[24,4096]{1,0:T(8,128)(2,1)S(1)}, bf16[24,4096]{1,0:T(8,128)(2,1)S(1)}, u32[]{:S(2)}, u32[]{:S(2)}) collective-permute-start(bf16[24,4096]{1,0:T(8,128)(2,1)S(1)} %get-tuple-element.23), channel_id=1, source_target_pairs={{0,2},{1,3},{2,0},{3,1},{4,6},{5,7},{6,4},{7,5},{8,10},{9,11},{10,... | collective-permute-start | bytes 589832 | tf_op jit(solution)/shard_map/ppermute | solution.py:153
  167.1 11.0 %collective-permute-start.4 = (bf16[24,4096]{1,0:T(8,128)(2,1)S(1)}, bf16[24,4096]{1,0:T(8,128)(2,1)S(1)}, u32[]{:S(2)}, u32[]{:S(2)}) collective-permute-start(bf16[24,4096]{1,0:T(8,128)(2,1)S(1)} %get-tuple-element.24), channel_id=1, source_target_pairs={{0,6},{1,7},{2,4},{3,5},{4,2},{5,3},{6,0},{7,1},{8,14},{9,15},{10,... | collective-permute-start | bytes 589832 | tf_op jit(solution)/shard_map/ppermute | solution.py:153
  167.2 18.7 %collective-permute-start.3 = (bf16[24,4096]{1,0:T(8,128)(2,1)S(1)}, bf16[24,4096]{1,0:T(8,128)(2,1)S(1)}, u32[]{:S(2)}, u32[]{:S(2)}) collective-permute-start(bf16[24,4096]{1,0:T(8,128)(2,1)S(1)} %get-tuple-element.25), channel_id=1, source_target_pairs={{0,4},{1,5},{2,6},{3,7},{4,0},{5,1},{6,2},{7,3},{8,12},{9,13},{10,... | collective-permute-start | bytes 589832 | tf_op jit(solution)/shard_map/ppermute | solution.py:153
Sparse Core Ops, SparseCore 0:
  23.5 71.0 all-gather.2
  111.6 55.3 reduce-scatter.1

commit v5 on v4

--- a/solution.py
+++ b/solution.py
@@ -1,4 +1,5 @@
 import functools
+import math
 
 import jax
 import jax.numpy as jnp
@@ -59,7 +60,7 @@
             part = None
             pv = None
             for c in range(cols):
-                p = jnp.exp((s[c] - m_b) * scale)
+                p = jnp.exp2((s[c] - m_b) * scale)
                 if masked:
                     p = jnp.where(allowed[c], p, 0.0)
                 part = p if part is None else part + p
@@ -67,7 +68,7 @@
                     p.astype(jnp.bfloat16), v_ref[c * LANES:(c + 1) * LANES, :], preferred_element_type=jnp.float32
                 )
                 pv = term if pv is None else pv + term
-            alpha = jnp.exp((m_prev - m_next) * scale)
+            alpha = jnp.exp2((m_prev - m_next) * scale)
             l_sc[h] = alpha * l_sc[h] + part
             acc_sc[h] = alpha[:, 0:1] * acc_sc[h] + pv
             m_sc[h] = m_next
@@ -94,7 +95,7 @@
     rows, width = queries.shape
     heads = width // HEAD_WIDTH
     steps = -(-(MOST - 1) // shard_rows) + 1
-    scale = HEAD_WIDTH ** (-0.5)
+    scale = HEAD_WIDTH ** (-0.5) * math.log2(math.e)
 
     at = 4 * chunk
 

time: 195 us -> 193 us (0.990)
  Pallas kernels: 15.8 us -> 13.1 us
    pallas_call x2, Pallas kernels: 15.8 us -> 13.1 us  [attention(): pl.pallas_call(kernel, out_shape=jax.ShapeDtypeStruct((rows, width), jnp....]
  transfers between devices with their start and end apart: 7 -> 7, of which waited for: 6 -> 6; matrix products, arithmetic and copies ran while one was open for 3% -> 3% of each run, Pallas kernels for 4% -> 3%
where the time goes in v5:
time: 193 us
  waiting for transfers between devices  134 us (69%)
  between operations  13.6 us (7%)
  Pallas kernels  13.1 us (7%)
  starting transfers between devices  11 us (6%)
  matrix products  7.73 us (4%)
  other arithmetic  7.65 us (4%)
  local copies, waits for them, and re-layouts  5.44 us (3%)
    all_gather x1, waiting for transfers between devices, per_device(): gathered = lax.all_gather(pair, 'xy')  69.3 us
    reduce_scatter x1, waiting for transfers between devices, per_device(): lax.psum_scatter(projected, 'head', scatter_dimension=0, tiled=True)  41.1 us
    ppermute x3, waiting for transfers between devices, chip_step(): lax.ppermute(send.astype(jnp.bfloat16), 'head', perm=[(i, i ^ 2 * k) for...  15.5 us
    pallas_call x2, Pallas kernels, attention(): pl.pallas_call(kernel, out_shape=jax.ShapeDtypeStruct((rows, width), jnp....  13.1 us
    dot_general x2, matrix products, per_device(): jnp.dot(attended, out_weight, preferred_element_type=jnp.float32)  7.73 us
    ppermute x1, starting transfers between devices, per_device(): partner = lax.ppermute(block, 'zh', perm=[(0, 1), (1, 0)])  7.28 us
    ppermute x1, waiting for transfers between devices, per_device(): partner = lax.ppermute(block, 'zh', perm=[(0, 1), (1, 0)])  6.02 us
  transfers between devices with their start and end apart: 7, of which 6 were waited for; matrix products, arithmetic and copies ran while one was open for 3% of the time, Pallas kernels for 3%

profile of v5, /device:TPU:2, one launch (start us, length us, event | category | flops | bytes accessed | tf_op | source)
XLA Modules:
  0.0 192.8 jit_solution(3454524999522652361)
XLA Ops:
  6.5 0.0 copy-start
  6.5 0.0 all-gather.3.cloned.1.call-start
  6.5 0.8 convert_convert_fusion
  7.3 1.0 copy.26
  8.3 0.9 fusion.7
  9.3 7.3 %collective-permute-start = (bf16[392,256]{1,0:T(8,128)(2,1)S(1)}, bf16[392,256]{1,0:T(8,128)(2,1)S(1)}, u32[]{:S(2)}, u32[]{:S(2)}) collective-permute-start(bf16[392,256]{1,0:T(8,128)(2,1)S(1)} %get-tuple-element.29), channel_id=1, source_target_pairs={{0,128},{128,0},{1,129},{129,1},{2,130},{130,2},{3,131},{131,3},{4... | collective-permute-start | bytes 602120 | tf_op jit(solution)/shard_map/ppermute | solution.py:172
  16.5 6.0 %collective-permute-done = bf16[392,256]{1,0:T(8,128)(2,1)S(1)} collective-permute-done((bf16[392,256]{1,0:T(8,128)(2,1)S(1)}, bf16[392,256]{1,0:T(8,128)(2,1)S(1)}, u32[]{:S(2)}, u32[]{:S(2)}) %collective-permute-start) | collective-permute-done | bytes 200736 | tf_op jit(solution)/shard_map/ppermute | solution.py:172
  22.6 0.8 pad_maximum_fusion
  23.3 0.0 all-gather.3.cloned.1.call-update
  23.4 0.0 reduce-scatter.2.cloned.1.call-start
  23.4 0.1 pad.9.clone
  23.5 1.8 fusion.8
  25.3 69.3 %all-gather.3.cloned.1.call-done = bf16[32,392,256]{2,1,0:T(8,128)(2,1)} async-done(((bf16[2,392,256]{2,1,0:T(8,128)(2,1)}), bf16[32,392,256]{2,1,0:T(8,128)(2,1)}) %all-gather.3.cloned.1.call-update) | async-done | bytes 6422544 | tf_op jit(solution)/shard_map/all_gather | solution.py:174
  94.6 0.9 slice_convert_fusion
  95.5 0.7 convert_reduce_fusion
  96.2 0.0 copy-done
  96.2 0.1 select_reduce_fusion
  96.3 0.1 convert_element_type.75
  96.4 0.1 and_reduce_fusion
  96.5 0.2 divide_reduce_fusion
  96.7 0.1 add_add_fusion.1
  96.8 0.1 copy.27
  96.9 0.6 reshape.129.sc_ref
  97.5 0.8 broadcast_in_dim.5.qp_ref
  98.3 0.8 broadcast_in_dim.4.qs_ref
  99.1 6.5 %shard_map.55 = bf16[192,512]{1,0:T(8,128)(2,1)} custom-call(s32[8]{0:T(128)} %reshape.129.sc_ref, bf16[192,512]{1,0:T(8,128)(2,1)} %bitcast.61, bf16[16,2,392,256]{3,2,1,0:T(8,128)(2,1)} %bitcast.53, bf16[16,2,392,256]{3,2,1,0:T(8,128)(2,1)} %bitcast.54, s32[8,2,24,128]{3,2,1,0:T(8,128)} %broadcast_in_dim.4.qs_ref, ...), custom_call_target="tpu_custom_call" | custom-call | flops 2717908992 | bytes 3932160 | tf_op jit(solution)/shard_map/pallas_call | solution.py:109
  105.7 4.4 %convolution_convert_fusion.1.after_ref = bf16[192,4096]{1,0:T(8,128)(2,1)} fusion(bf16[192,512]{1,0:T(8,128)(2,1)} %shard_map.55, bf16[512,4096]{1,0:T(8,128)(2,1)} %param.11), kind=kOutput, calls=%fused_computation.1 | convolution fusion | flops 806092800 | bytes 5963776 | tf_op jit(solution)/shard_map/dot_general | solution.py:206
  110.1 0.0 reduce-scatter.2.cloned.1.call-update
  110.1 6.5 %shard_map.56 = bf16[192,512]{1,0:T(8,128)(2,1)} custom-call(s32[8]{0:T(128)} %reshape.129.sc_ref, bf16[192,512]{1,0:T(8,128)(2,1)} %bitcast.60, bf16[16,2,392,256]{3,2,1,0:T(8,128)(2,1)} %bitcast.56, bf16[16,2,392,256]{3,2,1,0:T(8,128)(2,1)} %bitcast.57, s32[8,2,24,128]{3,2,1,0:T(8,128)} %broadcast_in_dim.4.qs_ref, ...), custom_call_target="tpu_custom_call" | custom-call | flops 2717908992 | bytes 3932160 | tf_op jit(solution)/shard_map/pallas_call | solution.py:109
  116.7 3.3 %convolution_convert_fusion = bf16[192,4096]{1,0:T(8,128)(2,1)S(1)} fusion(bf16[192,512]{1,0:T(8,128)(2,1)} %shard_map.56, bf16[512,4096]{1,0:T(8,128)(2,1)} %param.11), kind=kOutput, calls=%fused_computation | convolution fusion | flops 806092800 | bytes 5963776 | tf_op jit(solution)/shard_map/dot_general | solution.py:206
  120.0 0.1 dynamic-slice_bitcast_fusion
  120.1 0.1 collective-permute-start.1
  120.2 2.4 %collective-permute-done.1 = bf16[4,24,4096]{2,1,0:T(8,128)(2,1)} collective-permute-done((bf16[4,24,4096]{2,1,0:T(8,128)(2,1)S(1)}, bf16[4,24,4096]{2,1,0:T(8,128)(2,1)}, u32[]{:S(2)}, u32[]{:S(2)}) %collective-permute-start.1) | collective-permute-done | bytes 786464 | tf_op jit(solution)/shard_map/ppermute | solution.py:145
  122.6 1.3 convert_add_fusion
  123.9 41.1 %reduce-scatter.2.cloned.1.call-done = bf16[24,4096]{1,0:T(8,128)(2,1)} async-done(((bf16[192,4096]{1,0:T(8,128)(2,1)}), bf16[24,4096]{1,0:T(8,128)(2,1)}) %reduce-scatter.2.cloned.1.call-update) | async-done | bytes 196624 | tf_op jit(solution)/shard_map/reduce_scatter | solution.py:209
  165.0 0.1 fusion.3
  165.1 0.1 collective-permute-start.2
  165.2 0.1 collective-permute-start.4
  165.3 3.4 %collective-permute-start.3 = (bf16[24,4096]{1,0:T(8,128)(2,1)S(1)}, bf16[24,4096]{1,0:T(8,128)(2,1)S(1)}, u32[]{:S(2)}, u32[]{:S(2)}) collective-permute-start(bf16[24,4096]{1,0:T(8,128)(2,1)S(1)} %get-tuple-element.25), channel_id=1, source_target_pairs={{0,4},{1,5},{2,6},{3,7},{4,0},{5,1},{6,2},{7,3},{8,12},{9,13},{10,... | collective-permute-start | bytes 589832 | tf_op jit(solution)/shard_map/ppermute | solution.py:154
  168.7 7.4 %collective-permute-done.2 = bf16[24,4096]{1,0:T(8,128)(2,1)S(1)} collective-permute-done((bf16[24,4096]{1,0:T(8,128)(2,1)S(1)}, bf16[24,4096]{1,0:T(8,128)(2,1)S(1)}, u32[]{:S(2)}, u32[]{:S(2)}) %collective-permute-start.2) | collective-permute-done | bytes 196640 | tf_op jit(solution)/shard_map/ppermute | solution.py:154
  176.0 0.0 collective-permute-done.4
  176.0 8.1 %collective-permute-done.3 = bf16[24,4096]{1,0:T(8,128)(2,1)S(1)} collective-permute-done((bf16[24,4096]{1,0:T(8,128)(2,1)S(1)}, bf16[24,4096]{1,0:T(8,128)(2,1)S(1)}, u32[]{:S(2)}, u32[]{:S(2)}) %collective-permute-start.3) | collective-permute-done | bytes 196640 | tf_op jit(solution)/shard_map/ppermute | solution.py:154
  184.1 0.1 fusion.2
  184.2 1.7 pad_maximum_fusion.1
  (6 shorter events, 0.0 us)
Async XLA Ops:
  6.5 89.7 %copy-start = (s32[384]{0:T(512)S(1)}, s32[384]{0:T(512)}, u32[]{:S(2)}) copy-start(s32[384]{0:T(512)} %param.10) | copy-start | bytes 4612
  6.5 88.1 %all-gather.3.cloned.1.call-start = ((), (), s32[]{:S(2)}) async-start(), calls=%async_computation.2 | async-start | bytes 6823936 | tf_op jit(solution)/shard_map/all_gather | solution.py:174
  9.3 13.3 %collective-permute-start = (bf16[392,256]{1,0:T(8,128)(2,1)S(1)}, bf16[392,256]{1,0:T(8,128)(2,1)S(1)}, u32[]{:S(2)}, u32[]{:S(2)}) collective-permute-start(bf16[392,256]{1,0:T(8,128)(2,1)S(1)} %get-tuple-element.29), channel_id=1, source_target_pairs={{0,128},{128,0},{1,129},{129,1},{2,130},{130,2},{3,131},{131,3},{4... | collective-permute-start | bytes 602120 | tf_op jit(solution)/shard_map/ppermute | solution.py:172
  23.4 141.7 %reduce-scatter.2.cloned.1.call-start = ((), (), s32[]{:S(2)}) async-start(), calls=%async_computation.1 | async-start | bytes 1769472 | tf_op jit(solution)/shard_map/reduce_scatter | solution.py:209
  120.1 2.5 %collective-permute-start.1 = (bf16[4,24,4096]{2,1,0:T(8,128)(2,1)S(1)}, bf16[4,24,4096]{2,1,0:T(8,128)(2,1)}, u32[]{:S(2)}, u32[]{:S(2)}) collective-permute-start(bf16[4,24,4096]{2,1,0:T(8,128)(2,1)S(1)} %dynamic-slice_bitcast_fusion), channel_id=1, source_target_pairs={{0,1},{1,0},{2,3},{3,2},{4,5},{5,4},{6,7},{7,6},{8,9},{9,8},{10,11... | collective-permute-start | bytes 2359304 | tf_op jit(solution)/shard_map/ppermute | solution.py:145
  165.1 10.9 %collective-permute-start.2 = (bf16[24,4096]{1,0:T(8,128)(2,1)S(1)}, bf16[24,4096]{1,0:T(8,128)(2,1)S(1)}, u32[]{:S(2)}, u32[]{:S(2)}) collective-permute-start(bf16[24,4096]{1,0:T(8,128)(2,1)S(1)} %get-tuple-element.23), channel_id=1, source_target_pairs={{0,2},{1,3},{2,0},{3,1},{4,6},{5,7},{6,4},{7,5},{8,10},{9,11},{10,... | collective-permute-start | bytes 589832 | tf_op jit(solution)/shard_map/ppermute | solution.py:154
  165.2 10.8 %collective-permute-start.4 = (bf16[24,4096]{1,0:T(8,128)(2,1)S(1)}, bf16[24,4096]{1,0:T(8,128)(2,1)S(1)}, u32[]{:S(2)}, u32[]{:S(2)}) collective-permute-start(bf16[24,4096]{1,0:T(8,128)(2,1)S(1)} %get-tuple-element.24), channel_id=1, source_target_pairs={{0,6},{1,7},{2,4},{3,5},{4,2},{5,3},{6,0},{7,1},{8,14},{9,15},{10,... | collective-permute-start | bytes 589832 | tf_op jit(solution)/shard_map/ppermute | solution.py:154
  165.3 18.9 %collective-permute-start.3 = (bf16[24,4096]{1,0:T(8,128)(2,1)S(1)}, bf16[24,4096]{1,0:T(8,128)(2,1)S(1)}, u32[]{:S(2)}, u32[]{:S(2)}) collective-permute-start(bf16[24,4096]{1,0:T(8,128)(2,1)S(1)} %get-tuple-element.25), channel_id=1, source_target_pairs={{0,4},{1,5},{2,6},{3,7},{4,0},{5,1},{6,2},{7,3},{8,12},{9,13},{10,... | collective-permute-start | bytes 589832 | tf_op jit(solution)/shard_map/ppermute | solution.py:154
Sparse Core Ops, SparseCore 0:
  23.5 71.0 all-gather.2
  110.2 54.7 reduce-scatter.1

commit v6 on v4

--- a/solution.py
+++ b/solution.py
@@ -17,14 +17,15 @@
 
 
 def attn_kernel(
-    steps, shard_rows, heads, scale, at, sc_ref, q_ref, k_ref, v_ref, qs_ref, qp_ref, after_ref, o_ref, m_sc, l_sc, acc_sc
+    steps, per_step, shard_rows, heads, scale, at,
+    sc_ref, q_ref, k0_ref, v0_ref, k1_ref, v1_ref, qs_ref, qp_ref, after_ref, o_ref, m_sc, l_sc, acc_sc,
 ):
     j = pl.program_id(0)
     me = sc_ref[at]
     first = sc_ref[at + 1]
     q_last_start = sc_ref[at + 2]
-    shard = me - (steps - 1) + j
     rows = q_ref.shape[0]
+    grid_steps = steps // per_step
 
     @pl.when(j == 0)
     def _init():
@@ -32,7 +33,7 @@
         l_sc[...] = jnp.zeros(l_sc.shape, jnp.float32)
         acc_sc[...] = jnp.zeros(acc_sc.shape, jnp.float32)
 
-    def block(masked):
+    def block(masked, shard, k_ref, v_ref):
         cols = shard_rows // LANES
         if masked:
             lane = lax.broadcasted_iota(jnp.int32, (rows, LANES), 1)
@@ -72,18 +73,14 @@
             acc_sc[h] = alpha[:, 0:1] * acc_sc[h] + pv
             m_sc[h] = m_next
 
-    live = shard >= first
-    full = (shard < me) & (shard * shard_rows >= q_last_start)
-
-    @pl.when(live & full)
-    def _full():
-        block(False)
-
-    @pl.when(live & jnp.logical_not(full))
-    def _masked():
-        block(True)
-
-    @pl.when(j == steps - 1)
+    for sub, (k_ref, v_ref) in enumerate(((k0_ref, v0_ref), (k1_ref, v1_ref))):
+        shard = me - (steps - 1) + j * per_step + sub
+        live = shard >= first
+        full = (shard < me) & (shard * shard_rows >= q_last_start)
+        pl.when(live & full)(functools.partial(block, False, shard, k_ref, v_ref))
+        pl.when(live & jnp.logical_not(full))(functools.partial(block, True, shard, k_ref, v_ref))
+
+    @pl.when(j == grid_steps - 1)
     def _finish():
         for h in range(heads):
             denominator = jnp.sum(l_sc[h], axis=1, keepdims=True)
@@ -98,23 +95,28 @@
 
     at = 4 * chunk
 
-    def index(j, sc, half):
-        s = jnp.maximum(sc[at] - (steps - 1) + j, sc[at + 1])
+    per_step = 2
+    steps = -(-steps // per_step) * per_step
+
+    def index(j, sc, sub, half):
+        s = jnp.maximum(sc[at] - (steps - 1) + j * per_step + sub, sc[at + 1])
         slot = jnp.where(s // n_xy == sc[at + 3], 0, 1)
         return (s % n_xy, slot, 0, half)
 
     groups, _, piece, _ = q_start.shape
-    kernel = functools.partial(attn_kernel, steps, shard_rows, heads, scale, at)
+    kernel = functools.partial(attn_kernel, steps, per_step, shard_rows, heads, scale, at)
     return pl.pallas_call(
         kernel,
         out_shape=jax.ShapeDtypeStruct((rows, width), jnp.bfloat16),
         grid_spec=pltpu.PrefetchScalarGridSpec(
             num_scalar_prefetch=1,
-            grid=(steps,),
+            grid=(steps // per_step,),
             in_specs=[
                 pl.BlockSpec((rows, width), lambda j, sc: (0, 0)),
-                pl.BlockSpec((None, None, shard_rows, HEAD_WIDTH), lambda j, sc: index(j, sc, 0)),
-                pl.BlockSpec((None, None, shard_rows, HEAD_WIDTH), lambda j, sc: index(j, sc, 1)),
+                pl.BlockSpec((None, None, shard_rows, HEAD_WIDTH), lambda j, sc: index(j, sc, 0, 0)),
+                pl.BlockSpec((None, None, shard_rows, HEAD_WIDTH), lambda j, sc: index(j, sc, 0, 1)),
+                pl.BlockSpec((None, None, shard_rows, HEAD_WIDTH), lambda j, sc: index(j, sc, 1, 0)),
+                pl.BlockSpec((None, None, shard_rows, HEAD_WIDTH), lambda j, sc: index(j, sc, 1, 1)),
                 pl.BlockSpec((groups, None, piece, LANES), lambda j, sc: (0, chunk, 0, 0)),
                 pl.BlockSpec((groups, None, piece, LANES), lambda j, sc: (0, chunk, 0, 0)),
                 pl.BlockSpec(memory_space=pl.ANY),
@@ -132,7 +134,7 @@
             transcendentals=steps * heads * rows * shard_rows,
             bytes_accessed=steps * shard_rows * 2 * HEAD_WIDTH * 2 + 2 * rows * width * 2,
         ),
-    )(scalars, queries, kv, kv, q_start, q_pos, after)
+    )(scalars, queries, kv, kv, kv, kv, q_start, q_pos, after)
 
 
 def core_step(projected, n_head, piece):

time: 195 us -> 192 us (0.985)
  waiting for transfers between devices: 133 us -> 125 us
  Pallas kernels: 15.8 us -> 20.2 us
    reduce_scatter x1, waiting for transfers between devices: 40.4 us -> 31.8 us  [per_device(): lax.psum_scatter(projected, 'head', scatter_dimension=0, tiled=True)]
    pallas_call x2, Pallas kernels: 15.8 us -> 20.2 us  [attention(): pl.pallas_call(kernel, out_shape=jax.ShapeDtypeStruct((rows, width), jnp....]
  transfers between devices with their start and end apart: 7 -> 7, of which waited for: 6 -> 6; matrix products, arithmetic and copies ran while one was open for 3% -> 3% of each run, Pallas kernels for 4% -> 5%
where the time goes in v6:
time: 192 us; the launch traced here: 191 us
  waiting for transfers between devices  125 us (65%)
  Pallas kernels  20.2 us (11%)
  between operations  13.6 us (7%)
  starting transfers between devices  11 us (6%)
  matrix products  7.73 us (4%)
  other arithmetic  7.65 us (4%)
  local copies, waits for them, and re-layouts  5.44 us (3%)
    all_gather x1, waiting for transfers between devices, per_device(): gathered = lax.all_gather(pair, 'xy')  69.3 us
    reduce_scatter x1, waiting for transfers between devices, per_device(): lax.psum_scatter(projected, 'head', scatter_dimension=0, tiled=True)  31.8 us
    pallas_call x2, Pallas kernels, attention(): pl.pallas_call(kernel, out_shape=jax.ShapeDtypeStruct((rows, width), jnp....  20.2 us
    ppermute x3, waiting for transfers between devices, chip_step(): lax.ppermute(send.astype(jnp.bfloat16), 'head', perm=[(i, i ^ 2 * k) for...  15.6 us
    dot_general x2, matrix products, per_device(): jnp.dot(attended, out_weight, preferred_element_type=jnp.float32)  7.73 us
    ppermute x1, starting transfers between devices, per_device(): partner = lax.ppermute(block, 'zh', perm=[(0, 1), (1, 0)])  7.28 us
    ppermute x1, waiting for transfers between devices, per_device(): partner = lax.ppermute(block, 'zh', perm=[(0, 1), (1, 0)])  6.02 us
  transfers between devices with their start and end apart: 7, of which 6 were waited for; matrix products, arithmetic and copies ran while one was open for 3% of the time, Pallas kernels for 5%

profile of v6, /device:TPU:2, one launch (start us, length us, event | category | flops | bytes accessed | tf_op | source)
XLA Modules:
  0.0 190.7 jit_solution(1626709095486889272)
XLA Ops:
  6.5 0.0 copy-start
  6.5 0.0 all-gather.3.cloned.1.call-start
  6.5 0.8 convert_convert_fusion
  7.3 1.0 copy.26
  8.3 0.9 fusion.7
  9.3 7.3 %collective-permute-start = (bf16[392,256]{1,0:T(8,128)(2,1)S(1)}, bf16[392,256]{1,0:T(8,128)(2,1)S(1)}, u32[]{:S(2)}, u32[]{:S(2)}) collective-permute-start(bf16[392,256]{1,0:T(8,128)(2,1)S(1)} %get-tuple-element.29), channel_id=1, source_target_pairs={{0,128},{128,0},{1,129},{129,1},{2,130},{130,2},{3,131},{131,3},{4... | collective-permute-start | bytes 602120 | tf_op jit(solution)/shard_map/ppermute | solution.py:173
  16.5 6.0 %collective-permute-done = bf16[392,256]{1,0:T(8,128)(2,1)S(1)} collective-permute-done((bf16[392,256]{1,0:T(8,128)(2,1)S(1)}, bf16[392,256]{1,0:T(8,128)(2,1)S(1)}, u32[]{:S(2)}, u32[]{:S(2)}) %collective-permute-start) | collective-permute-done | bytes 200736 | tf_op jit(solution)/shard_map/ppermute | solution.py:173
  22.6 0.8 pad_maximum_fusion
  23.3 0.0 all-gather.3.cloned.1.call-update
  23.4 0.0 reduce-scatter.2.cloned.1.call-start
  23.4 0.1 pad.9.clone
  23.5 1.8 fusion.8
  25.3 69.3 %all-gather.3.cloned.1.call-done = bf16[32,392,256]{2,1,0:T(8,128)(2,1)} async-done(((bf16[2,392,256]{2,1,0:T(8,128)(2,1)}), bf16[32,392,256]{2,1,0:T(8,128)(2,1)}) %all-gather.3.cloned.1.call-update) | async-done | bytes 6422544 | tf_op jit(solution)/shard_map/all_gather | solution.py:175
  94.6 0.9 slice_convert_fusion
  95.5 0.7 convert_reduce_fusion
  96.2 0.0 copy-done
  96.2 0.1 select_reduce_fusion
  96.3 0.1 convert_element_type.75
  96.4 0.1 and_reduce_fusion
  96.5 0.2 divide_reduce_fusion
  96.7 0.1 add_add_fusion.1
  96.8 0.1 copy.27
  96.9 0.6 reshape.129.sc_ref
  97.5 0.8 broadcast_in_dim.5.qp_ref
  98.3 0.8 broadcast_in_dim.4.qs_ref
  99.1 10.1 %shard_map.55 = bf16[192,512]{1,0:T(8,128)(2,1)} custom-call(s32[8]{0:T(128)} %reshape.129.sc_ref, bf16[192,512]{1,0:T(8,128)(2,1)} %bitcast.65, bf16[16,2,392,256]{3,2,1,0:T(8,128)(2,1)} %bitcast.53, bf16[16,2,392,256]{3,2,1,0:T(8,128)(2,1)} %bitcast.54, bf16[16,2,392,256]{3,2,1,0:T(8,128)(2,1)} %bitcast.55, bf16[16,2,392,256]{3,2,1,0:T(8,128)(2,1)} %bitcast.56, ...), custom_call_target="tpu_custom_call" | custom-call | flops 2717908992 | bytes 3932160 | tf_op jit(solution)/shard_map/pallas_call | solution.py:108
  109.2 4.4 %convolution_convert_fusion.1.after_ref = bf16[192,4096]{1,0:T(8,128)(2,1)} fusion(bf16[192,512]{1,0:T(8,128)(2,1)} %shard_map.55, bf16[512,4096]{1,0:T(8,128)(2,1)} %param.11), kind=kOutput, calls=%fused_computation.1 | convolution fusion | flops 806092800 | bytes 5963776 | tf_op jit(solution)/shard_map/dot_general | solution.py:207
  113.6 0.0 reduce-scatter.2.cloned.1.call-update
  113.7 10.1 %shard_map.56 = bf16[192,512]{1,0:T(8,128)(2,1)} custom-call(s32[8]{0:T(128)} %reshape.129.sc_ref, bf16[192,512]{1,0:T(8,128)(2,1)} %bitcast.64, bf16[16,2,392,256]{3,2,1,0:T(8,128)(2,1)} %bitcast.58, bf16[16,2,392,256]{3,2,1,0:T(8,128)(2,1)} %bitcast.59, bf16[16,2,392,256]{3,2,1,0:T(8,128)(2,1)} %bitcast.60, bf16[16,2,392,256]{3,2,1,0:T(8,128)(2,1)} %bitcast.61, ...), custom_call_target="tpu_custom_call" | custom-call | flops 2717908992 | bytes 3932160 | tf_op jit(solution)/shard_map/pallas_call | solution.py:108
  123.8 3.3 %convolution_convert_fusion = bf16[192,4096]{1,0:T(8,128)(2,1)S(1)} fusion(bf16[192,512]{1,0:T(8,128)(2,1)} %shard_map.56, bf16[512,4096]{1,0:T(8,128)(2,1)} %param.11), kind=kOutput, calls=%fused_computation | convolution fusion | flops 806092800 | bytes 5963776 | tf_op jit(solution)/shard_map/dot_general | solution.py:207
  127.1 0.1 dynamic-slice_bitcast_fusion
  127.1 0.1 collective-permute-start.1
  127.3 2.4 %collective-permute-done.1 = bf16[4,24,4096]{2,1,0:T(8,128)(2,1)} collective-permute-done((bf16[4,24,4096]{2,1,0:T(8,128)(2,1)S(1)}, bf16[4,24,4096]{2,1,0:T(8,128)(2,1)}, u32[]{:S(2)}, u32[]{:S(2)}) %collective-permute-start.1) | collective-permute-done | bytes 786464 | tf_op jit(solution)/shard_map/ppermute | solution.py:146
  129.6 1.3 convert_add_fusion
  131.0 31.8 %reduce-scatter.2.cloned.1.call-done = bf16[24,4096]{1,0:T(8,128)(2,1)} async-done(((bf16[192,4096]{1,0:T(8,128)(2,1)}), bf16[24,4096]{1,0:T(8,128)(2,1)}) %reduce-scatter.2.cloned.1.call-update) | async-done | bytes 196624 | tf_op jit(solution)/shard_map/reduce_scatter | solution.py:210
  162.8 0.1 fusion.3
  162.8 0.1 collective-permute-start.2
  162.9 0.1 collective-permute-start.4
  163.0 3.4 %collective-permute-start.3 = (bf16[24,4096]{1,0:T(8,128)(2,1)S(1)}, bf16[24,4096]{1,0:T(8,128)(2,1)S(1)}, u32[]{:S(2)}, u32[]{:S(2)}) collective-permute-start(bf16[24,4096]{1,0:T(8,128)(2,1)S(1)} %get-tuple-element.25), channel_id=1, source_target_pairs={{0,4},{1,5},{2,6},{3,7},{4,0},{5,1},{6,2},{7,3},{8,12},{9,13},{10,... | collective-permute-start | bytes 589832 | tf_op jit(solution)/shard_map/ppermute | solution.py:155
  166.4 7.2 %collective-permute-done.2 = bf16[24,4096]{1,0:T(8,128)(2,1)S(1)} collective-permute-done((bf16[24,4096]{1,0:T(8,128)(2,1)S(1)}, bf16[24,4096]{1,0:T(8,128)(2,1)S(1)}, u32[]{:S(2)}, u32[]{:S(2)}) %collective-permute-start.2) | collective-permute-done | bytes 196640 | tf_op jit(solution)/shard_map/ppermute | solution.py:155
  173.6 0.0 collective-permute-done.4
  173.6 8.4 %collective-permute-done.3 = bf16[24,4096]{1,0:T(8,128)(2,1)S(1)} collective-permute-done((bf16[24,4096]{1,0:T(8,128)(2,1)S(1)}, bf16[24,4096]{1,0:T(8,128)(2,1)S(1)}, u32[]{:S(2)}, u32[]{:S(2)}) %collective-permute-start.3) | collective-permute-done | bytes 196640 | tf_op jit(solution)/shard_map/ppermute | solution.py:155
  182.0 0.1 fusion.2
  182.1 1.7 pad_maximum_fusion.1
  (6 shorter events, 0.0 us)
Async XLA Ops:
  6.5 89.7 %copy-start = (s32[384]{0:T(512)S(1)}, s32[384]{0:T(512)}, u32[]{:S(2)}) copy-start(s32[384]{0:T(512)} %param.10) | copy-start | bytes 4612
  6.5 88.1 %all-gather.3.cloned.1.call-start = ((), (), s32[]{:S(2)}) async-start(), calls=%async_computation.2 | async-start | bytes 6823936 | tf_op jit(solution)/shard_map/all_gather | solution.py:175
  9.3 13.3 %collective-permute-start = (bf16[392,256]{1,0:T(8,128)(2,1)S(1)}, bf16[392,256]{1,0:T(8,128)(2,1)S(1)}, u32[]{:S(2)}, u32[]{:S(2)}) collective-permute-start(bf16[392,256]{1,0:T(8,128)(2,1)S(1)} %get-tuple-element.29), channel_id=1, source_target_pairs={{0,128},{128,0},{1,129},{129,1},{2,130},{130,2},{3,131},{131,3},{4... | collective-permute-start | bytes 602120 | tf_op jit(solution)/shard_map/ppermute | solution.py:173
  23.4 139.4 %reduce-scatter.2.cloned.1.call-start = ((), (), s32[]{:S(2)}) async-start(), calls=%async_computation.1 | async-start | bytes 1769472 | tf_op jit(solution)/shard_map/reduce_scatter | solution.py:210
  127.1 2.5 %collective-permute-start.1 = (bf16[4,24,4096]{2,1,0:T(8,128)(2,1)S(1)}, bf16[4,24,4096]{2,1,0:T(8,128)(2,1)}, u32[]{:S(2)}, u32[]{:S(2)}) collective-permute-start(bf16[4,24,4096]{2,1,0:T(8,128)(2,1)S(1)} %dynamic-slice_bitcast_fusion), channel_id=1, source_target_pairs={{0,1},{1,0},{2,3},{3,2},{4,5},{5,4},{6,7},{7,6},{8,9},{9,8},{10,11... | collective-permute-start | bytes 2359304 | tf_op jit(solution)/shard_map/ppermute | solution.py:146
  162.8 10.8 %collective-permute-start.2 = (bf16[24,4096]{1,0:T(8,128)(2,1)S(1)}, bf16[24,4096]{1,0:T(8,128)(2,1)S(1)}, u32[]{:S(2)}, u32[]{:S(2)}) collective-permute-start(bf16[24,4096]{1,0:T(8,128)(2,1)S(1)} %get-tuple-element.23), channel_id=1, source_target_pairs={{0,2},{1,3},{2,0},{3,1},{4,6},{5,7},{6,4},{7,5},{8,10},{9,11},{10,... | collective-permute-start | bytes 589832 | tf_op jit(solution)/shard_map/ppermute | solution.py:155
  162.9 10.7 %collective-permute-start.4 = (bf16[24,4096]{1,0:T(8,128)(2,1)S(1)}, bf16[24,4096]{1,0:T(8,128)(2,1)S(1)}, u32[]{:S(2)}, u32[]{:S(2)}) collective-permute-start(bf16[24,4096]{1,0:T(8,128)(2,1)S(1)} %get-tuple-element.24), channel_id=1, source_target_pairs={{0,6},{1,7},{2,4},{3,5},{4,2},{5,3},{6,0},{7,1},{8,14},{9,15},{10,... | collective-permute-start | bytes 589832 | tf_op jit(solution)/shard_map/ppermute | solution.py:155
  163.0 19.0 %collective-permute-start.3 = (bf16[24,4096]{1,0:T(8,128)(2,1)S(1)}, bf16[24,4096]{1,0:T(8,128)(2,1)S(1)}, u32[]{:S(2)}, u32[]{:S(2)}) collective-permute-start(bf16[24,4096]{1,0:T(8,128)(2,1)S(1)} %get-tuple-element.25), channel_id=1, source_target_pairs={{0,4},{1,5},{2,6},{3,7},{4,0},{5,1},{6,2},{7,3},{8,12},{9,13},{10,... | collective-permute-start | bytes 589832 | tf_op jit(solution)/shard_map/ppermute | solution.py:155
Sparse Core Ops, SparseCore 0:
  23.5 71.0 all-gather.2
  113.8 48.9 reduce-scatter.1

commit v7 on v4

--- a/solution.py
+++ b/solution.py
@@ -14,6 +14,7 @@
 DOCS = 16
 NEG = -1e30
 CHUNKS = 2
+HALVES = 2
 
 
 def attn_kernel(
@@ -34,43 +35,46 @@
 
     def block(masked):
         cols = shard_rows // LANES
-        if masked:
-            lane = lax.broadcasted_iota(jnp.int32, (rows, LANES), 1)
-            q_start = qs_ref[...].reshape(rows, LANES)[:, 0:1]
-            q_pos = qp_ref[...].reshape(rows, LANES)[:, 0:1]
-            allowed = []
-            for c in range(cols):
-                k_pos = shard * shard_rows + c * LANES + lane
-                allowed.append((k_pos >= q_start) & (k_pos <= q_pos))
-        for h in range(heads):
-            qh = q_ref[:, h * HEAD_WIDTH:(h + 1) * HEAD_WIDTH]
-            s = []
-            for c in range(cols):
-                s_c = jnp.dot(qh, k_ref[c * LANES:(c + 1) * LANES, :], preferred_element_type=jnp.float32)
-                if masked:
-                    s_c = jnp.where(allowed[c], s_c, NEG)
-                s.append(s_c)
-            top = s[0]
-            for c in range(1, cols):
-                top = jnp.maximum(top, s[c])
-            m_prev = m_sc[h]
-            m_next = jnp.maximum(m_prev, jnp.max(top, axis=1, keepdims=True))
-            m_b = m_next[:, 0:1]
-            part = None
-            pv = None
-            for c in range(cols):
-                p = jnp.exp((s[c] - m_b) * scale)
-                if masked:
-                    p = jnp.where(allowed[c], p, 0.0)
-                part = p if part is None else part + p
-                term = jnp.dot(
-                    p.astype(jnp.bfloat16), v_ref[c * LANES:(c + 1) * LANES, :], preferred_element_type=jnp.float32
-                )
-                pv = term if pv is None else pv + term
-            alpha = jnp.exp((m_prev - m_next) * scale)
-            l_sc[h] = alpha * l_sc[h] + part
-            acc_sc[h] = alpha[:, 0:1] * acc_sc[h] + pv
-            m_sc[h] = m_next
+        part_rows = rows // HALVES
+        lane = lax.broadcasted_iota(jnp.int32, (part_rows, LANES), 1)
+        for half in range(HALVES):
+            r = slice(half * part_rows, (half + 1) * part_rows)
+            if masked:
+                q_start = qs_ref[...].reshape(rows, LANES)[r, 0:1]
+                q_pos = qp_ref[...].reshape(rows, LANES)[r, 0:1]
+                allowed = []
+                for c in range(cols):
+                    k_pos = shard * shard_rows + c * LANES + lane
+                    allowed.append((k_pos >= q_start) & (k_pos <= q_pos))
+            for h in range(heads):
+                qh = q_ref[r, h * HEAD_WIDTH:(h + 1) * HEAD_WIDTH]
+                s = []
+                for c in range(cols):
+                    s_c = jnp.dot(qh, k_ref[c * LANES:(c + 1) * LANES, :], preferred_element_type=jnp.float32)
+                    if masked:
+                        s_c = jnp.where(allowed[c], s_c, NEG)
+                    s.append(s_c)
+                top = s[0]
+                for c in range(1, cols):
+                    top = jnp.maximum(top, s[c])
+                m_prev = m_sc[h, r, :]
+                m_next = jnp.maximum(m_prev, jnp.max(top, axis=1, keepdims=True))
+                m_b = m_next[:, 0:1]
+                part = None
+                pv = None
+                for c in range(cols):
+                    p = jnp.exp((s[c] - m_b) * scale)
+                    if masked:
+                        p = jnp.where(allowed[c], p, 0.0)
+                    part = p if part is None else part + p
+                    term = jnp.dot(
+                        p.astype(jnp.bfloat16), v_ref[c * LANES:(c + 1) * LANES, :], preferred_element_type=jnp.float32
+                    )
+                    pv = term if pv is None else pv + term
+                alpha = jnp.exp((m_prev - m_next) * scale)
+                l_sc[h, r, :] = alpha * l_sc[h, r, :] + part
+                acc_sc[h, r, :] = alpha[:, 0:1] * acc_sc[h, r, :] + pv
+                m_sc[h, r, :] = m_next
 
     live = shard >= first
     full = (shard < me) & (shard * shard_rows >= q_last_start)

time: 195 us -> 193 us (0.990)
  waiting for transfers between devices: 133 us -> 126 us
  Pallas kernels: 15.8 us -> 20.5 us
    reduce_scatter x1, waiting for transfers between devices: 40.4 us -> 32.2 us  [per_device(): lax.psum_scatter(projected, 'head', scatter_dimension=0, tiled=True)]
    pallas_call x2, Pallas kernels: 15.8 us -> 20.5 us  [attention(): pl.pallas_call(kernel, out_shape=jax.ShapeDtypeStruct((rows, width), jnp....]
  transfers between devices with their start and end apart: 7 -> 7, of which waited for: 6 -> 6; matrix products, arithmetic and copies ran while one was open for 3% -> 3% of each run, Pallas kernels for 4% -> 5%
where the time goes in v7:
time: 193 us; the launch traced here: 191 us
  waiting for transfers between devices  126 us (65%)
  Pallas kernels  20.5 us (11%)
  between operations  13.6 us (7%)
  starting transfers between devices  11 us (6%)
  matrix products  7.73 us (4%)
  other arithmetic  7.65 us (4%)
  local copies, waits for them, and re-layouts  5.44 us (3%)
    all_gather x1, waiting for transfers between devices, per_device(): gathered = lax.all_gather(pair, 'xy')  69.3 us
    reduce_scatter x1, waiting for transfers between devices, per_device(): lax.psum_scatter(projected, 'head', scatter_dimension=0, tiled=True)  32.2 us
    pallas_call x2, Pallas kernels, attention(): pl.pallas_call(kernel, out_shape=jax.ShapeDtypeStruct((rows, width), jnp....  20.5 us
    ppermute x3, waiting for transfers between devices, chip_step(): lax.ppermute(send.astype(jnp.bfloat16), 'head', perm=[(i, i ^ 2 * k) for...  15.6 us
    dot_general x2, matrix products, per_device(): jnp.dot(attended, out_weight, preferred_element_type=jnp.float32)  7.73 us
    ppermute x1, starting transfers between devices, per_device(): partner = lax.ppermute(block, 'zh', perm=[(0, 1), (1, 0)])  7.28 us
    ppermute x1, waiting for transfers between devices, per_device(): partner = lax.ppermute(block, 'zh', perm=[(0, 1), (1, 0)])  6.02 us
  transfers between devices with their start and end apart: 7, of which 6 were waited for; matrix products, arithmetic and copies ran while one was open for 3% of the time, Pallas kernels for 5%

profile of v7, /device:TPU:2, one launch (start us, length us, event | category | flops | bytes accessed | tf_op | source)
XLA Modules:
  0.0 191.4 jit_solution(6864382865517539796)
XLA Ops:
  6.5 0.0 copy-start
  6.5 0.0 all-gather.3.cloned.1.call-start
  6.5 0.8 convert_convert_fusion
  7.3 1.0 copy.26
  8.3 0.9 fusion.7
  9.3 7.3 %collective-permute-start = (bf16[392,256]{1,0:T(8,128)(2,1)S(1)}, bf16[392,256]{1,0:T(8,128)(2,1)S(1)}, u32[]{:S(2)}, u32[]{:S(2)}) collective-permute-start(bf16[392,256]{1,0:T(8,128)(2,1)S(1)} %get-tuple-element.29), channel_id=1, source_target_pairs={{0,128},{128,0},{1,129},{129,1},{2,130},{130,2},{3,131},{131,3},{4... | collective-permute-start | bytes 602120 | tf_op jit(solution)/shard_map/ppermute | solution.py:175
  16.5 6.0 %collective-permute-done = bf16[392,256]{1,0:T(8,128)(2,1)S(1)} collective-permute-done((bf16[392,256]{1,0:T(8,128)(2,1)S(1)}, bf16[392,256]{1,0:T(8,128)(2,1)S(1)}, u32[]{:S(2)}, u32[]{:S(2)}) %collective-permute-start) | collective-permute-done | bytes 200736 | tf_op jit(solution)/shard_map/ppermute | solution.py:175
  22.6 0.8 pad_maximum_fusion
  23.3 0.0 all-gather.3.cloned.1.call-update
  23.4 0.0 reduce-scatter.2.cloned.1.call-start
  23.4 0.1 pad.9.clone
  23.5 1.8 fusion.8
  25.3 69.3 %all-gather.3.cloned.1.call-done = bf16[32,392,256]{2,1,0:T(8,128)(2,1)} async-done(((bf16[2,392,256]{2,1,0:T(8,128)(2,1)}), bf16[32,392,256]{2,1,0:T(8,128)(2,1)}) %all-gather.3.cloned.1.call-update) | async-done | bytes 6422544 | tf_op jit(solution)/shard_map/all_gather | solution.py:177
  94.6 0.9 slice_convert_fusion
  95.5 0.7 convert_reduce_fusion
  96.2 0.0 copy-done
  96.2 0.1 select_reduce_fusion
  96.3 0.1 convert_element_type.75
  96.4 0.1 and_reduce_fusion
  96.5 0.2 divide_reduce_fusion
  96.7 0.1 add_add_fusion.1
  96.8 0.1 copy.27
  96.9 0.6 reshape.129.sc_ref
  97.5 0.8 broadcast_in_dim.5.qp_ref
  98.3 0.8 broadcast_in_dim.4.qs_ref
  99.1 10.3 %shard_map.55 = bf16[192,512]{1,0:T(8,128)(2,1)} custom-call(s32[8]{0:T(128)} %reshape.129.sc_ref, bf16[192,512]{1,0:T(8,128)(2,1)} %bitcast.61, bf16[16,2,392,256]{3,2,1,0:T(8,128)(2,1)} %bitcast.53, bf16[16,2,392,256]{3,2,1,0:T(8,128)(2,1)} %bitcast.54, s32[8,2,24,128]{3,2,1,0:T(8,128)} %broadcast_in_dim.4.qs_ref, ...), custom_call_target="tpu_custom_call" | custom-call | flops 2717908992 | bytes 3932160 | tf_op jit(solution)/shard_map/pallas_call | solution.py:112
  109.4 4.4 %convolution_convert_fusion.1.after_ref = bf16[192,4096]{1,0:T(8,128)(2,1)} fusion(bf16[192,512]{1,0:T(8,128)(2,1)} %shard_map.55, bf16[512,4096]{1,0:T(8,128)(2,1)} %param.11), kind=kOutput, calls=%fused_computation.1 | convolution fusion | flops 806092800 | bytes 5963776 | tf_op jit(solution)/shard_map/dot_general | solution.py:209
  113.8 0.0 reduce-scatter.2.cloned.1.call-update
  113.9 10.3 %shard_map.56 = bf16[192,512]{1,0:T(8,128)(2,1)} custom-call(s32[8]{0:T(128)} %reshape.129.sc_ref, bf16[192,512]{1,0:T(8,128)(2,1)} %bitcast.60, bf16[16,2,392,256]{3,2,1,0:T(8,128)(2,1)} %bitcast.56, bf16[16,2,392,256]{3,2,1,0:T(8,128)(2,1)} %bitcast.57, s32[8,2,24,128]{3,2,1,0:T(8,128)} %broadcast_in_dim.4.qs_ref, ...), custom_call_target="tpu_custom_call" | custom-call | flops 2717908992 | bytes 3932160 | tf_op jit(solution)/shard_map/pallas_call | solution.py:112
  124.1 3.3 %convolution_convert_fusion = bf16[192,4096]{1,0:T(8,128)(2,1)S(1)} fusion(bf16[192,512]{1,0:T(8,128)(2,1)} %shard_map.56, bf16[512,4096]{1,0:T(8,128)(2,1)} %param.11), kind=kOutput, calls=%fused_computation | convolution fusion | flops 806092800 | bytes 5963776 | tf_op jit(solution)/shard_map/dot_general | solution.py:209
  127.4 0.1 dynamic-slice_bitcast_fusion
  127.5 0.1 collective-permute-start.1
  127.7 2.4 %collective-permute-done.1 = bf16[4,24,4096]{2,1,0:T(8,128)(2,1)} collective-permute-done((bf16[4,24,4096]{2,1,0:T(8,128)(2,1)S(1)}, bf16[4,24,4096]{2,1,0:T(8,128)(2,1)}, u32[]{:S(2)}, u32[]{:S(2)}) %collective-permute-start.1) | collective-permute-done | bytes 786464 | tf_op jit(solution)/shard_map/ppermute | solution.py:148
  130.0 1.3 convert_add_fusion
  131.3 32.2 %reduce-scatter.2.cloned.1.call-done = bf16[24,4096]{1,0:T(8,128)(2,1)} async-done(((bf16[192,4096]{1,0:T(8,128)(2,1)}), bf16[24,4096]{1,0:T(8,128)(2,1)}) %reduce-scatter.2.cloned.1.call-update) | async-done | bytes 196624 | tf_op jit(solution)/shard_map/reduce_scatter | solution.py:212
  163.5 0.1 fusion.3
  163.6 0.1 collective-permute-start.2
  163.7 0.1 collective-permute-start.4
  163.8 3.4 %collective-permute-start.3 = (bf16[24,4096]{1,0:T(8,128)(2,1)S(1)}, bf16[24,4096]{1,0:T(8,128)(2,1)S(1)}, u32[]{:S(2)}, u32[]{:S(2)}) collective-permute-start(bf16[24,4096]{1,0:T(8,128)(2,1)S(1)} %get-tuple-element.25), channel_id=1, source_target_pairs={{0,4},{1,5},{2,6},{3,7},{4,0},{5,1},{6,2},{7,3},{8,12},{9,13},{10,... | collective-permute-start | bytes 589832 | tf_op jit(solution)/shard_map/ppermute | solution.py:157
  167.2 7.2 %collective-permute-done.2 = bf16[24,4096]{1,0:T(8,128)(2,1)S(1)} collective-permute-done((bf16[24,4096]{1,0:T(8,128)(2,1)S(1)}, bf16[24,4096]{1,0:T(8,128)(2,1)S(1)}, u32[]{:S(2)}, u32[]{:S(2)}) %collective-permute-start.2) | collective-permute-done | bytes 196640 | tf_op jit(solution)/shard_map/ppermute | solution.py:157
  174.3 0.0 collective-permute-done.4
  174.3 8.5 %collective-permute-done.3 = bf16[24,4096]{1,0:T(8,128)(2,1)S(1)} collective-permute-done((bf16[24,4096]{1,0:T(8,128)(2,1)S(1)}, bf16[24,4096]{1,0:T(8,128)(2,1)S(1)}, u32[]{:S(2)}, u32[]{:S(2)}) %collective-permute-start.3) | collective-permute-done | bytes 196640 | tf_op jit(solution)/shard_map/ppermute | solution.py:157
  182.8 0.1 fusion.2
  182.9 1.7 pad_maximum_fusion.1
  (6 shorter events, 0.0 us)
Async XLA Ops:
  6.5 89.7 %copy-start = (s32[384]{0:T(512)S(1)}, s32[384]{0:T(512)}, u32[]{:S(2)}) copy-start(s32[384]{0:T(512)} %param.10) | copy-start | bytes 4612
  6.5 88.1 %all-gather.3.cloned.1.call-start = ((), (), s32[]{:S(2)}) async-start(), calls=%async_computation.2 | async-start | bytes 6823936 | tf_op jit(solution)/shard_map/all_gather | solution.py:177
  9.3 13.3 %collective-permute-start = (bf16[392,256]{1,0:T(8,128)(2,1)S(1)}, bf16[392,256]{1,0:T(8,128)(2,1)S(1)}, u32[]{:S(2)}, u32[]{:S(2)}) collective-permute-start(bf16[392,256]{1,0:T(8,128)(2,1)S(1)} %get-tuple-element.29), channel_id=1, source_target_pairs={{0,128},{128,0},{1,129},{129,1},{2,130},{130,2},{3,131},{131,3},{4... | collective-permute-start | bytes 602120 | tf_op jit(solution)/shard_map/ppermute | solution.py:175
  23.4 140.1 %reduce-scatter.2.cloned.1.call-start = ((), (), s32[]{:S(2)}) async-start(), calls=%async_computation.1 | async-start | bytes 1769472 | tf_op jit(solution)/shard_map/reduce_scatter | solution.py:212
  127.5 2.5 %collective-permute-start.1 = (bf16[4,24,4096]{2,1,0:T(8,128)(2,1)S(1)}, bf16[4,24,4096]{2,1,0:T(8,128)(2,1)}, u32[]{:S(2)}, u32[]{:S(2)}) collective-permute-start(bf16[4,24,4096]{2,1,0:T(8,128)(2,1)S(1)} %dynamic-slice_bitcast_fusion), channel_id=1, source_target_pairs={{0,1},{1,0},{2,3},{3,2},{4,5},{5,4},{6,7},{7,6},{8,9},{9,8},{10,11... | collective-permute-start | bytes 2359304 | tf_op jit(solution)/shard_map/ppermute | solution.py:148
  163.6 10.7 %collective-permute-start.2 = (bf16[24,4096]{1,0:T(8,128)(2,1)S(1)}, bf16[24,4096]{1,0:T(8,128)(2,1)S(1)}, u32[]{:S(2)}, u32[]{:S(2)}) collective-permute-start(bf16[24,4096]{1,0:T(8,128)(2,1)S(1)} %get-tuple-element.23), channel_id=1, source_target_pairs={{0,2},{1,3},{2,0},{3,1},{4,6},{5,7},{6,4},{7,5},{8,10},{9,11},{10,... | collective-permute-start | bytes 589832 | tf_op jit(solution)/shard_map/ppermute | solution.py:157
  163.7 10.7 %collective-permute-start.4 = (bf16[24,4096]{1,0:T(8,128)(2,1)S(1)}, bf16[24,4096]{1,0:T(8,128)(2,1)S(1)}, u32[]{:S(2)}, u32[]{:S(2)}) collective-permute-start(bf16[24,4096]{1,0:T(8,128)(2,1)S(1)} %get-tuple-element.24), channel_id=1, source_target_pairs={{0,6},{1,7},{2,4},{3,5},{4,2},{5,3},{6,0},{7,1},{8,14},{9,15},{10,... | collective-permute-start | bytes 589832 | tf_op jit(solution)/shard_map/ppermute | solution.py:157
  163.8 19.0 %collective-permute-start.3 = (bf16[24,4096]{1,0:T(8,128)(2,1)S(1)}, bf16[24,4096]{1,0:T(8,128)(2,1)S(1)}, u32[]{:S(2)}, u32[]{:S(2)}) collective-permute-start(bf16[24,4096]{1,0:T(8,128)(2,1)S(1)} %get-tuple-element.25), channel_id=1, source_target_pairs={{0,4},{1,5},{2,6},{3,7},{4,0},{5,1},{6,2},{7,3},{8,12},{9,13},{10,... | collective-permute-start | bytes 589832 | tf_op jit(solution)/shard_map/ppermute | solution.py:157
Sparse Core Ops, SparseCore 0:
  23.5 71.0 all-gather.2
  114.0 49.4 reduce-scatter.1

commit v8 on v4

--- a/solution.py
+++ b/solution.py
@@ -168,13 +168,15 @@
     ids = jnp.full((tile * lanes,), -1.0, jnp.float32).at[:rows].set(doc_ids.astype(jnp.float32))
     block = jnp.concatenate([kv, ids.reshape(tile, lanes).astype(kv.dtype)], axis=0)
 
-    partner = lax.ppermute(block, "zh", perm=[(0, 1), (1, 0)])
+    partner = lax.ppermute(block, "zh", perm=[(0, 1)])
     pair = jnp.stack([block, partner])
     gathered = lax.all_gather(pair, "xy")
 
     id_rows = gathered[:, :, rows:, :].astype(jnp.float32)
     docs = jnp.arange(DOCS, dtype=jnp.float32)
-    counts = jnp.sum((id_rows[..., None] == docs).astype(jnp.float32), axis=(0, 1, 2, 3))
+    slot_used = jnp.stack([jnp.float32(1.0), (zh == 1).astype(jnp.float32)])
+    hits = (id_rows[..., None] == docs).astype(jnp.float32) * slot_used[None, :, None, None, None]
+    counts = jnp.sum(hits, axis=(0, 1, 2, 3))
     below = (jnp.arange(DOCS, dtype=jnp.int32)[None, :] < doc_ids[:, None]).astype(jnp.float32)
     q_start = jnp.sum(below * counts[None, :], axis=1).astype(jnp.int32)
     q_pos = me * rows + jnp.arange(rows, dtype=jnp.int32)

time: 195 us -> 195 us (level)
  Pallas kernels: 15.8 us -> 13.5 us
    pallas_call x2, Pallas kernels: 15.8 us -> 13.5 us  [attention(): pl.pallas_call(kernel, out_shape=jax.ShapeDtypeStruct((rows, width), jnp....]
  transfers between devices with their start and end apart: 7 -> 7, of which waited for: 6 -> 6; matrix products, arithmetic and copies ran while one was open for 3% -> 3% of each run, Pallas kernels for 4% -> 3%
where the time goes in v8:
time: 195 us; the launch traced here: 196 us
  waiting for transfers between devices  134 us (69%)
  between operations  13.6 us (7%)
  Pallas kernels  13.5 us (7%)
  starting transfers between devices  12.8 us (7%)
  other arithmetic  8.51 us (4%)
  matrix products  7.73 us (4%)
  local copies, waits for them, and re-layouts  5.44 us (3%)
    all_gather x1, waiting for transfers between devices, per_device(): gathered = lax.all_gather(pair, 'xy')  71 us
    reduce_scatter x1, waiting for transfers between devices, per_device(): lax.psum_scatter(projected, 'head', scatter_dimension=0, tiled=True)  41.1 us
    ppermute x3, waiting for transfers between devices, chip_step(): lax.ppermute(send.astype(jnp.bfloat16), 'head', perm=[(i, i ^ 2 * k) for...  15.4 us
    pallas_call x2, Pallas kernels, attention(): pl.pallas_call(kernel, out_shape=jax.ShapeDtypeStruct((rows, width), jnp....  13.5 us
    ppermute x1, starting transfers between devices, per_device(): partner = lax.ppermute(block, 'zh', perm=[(0, 1)])  9.11 us
    dot_general x2, matrix products, per_device(): jnp.dot(attended, out_weight, preferred_element_type=jnp.float32)  7.73 us
    ppermute x1, waiting for transfers between devices, per_device(): partner = lax.ppermute(block, 'zh', perm=[(0, 1)])  4.22 us
  transfers between devices with their start and end apart: 7, of which 6 were waited for; matrix products, arithmetic and copies ran while one was open for 3% of the time, Pallas kernels for 3%

profile of v8, /device:TPU:2, one launch (start us, length us, event | category | flops | bytes accessed | tf_op | source)
XLA Modules:
  0.0 195.7 jit_solution(12673950919160930693)
XLA Ops:
  6.5 0.0 all-gather.3.cloned.1.call-start
  6.5 0.7 convert_convert_fusion
  7.2 1.0 copy.26
  8.3 0.9 fusion.7
  9.2 9.1 %collective-permute-start = (bf16[392,256]{1,0:T(8,128)(2,1)S(1)}, bf16[392,256]{1,0:T(8,128)(2,1)S(1)}, u32[]{:S(2)}, u32[]{:S(2)}) collective-permute-start(bf16[392,256]{1,0:T(8,128)(2,1)S(1)} %get-tuple-element.29), channel_id=1, source_target_pairs={{0,128},{1,129},{2,130},{3,131},{4,132},{5,133},{6,134},{7,135},{8... | collective-permute-start | bytes 602120 | tf_op jit(solution)/shard_map/ppermute | solution.py:171
  18.3 4.2 %collective-permute-done = bf16[392,256]{1,0:T(8,128)(2,1)S(1)} collective-permute-done((bf16[392,256]{1,0:T(8,128)(2,1)S(1)}, bf16[392,256]{1,0:T(8,128)(2,1)S(1)}, u32[]{:S(2)}, u32[]{:S(2)}) %collective-permute-start) | collective-permute-done | bytes 200736 | tf_op jit(solution)/shard_map/ppermute | solution.py:171
  22.5 0.8 pad_maximum_fusion
  23.3 0.0 all-gather.3.cloned.1.call-update
  23.3 0.0 reduce-scatter.2.cloned.1.call-start
  23.4 0.1 pad.9.clone
  23.5 0.1 add_convert_fusion
  23.6 1.8 fusion.8
  25.4 71.0 %all-gather.3.cloned.1.call-done = bf16[32,392,256]{2,1,0:T(8,128)(2,1)} async-done(((bf16[2,392,256]{2,1,0:T(8,128)(2,1)}), bf16[32,392,256]{2,1,0:T(8,128)(2,1)}) %all-gather.3.cloned.1.call-update) | async-done | bytes 6422544 | tf_op jit(solution)/shard_map/all_gather | solution.py:173
  96.3 0.9 slice_convert_fusion
  97.3 0.9 select_reduce_fusion
  98.1 0.8 select_reduce_fusion.1
  98.9 0.1 convert_element_type.73
  99.0 0.1 and_reduce_fusion
  99.1 0.2 divide_reduce_fusion
  99.3 0.1 add_add_fusion.1
  99.4 0.1 copy.27
  99.5 0.6 reshape.130.sc_ref
  100.1 0.8 broadcast_in_dim.5.qp_ref
  100.9 0.8 broadcast_in_dim.4.qs_ref
  101.7 6.7 %shard_map.55 = bf16[192,512]{1,0:T(8,128)(2,1)} custom-call(s32[8]{0:T(128)} %reshape.130.sc_ref, bf16[192,512]{1,0:T(8,128)(2,1)} %bitcast.62, bf16[16,2,392,256]{3,2,1,0:T(8,128)(2,1)} %bitcast.54, bf16[16,2,392,256]{3,2,1,0:T(8,128)(2,1)} %bitcast.55, s32[8,2,24,128]{3,2,1,0:T(8,128)} %broadcast_in_dim.4.qs_ref, ...), custom_call_target="tpu_custom_call" | custom-call | flops 2717908992 | bytes 3932160 | tf_op jit(solution)/shard_map/pallas_call | solution.py:108
  108.5 4.4 %convolution_convert_fusion.1.after_ref = bf16[192,4096]{1,0:T(8,128)(2,1)} fusion(bf16[192,512]{1,0:T(8,128)(2,1)} %shard_map.55, bf16[512,4096]{1,0:T(8,128)(2,1)} %param.11), kind=kOutput, calls=%fused_computation.1 | convolution fusion | flops 806092800 | bytes 5963776 | tf_op jit(solution)/shard_map/dot_general | solution.py:207
  112.9 0.0 reduce-scatter.2.cloned.1.call-update
  112.9 6.7 %shard_map.56 = bf16[192,512]{1,0:T(8,128)(2,1)} custom-call(s32[8]{0:T(128)} %reshape.130.sc_ref, bf16[192,512]{1,0:T(8,128)(2,1)} %bitcast.61, bf16[16,2,392,256]{3,2,1,0:T(8,128)(2,1)} %bitcast.57, bf16[16,2,392,256]{3,2,1,0:T(8,128)(2,1)} %bitcast.58, s32[8,2,24,128]{3,2,1,0:T(8,128)} %broadcast_in_dim.4.qs_ref, ...), custom_call_target="tpu_custom_call" | custom-call | flops 2717908992 | bytes 3932160 | tf_op jit(solution)/shard_map/pallas_call | solution.py:108
  119.7 3.3 %convolution_convert_fusion = bf16[192,4096]{1,0:T(8,128)(2,1)S(1)} fusion(bf16[192,512]{1,0:T(8,128)(2,1)} %shard_map.56, bf16[512,4096]{1,0:T(8,128)(2,1)} %param.11), kind=kOutput, calls=%fused_computation | convolution fusion | flops 806092800 | bytes 5963776 | tf_op jit(solution)/shard_map/dot_general | solution.py:207
  123.0 0.1 dynamic-slice_bitcast_fusion
  123.0 0.1 collective-permute-start.1
  123.2 2.4 %collective-permute-done.1 = bf16[4,24,4096]{2,1,0:T(8,128)(2,1)} collective-permute-done((bf16[4,24,4096]{2,1,0:T(8,128)(2,1)S(1)}, bf16[4,24,4096]{2,1,0:T(8,128)(2,1)}, u32[]{:S(2)}, u32[]{:S(2)}) %collective-permute-start.1) | collective-permute-done | bytes 786464 | tf_op jit(solution)/shard_map/ppermute | solution.py:144
  125.5 1.3 convert_add_fusion
  126.9 41.1 %reduce-scatter.2.cloned.1.call-done = bf16[24,4096]{1,0:T(8,128)(2,1)} async-done(((bf16[192,4096]{1,0:T(8,128)(2,1)}), bf16[24,4096]{1,0:T(8,128)(2,1)}) %reduce-scatter.2.cloned.1.call-update) | async-done | bytes 196624 | tf_op jit(solution)/shard_map/reduce_scatter | solution.py:210
  168.0 0.1 fusion.3
  168.1 0.1 collective-permute-start.2
  168.2 0.1 collective-permute-start.4
  168.3 3.4 %collective-permute-start.3 = (bf16[24,4096]{1,0:T(8,128)(2,1)S(1)}, bf16[24,4096]{1,0:T(8,128)(2,1)S(1)}, u32[]{:S(2)}, u32[]{:S(2)}) collective-permute-start(bf16[24,4096]{1,0:T(8,128)(2,1)S(1)} %get-tuple-element.25), channel_id=1, source_target_pairs={{0,4},{1,5},{2,6},{3,7},{4,0},{5,1},{6,2},{7,3},{8,12},{9,13},{10,... | collective-permute-start | bytes 589832 | tf_op jit(solution)/shard_map/ppermute | solution.py:153
  171.6 7.4 %collective-permute-done.2 = bf16[24,4096]{1,0:T(8,128)(2,1)S(1)} collective-permute-done((bf16[24,4096]{1,0:T(8,128)(2,1)S(1)}, bf16[24,4096]{1,0:T(8,128)(2,1)S(1)}, u32[]{:S(2)}, u32[]{:S(2)}) %collective-permute-start.2) | collective-permute-done | bytes 196640 | tf_op jit(solution)/shard_map/ppermute | solution.py:153
  179.1 0.0 collective-permute-done.4
  179.1 8.0 %collective-permute-done.3 = bf16[24,4096]{1,0:T(8,128)(2,1)S(1)} collective-permute-done((bf16[24,4096]{1,0:T(8,128)(2,1)S(1)}, bf16[24,4096]{1,0:T(8,128)(2,1)S(1)}, u32[]{:S(2)}, u32[]{:S(2)}) %collective-permute-start.3) | collective-permute-done | bytes 196640 | tf_op jit(solution)/shard_map/ppermute | solution.py:153
  187.0 0.1 fusion.2
  187.1 1.7 pad_maximum_fusion.1
  (6 shorter events, 0.0 us)
Async XLA Ops:
  6.5 89.8 %all-gather.3.cloned.1.call-start = ((), (), s32[]{:S(2)}) async-start(), calls=%async_computation.2 | async-start | bytes 6823936 | tf_op jit(solution)/shard_map/all_gather | solution.py:173
  9.2 13.3 %collective-permute-start = (bf16[392,256]{1,0:T(8,128)(2,1)S(1)}, bf16[392,256]{1,0:T(8,128)(2,1)S(1)}, u32[]{:S(2)}, u32[]{:S(2)}) collective-permute-start(bf16[392,256]{1,0:T(8,128)(2,1)S(1)} %get-tuple-element.29), channel_id=1, source_target_pairs={{0,128},{1,129},{2,130},{3,131},{4,132},{5,133},{6,134},{7,135},{8... | collective-permute-start | bytes 602120 | tf_op jit(solution)/shard_map/ppermute | solution.py:171
  23.3 144.7 %reduce-scatter.2.cloned.1.call-start = ((), (), s32[]{:S(2)}) async-start(), calls=%async_computation.1 | async-start | bytes 1769472 | tf_op jit(solution)/shard_map/reduce_scatter | solution.py:210
  123.0 2.5 %collective-permute-start.1 = (bf16[4,24,4096]{2,1,0:T(8,128)(2,1)S(1)}, bf16[4,24,4096]{2,1,0:T(8,128)(2,1)}, u32[]{:S(2)}, u32[]{:S(2)}) collective-permute-start(bf16[4,24,4096]{2,1,0:T(8,128)(2,1)S(1)} %dynamic-slice_bitcast_fusion), channel_id=1, source_target_pairs={{0,1},{1,0},{2,3},{3,2},{4,5},{5,4},{6,7},{7,6},{8,9},{9,8},{10,11... | collective-permute-start | bytes 2359304 | tf_op jit(solution)/shard_map/ppermute | solution.py:144
  168.1 11.0 %collective-permute-start.2 = (bf16[24,4096]{1,0:T(8,128)(2,1)S(1)}, bf16[24,4096]{1,0:T(8,128)(2,1)S(1)}, u32[]{:S(2)}, u32[]{:S(2)}) collective-permute-start(bf16[24,4096]{1,0:T(8,128)(2,1)S(1)} %get-tuple-element.23), channel_id=1, source_target_pairs={{0,2},{1,3},{2,0},{3,1},{4,6},{5,7},{6,4},{7,5},{8,10},{9,11},{10,... | collective-permute-start | bytes 589832 | tf_op jit(solution)/shard_map/ppermute | solution.py:153
  168.2 10.9 %collective-permute-start.4 = (bf16[24,4096]{1,0:T(8,128)(2,1)S(1)}, bf16[24,4096]{1,0:T(8,128)(2,1)S(1)}, u32[]{:S(2)}, u32[]{:S(2)}) collective-permute-start(bf16[24,4096]{1,0:T(8,128)(2,1)S(1)} %get-tuple-element.24), channel_id=1, source_target_pairs={{0,6},{1,7},{2,4},{3,5},{4,2},{5,3},{6,0},{7,1},{8,14},{9,15},{10,... | collective-permute-start | bytes 589832 | tf_op jit(solution)/shard_map/ppermute | solution.py:153
  168.3 18.8 %collective-permute-start.3 = (bf16[24,4096]{1,0:T(8,128)(2,1)S(1)}, bf16[24,4096]{1,0:T(8,128)(2,1)S(1)}, u32[]{:S(2)}, u32[]{:S(2)}) collective-permute-start(bf16[24,4096]{1,0:T(8,128)(2,1)S(1)} %get-tuple-element.25), channel_id=1, source_target_pairs={{0,4},{1,5},{2,6},{3,7},{4,0},{5,1},{6,2},{7,3},{8,12},{9,13},{10,... | collective-permute-start | bytes 589832 | tf_op jit(solution)/shard_map/ppermute | solution.py:153
Sparse Core Ops, SparseCore 0:
  23.4 72.8 all-gather.2
  113.0 54.9 reduce-scatter.1

commit v9 on v4

--- a/solution.py
+++ b/solution.py
@@ -147,12 +147,16 @@
 
 def chip_step(held, n_head):
     chip = lax.axis_index("head") // 2
-    total = lax.dynamic_index_in_dim(held, chip, axis=0, keepdims=False)
-    for k in range(1, n_head // 2):
-        send = lax.dynamic_index_in_dim(held, chip ^ k, axis=0, keepdims=False)
-        got = lax.ppermute(send.astype(jnp.bfloat16), "head", perm=[(i, i ^ (2 * k)) for i in range(n_head)])
-        total = total + got.astype(jnp.float32)
-    return total.astype(jnp.bfloat16)
+    bit = 1
+    while bit < n_head // 2:
+        mine = (chip // bit) % 2
+        held = held.reshape((-1, 2) + held.shape[1:])
+        keep = lax.dynamic_index_in_dim(held, mine, axis=1, keepdims=False)
+        send = lax.dynamic_index_in_dim(held, 1 - mine, axis=1, keepdims=False)
+        got = lax.ppermute(send.astype(jnp.bfloat16), "head", perm=[(i, i ^ (2 * bit)) for i in range(n_head)])
+        held = keep + got.astype(jnp.float32)
+        bit *= 2
+    return held[0].astype(jnp.bfloat16)
 
 
 def per_device(n_xy, n_head, queries, key_matrix, value_matrix, doc_ids, out_weight):

time: 195 us -> 195 us (level)
  waiting for transfers between devices: 133 us -> 139 us
  Pallas kernels: 15.8 us -> 13.5 us
  starting transfers between devices: 11 us -> 9.02 us
    reduce_scatter x1, waiting for transfers between devices: 40.4 us -> 43.3 us  [per_device(): lax.psum_scatter(projected, 'head', scatter_dimension=0, tiled=True)]
    ppermute x3 -> x2, waiting for transfers between devices: 15.4 us -> 17.6 us  [chip_step(): lax.ppermute(send.astype(jnp.bfloat16), 'head', perm=[(i, i ^ 2 * bit) fo...]
    pallas_call x2, Pallas kernels: 15.8 us -> 13.5 us  [attention(): pl.pallas_call(kernel, out_shape=jax.ShapeDtypeStruct((rows, width), jnp....]
    ppermute x3 -> x2, starting transfers between devices: 3.56 us -> 1.61 us  [chip_step(): lax.ppermute(send.astype(jnp.bfloat16), 'head', perm=[(i, i ^ 2 * bit) fo...]
  transfers between devices with their start and end apart: 7 -> 6, of which waited for: 6 -> 6; matrix products, arithmetic and copies ran while one was open for 3% -> 3% of each run, Pallas kernels for 4% -> 3%
where the time goes in v9:
time: 195 us
  waiting for transfers between devices  139 us (71%)
  between operations  13.6 us (7%)
  Pallas kernels  13.5 us (7%)
  starting transfers between devices  9.02 us (5%)
  matrix products  7.73 us (4%)
  other arithmetic  6.75 us (3%)
  local copies, waits for them, and re-layouts  5.45 us (3%)
    all_gather x1, waiting for transfers between devices, per_device(): gathered = lax.all_gather(pair, 'xy')  69.3 us
    reduce_scatter x1, waiting for transfers between devices, per_device(): lax.psum_scatter(projected, 'head', scatter_dimension=0, tiled=True)  43.3 us
    ppermute x2, waiting for transfers between devices, chip_step(): lax.ppermute(send.astype(jnp.bfloat16), 'head', perm=[(i, i ^ 2 * bit) fo...  17.6 us
    pallas_call x2, Pallas kernels, attention(): pl.pallas_call(kernel, out_shape=jax.ShapeDtypeStruct((rows, width), jnp....  13.5 us
    dot_general x2, matrix products, per_device(): jnp.dot(attended, out_weight, preferred_element_type=jnp.float32)  7.73 us
    ppermute x1, starting transfers between devices, per_device(): partner = lax.ppermute(block, 'zh', perm=[(0, 1), (1, 0)])  7.28 us
    ppermute x1, waiting for transfers between devices, per_device(): partner = lax.ppermute(block, 'zh', perm=[(0, 1), (1, 0)])  6.02 us
  transfers between devices with their start and end apart: 6, of which 6 were waited for; matrix products, arithmetic and copies ran while one was open for 3% of the time, Pallas kernels for 3%

profile of v9, /device:TPU:2, one launch (start us, length us, event | category | flops | bytes accessed | tf_op | source)
XLA Modules:
  0.0 194.7 jit_solution(14299878013964127812)
XLA Ops:
  6.5 0.0 copy-start.1
  6.5 0.0 all-gather.3.cloned.1.call-start
  6.5 0.8 convert_convert_fusion
  7.3 1.0 copy.29
  8.3 0.9 fusion.3
  9.3 7.3 %collective-permute-start = (bf16[392,256]{1,0:T(8,128)(2,1)S(1)}, bf16[392,256]{1,0:T(8,128)(2,1)S(1)}, u32[]{:S(2)}, u32[]{:S(2)}) collective-permute-start(bf16[392,256]{1,0:T(8,128)(2,1)S(1)} %get-tuple-element.26), channel_id=1, source_target_pairs={{0,128},{128,0},{1,129},{129,1},{2,130},{130,2},{3,131},{131,3},{4... | collective-permute-start | bytes 602120 | tf_op jit(solution)/shard_map/ppermute | solution.py:175
  16.5 6.0 %collective-permute-done = bf16[392,256]{1,0:T(8,128)(2,1)S(1)} collective-permute-done((bf16[392,256]{1,0:T(8,128)(2,1)S(1)}, bf16[392,256]{1,0:T(8,128)(2,1)S(1)}, u32[]{:S(2)}, u32[]{:S(2)}) %collective-permute-start) | collective-permute-done | bytes 200736 | tf_op jit(solution)/shard_map/ppermute | solution.py:175
  22.6 0.8 pad_maximum_fusion
  23.3 0.0 all-gather.3.cloned.1.call-update
  23.4 0.0 reduce-scatter.2.cloned.1.call-start
  23.4 0.1 pad.9.clone
  23.5 1.8 fusion.4
  25.3 69.3 %all-gather.3.cloned.1.call-done = bf16[32,392,256]{2,1,0:T(8,128)(2,1)} async-done(((bf16[2,392,256]{2,1,0:T(8,128)(2,1)}), bf16[32,392,256]{2,1,0:T(8,128)(2,1)}) %all-gather.3.cloned.1.call-update) | async-done | bytes 6422544 | tf_op jit(solution)/shard_map/all_gather | solution.py:177
  94.6 0.9 slice_convert_fusion
  95.5 0.7 convert_reduce_fusion
  96.2 0.0 copy-done.1
  96.2 0.1 select_reduce_fusion
  96.3 0.1 convert_element_type.68
  96.4 0.1 and_reduce_fusion
  96.5 0.2 divide_reduce_fusion
  96.7 0.1 add_add_fusion.1
  96.8 0.1 copy.30
  96.9 0.6 reshape.138.sc_ref
  97.5 0.8 broadcast_in_dim.5.qp_ref
  98.3 0.8 broadcast_in_dim.4.qs_ref
  99.1 6.7 %shard_map.55 = bf16[192,512]{1,0:T(8,128)(2,1)} custom-call(s32[8]{0:T(128)} %reshape.138.sc_ref, bf16[192,512]{1,0:T(8,128)(2,1)} %bitcast.60, bf16[16,2,392,256]{3,2,1,0:T(8,128)(2,1)} %bitcast.50, bf16[16,2,392,256]{3,2,1,0:T(8,128)(2,1)} %bitcast.51, s32[8,2,24,128]{3,2,1,0:T(8,128)} %broadcast_in_dim.4.qs_ref, ...), custom_call_target="tpu_custom_call" | custom-call | flops 2717908992 | bytes 3932160 | tf_op jit(solution)/shard_map/pallas_call | solution.py:108
  105.9 4.4 %convolution_convert_fusion.1.after_ref = bf16[192,4096]{1,0:T(8,128)(2,1)} fusion(bf16[192,512]{1,0:T(8,128)(2,1)} %shard_map.55, bf16[512,4096]{1,0:T(8,128)(2,1)} %param.11), kind=kOutput, calls=%fused_computation.1 | convolution fusion | flops 806092800 | bytes 5963776 | tf_op jit(solution)/shard_map/dot_general | solution.py:209
  110.3 0.0 reduce-scatter.2.cloned.1.call-update
  110.3 6.7 %shard_map.56 = bf16[192,512]{1,0:T(8,128)(2,1)} custom-call(s32[8]{0:T(128)} %reshape.138.sc_ref, bf16[192,512]{1,0:T(8,128)(2,1)} %bitcast.59, bf16[16,2,392,256]{3,2,1,0:T(8,128)(2,1)} %bitcast.53, bf16[16,2,392,256]{3,2,1,0:T(8,128)(2,1)} %bitcast.54, s32[8,2,24,128]{3,2,1,0:T(8,128)} %broadcast_in_dim.4.qs_ref, ...), custom_call_target="tpu_custom_call" | custom-call | flops 2717908992 | bytes 3932160 | tf_op jit(solution)/shard_map/pallas_call | solution.py:108
  117.1 3.3 %convolution_convert_fusion = bf16[192,4096]{1,0:T(8,128)(2,1)S(1)} fusion(bf16[192,512]{1,0:T(8,128)(2,1)} %shard_map.56, bf16[512,4096]{1,0:T(8,128)(2,1)} %param.11), kind=kOutput, calls=%fused_computation | convolution fusion | flops 806092800 | bytes 5963776 | tf_op jit(solution)/shard_map/dot_general | solution.py:209
  120.4 0.1 dynamic-slice_bitcast_fusion
  120.5 0.1 collective-permute-start.1
  120.6 2.4 %collective-permute-done.1 = bf16[4,24,4096]{2,1,0:T(8,128)(2,1)} collective-permute-done((bf16[4,24,4096]{2,1,0:T(8,128)(2,1)S(1)}, bf16[4,24,4096]{2,1,0:T(8,128)(2,1)}, u32[]{:S(2)}, u32[]{:S(2)}) %collective-permute-start.1) | collective-permute-done | bytes 786464 | tf_op jit(solution)/shard_map/ppermute | solution.py:144
  123.0 1.3 convert_add_fusion
  124.3 43.3 %reduce-scatter.2.cloned.1.call-done = bf16[24,4096]{1,0:T(8,128)(2,1)} async-done(((bf16[192,4096]{1,0:T(8,128)(2,1)}), bf16[24,4096]{1,0:T(8,128)(2,1)}) %reduce-scatter.2.cloned.1.call-update) | async-done | bytes 196624 | tf_op jit(solution)/shard_map/reduce_scatter | solution.py:212
  167.6 0.0 copy-start
  167.6 0.1 collective-permute-start.2
  167.8 7.7 %collective-permute-done.2 = bf16[2,24,4096]{2,1,0:T(8,128)(2,1)S(1)} collective-permute-done((bf16[2,24,4096]{2,1,0:T(8,128)(2,1)S(1)}, bf16[2,24,4096]{2,1,0:T(8,128)(2,1)S(1)}, u32[]{:S(2)}, u32[]{:S(2)}) %collective-permute-start.2) | collective-permute-done | bytes 393248 | tf_op jit(solution)/shard_map/ppermute | solution.py:156
  175.5 0.1 bitcast_add_fusion
  175.6 1.5 collective-permute-start.3
  177.1 9.9 %collective-permute-done.3 = bf16[1,24,4096]{2,1,0:T(8,128)(2,1)S(1)} collective-permute-done((bf16[1,24,4096]{2,1,0:T(8,128)(2,1)S(1)}, bf16[1,24,4096]{2,1,0:T(8,128)(2,1)S(1)}, u32[]{:S(2)}, u32[]{:S(2)}) %collective-permute-start.3) | collective-permute-done | bytes 196640 | tf_op jit(solution)/shard_map/ppermute | solution.py:156
  187.1 0.0 copy-done
  187.1 0.8 pad_maximum_fusion.1
  (9 shorter events, 0.2 us)
Async XLA Ops:
  6.5 89.7 %copy-start.1 = (s32[384]{0:T(512)S(1)}, s32[384]{0:T(512)}, u32[]{:S(2)}) copy-start(s32[384]{0:T(512)} %param.10) | copy-start | bytes 4612
  6.5 88.1 %all-gather.3.cloned.1.call-start = ((), (), s32[]{:S(2)}) async-start(), calls=%async_computation.2 | async-start | bytes 6823936 | tf_op jit(solution)/shard_map/all_gather | solution.py:177
  9.3 13.3 %collective-permute-start = (bf16[392,256]{1,0:T(8,128)(2,1)S(1)}, bf16[392,256]{1,0:T(8,128)(2,1)S(1)}, u32[]{:S(2)}, u32[]{:S(2)}) collective-permute-start(bf16[392,256]{1,0:T(8,128)(2,1)S(1)} %get-tuple-element.26), channel_id=1, source_target_pairs={{0,128},{128,0},{1,129},{129,1},{2,130},{130,2},{3,131},{131,3},{4... | collective-permute-start | bytes 602120 | tf_op jit(solution)/shard_map/ppermute | solution.py:175
  23.4 144.2 %reduce-scatter.2.cloned.1.call-start = ((), (), s32[]{:S(2)}) async-start(), calls=%async_computation.1 | async-start | bytes 1769472 | tf_op jit(solution)/shard_map/reduce_scatter | solution.py:212
  120.5 2.5 %collective-permute-start.1 = (bf16[4,24,4096]{2,1,0:T(8,128)(2,1)S(1)}, bf16[4,24,4096]{2,1,0:T(8,128)(2,1)}, u32[]{:S(2)}, u32[]{:S(2)}) collective-permute-start(bf16[4,24,4096]{2,1,0:T(8,128)(2,1)S(1)} %dynamic-slice_bitcast_fusion), channel_id=1, source_target_pairs={{0,1},{1,0},{2,3},{3,2},{4,5},{5,4},{6,7},{7,6},{8,9},{9,8},{10,11... | collective-permute-start | bytes 2359304 | tf_op jit(solution)/shard_map/ppermute | solution.py:144
  167.6 19.5 %copy-start = (bf16[24,4096]{1,0:T(8,128)(2,1)S(1)}, bf16[24,4096]{1,0:T(8,128)(2,1)}, u32[]{:S(2)}) copy-start(bf16[24,4096]{1,0:T(8,128)(2,1)} %reduce-scatter.2.cloned.1.call-done) | copy-start | bytes 589828
  167.6 7.9 %collective-permute-start.2 = (bf16[2,24,4096]{2,1,0:T(8,128)(2,1)S(1)}, bf16[2,24,4096]{2,1,0:T(8,128)(2,1)S(1)}, u32[]{:S(2)}, u32[]{:S(2)}) collective-permute-start(bf16[2,24,4096]{2,1,0:T(8,128)(2,1)S(1)} %fusion), channel_id=1, source_target_pairs={{0,2},{1,3},{2,0},{3,1},{4,6},{5,7},{6,4},{7,5},{8,10},{9,11},{10,... | collective-permute-start | bytes 1179656 | tf_op jit(solution)/shard_map/ppermute | solution.py:156
  175.6 11.4 %collective-permute-start.3 = (bf16[1,24,4096]{2,1,0:T(8,128)(2,1)S(1)}, bf16[1,24,4096]{2,1,0:T(8,128)(2,1)S(1)}, u32[]{:S(2)}, u32[]{:S(2)}) collective-permute-start(bf16[1,24,4096]{2,1,0:T(8,128)(2,1)S(1)} %dynamic-slice_convert_fusion), channel_id=1, source_target_pairs={{0,4},{1,5},{2,6},{3,7},{4,0},{5,1},{6,2},{7,3},{8,12},{9,13},{10,... | collective-permute-start | bytes 589832 | tf_op jit(solution)/shard_map/ppermute | solution.py:156
Sparse Core Ops, SparseCore 0:
  23.5 71.0 all-gather.2
  110.4 57.0 reduce-scatter.1

commit v10 on v4

--- a/solution.py
+++ b/solution.py
@@ -17,7 +17,7 @@
 
 
 def attn_kernel(
-    steps, shard_rows, heads, scale, at, sc_ref, q_ref, k_ref, v_ref, qs_ref, qp_ref, after_ref, o_ref, m_sc, l_sc, acc_sc
+    steps, shard_rows, heads, scale, at, chunk, sc_ref, q_ref, k_ref, v_ref, qs_ref, after_ref, o_ref, m_sc, l_sc, acc_sc
 ):
     j = pl.program_id(0)
     me = sc_ref[at]
@@ -37,7 +37,12 @@
         if masked:
             lane = lax.broadcasted_iota(jnp.int32, (rows, LANES), 1)
             q_start = qs_ref[...].reshape(rows, LANES)[:, 0:1]
-            q_pos = qp_ref[...].reshape(rows, LANES)[:, 0:1]
+            groups, piece, _ = qs_ref.shape
+            shape = (groups, piece, LANES)
+            group = lax.broadcasted_iota(jnp.int32, shape, 0)
+            in_piece = lax.broadcasted_iota(jnp.int32, shape, 1)
+            q_pos = me * shard_rows + group * (shard_rows // groups) + chunk * piece + in_piece
+            q_pos = q_pos.reshape(rows, LANES)[:, 0:1]
             allowed = []
             for c in range(cols):
                 k_pos = shard * shard_rows + c * LANES + lane
@@ -90,7 +95,7 @@
             o_ref[:, h * HEAD_WIDTH:(h + 1) * HEAD_WIDTH] = (acc_sc[h] / denominator).astype(o_ref.dtype)
 
 
-def attention(scalars, chunk, queries, kv, q_start, q_pos, after, n_xy, shard_rows):
+def attention(scalars, chunk, queries, kv, q_start, after, n_xy, shard_rows):
     rows, width = queries.shape
     heads = width // HEAD_WIDTH
     steps = -(-(MOST - 1) // shard_rows) + 1
@@ -104,7 +109,7 @@
         return (s % n_xy, slot, 0, half)
 
     groups, _, piece, _ = q_start.shape
-    kernel = functools.partial(attn_kernel, steps, shard_rows, heads, scale, at)
+    kernel = functools.partial(attn_kernel, steps, shard_rows, heads, scale, at, chunk)
     return pl.pallas_call(
         kernel,
         out_shape=jax.ShapeDtypeStruct((rows, width), jnp.bfloat16),
@@ -115,7 +120,6 @@
                 pl.BlockSpec((rows, width), lambda j, sc: (0, 0)),
                 pl.BlockSpec((None, None, shard_rows, HEAD_WIDTH), lambda j, sc: index(j, sc, 0)),
                 pl.BlockSpec((None, None, shard_rows, HEAD_WIDTH), lambda j, sc: index(j, sc, 1)),
-                pl.BlockSpec((groups, None, piece, LANES), lambda j, sc: (0, chunk, 0, 0)),
                 pl.BlockSpec((groups, None, piece, LANES), lambda j, sc: (0, chunk, 0, 0)),
                 pl.BlockSpec(memory_space=pl.ANY),
             ],
@@ -132,7 +136,7 @@
             transcendentals=steps * heads * rows * shard_rows,
             bytes_accessed=steps * shard_rows * 2 * HEAD_WIDTH * 2 + 2 * rows * width * 2,
         ),
-    )(scalars, queries, kv, kv, q_start, q_pos, after)
+    )(scalars, queries, kv, kv, q_start, after)
 
 
 def core_step(projected, n_head, piece):
@@ -190,7 +194,6 @@
         return jnp.broadcast_to(x[:, None], (rows, LANES)).reshape(n_head, CHUNKS, piece, LANES)
 
     q_start_b = rows_view(q_start)
-    q_pos_b = rows_view(q_pos)
     q_start_c = q_start.reshape(n_head, CHUNKS, piece)
     firsts = jnp.maximum(q_start_c[0, :, 0] // rows, 0)
     lasts = q_start_c[n_head - 1, :, piece - 1]
@@ -201,7 +204,7 @@
     outs = []
     after = gathered
     for c in range(CHUNKS):
-        attended = attention(scalars, c, chunk_of(queries, c), gathered, q_start_b, q_pos_b, after, n_xy, rows)
+        attended = attention(scalars, c, chunk_of(queries, c), gathered, q_start_b, after, n_xy, rows)
         projected = jnp.dot(attended, out_weight, preferred_element_type=jnp.float32).astype(jnp.bfloat16)
         after = projected
         if c < CHUNKS - 1:

time: 195 us -> 193 us (0.990)
  Pallas kernels: 15.8 us -> 13.1 us
    pallas_call x2, Pallas kernels: 15.8 us -> 13.1 us  [attention(): pl.pallas_call(kernel, out_shape=jax.ShapeDtypeStruct((rows, width), jnp....]
  transfers between devices with their start and end apart: 7 -> 7, of which waited for: 6 -> 6; matrix products, arithmetic and copies ran while one was open for 3% -> 3% of each run, Pallas kernels for 4% -> 3%
where the time goes in v10:
time: 193 us; the launch traced here: 192 us
  waiting for transfers between devices  134 us (69%)
  between operations  13.6 us (7%)
  Pallas kernels  13.1 us (7%)
  starting transfers between devices  11 us (6%)
  matrix products  7.73 us (4%)
  other arithmetic  7.64 us (4%)
  local copies, waits for them, and re-layouts  4.61 us (2%)
    all_gather x1, waiting for transfers between devices, per_device(): gathered = lax.all_gather(pair, 'xy')  69.3 us
    reduce_scatter x1, waiting for transfers between devices, per_device(): lax.psum_scatter(projected, 'head', scatter_dimension=0, tiled=True)  41.3 us
    ppermute x3, waiting for transfers between devices, chip_step(): lax.ppermute(send.astype(jnp.bfloat16), 'head', perm=[(i, i ^ 2 * k) for...  15.4 us
    pallas_call x2, Pallas kernels, attention(): pl.pallas_call(kernel, out_shape=jax.ShapeDtypeStruct((rows, width), jnp....  13.1 us
    dot_general x2, matrix products, per_device(): jnp.dot(attended, out_weight, preferred_element_type=jnp.float32)  7.73 us
    ppermute x1, starting transfers between devices, per_device(): partner = lax.ppermute(block, 'zh', perm=[(0, 1), (1, 0)])  7.28 us
    ppermute x1, waiting for transfers between devices, per_device(): partner = lax.ppermute(block, 'zh', perm=[(0, 1), (1, 0)])  6.02 us
  transfers between devices with their start and end apart: 7, of which 6 were waited for; matrix products, arithmetic and copies ran while one was open for 3% of the time, Pallas kernels for 3%

profile of v10, /device:TPU:2, one launch (start us, length us, event | category | flops | bytes accessed | tf_op | source)
XLA Modules:
  0.0 192.1 jit_solution(6229421459054442647)
XLA Ops:
  6.5 0.0 copy-start
  6.5 0.0 all-gather.3.cloned.1.call-start
  6.5 0.8 convert_convert_fusion
  7.3 1.0 copy.26
  8.3 0.9 fusion.7
  9.3 7.3 %collective-permute-start = (bf16[392,256]{1,0:T(8,128)(2,1)S(1)}, bf16[392,256]{1,0:T(8,128)(2,1)S(1)}, u32[]{:S(2)}, u32[]{:S(2)}) collective-permute-start(bf16[392,256]{1,0:T(8,128)(2,1)S(1)} %get-tuple-element.29), channel_id=1, source_target_pairs={{0,128},{128,0},{1,129},{129,1},{2,130},{130,2},{3,131},{131,3},{4... | collective-permute-start | bytes 602120 | tf_op jit(solution)/shard_map/ppermute | solution.py:175
  16.5 6.0 %collective-permute-done = bf16[392,256]{1,0:T(8,128)(2,1)S(1)} collective-permute-done((bf16[392,256]{1,0:T(8,128)(2,1)S(1)}, bf16[392,256]{1,0:T(8,128)(2,1)S(1)}, u32[]{:S(2)}, u32[]{:S(2)}) %collective-permute-start) | collective-permute-done | bytes 200736 | tf_op jit(solution)/shard_map/ppermute | solution.py:175
  22.6 0.8 pad_maximum_fusion
  23.3 0.0 all-gather.3.cloned.1.call-update
  23.4 0.0 reduce-scatter.2.cloned.1.call-start
  23.4 0.1 pad.9.clone
  23.5 1.8 fusion.8
  25.3 69.3 %all-gather.3.cloned.1.call-done = bf16[32,392,256]{2,1,0:T(8,128)(2,1)} async-done(((bf16[2,392,256]{2,1,0:T(8,128)(2,1)}), bf16[32,392,256]{2,1,0:T(8,128)(2,1)}) %all-gather.3.cloned.1.call-update) | async-done | bytes 6422544 | tf_op jit(solution)/shard_map/all_gather | solution.py:177
  94.6 0.9 slice_convert_fusion
  95.5 0.7 convert_reduce_fusion
  96.2 0.0 copy-done
  96.2 0.1 select_reduce_fusion
  96.3 0.1 convert_element_type.75
  96.4 0.1 and_reduce_fusion
  96.5 0.2 divide_reduce_fusion
  96.7 0.1 add_add_fusion
  96.8 0.1 copy.27
  96.9 0.6 reshape.119.sc_ref
  97.5 0.8 broadcast_in_dim.2.qs_ref
  98.3 6.5 %shard_map.55 = bf16[192,512]{1,0:T(8,128)(2,1)} custom-call(s32[8]{0:T(128)} %reshape.119.sc_ref, bf16[192,512]{1,0:T(8,128)(2,1)} %bitcast.61, bf16[16,2,392,256]{3,2,1,0:T(8,128)(2,1)} %bitcast.53, bf16[16,2,392,256]{3,2,1,0:T(8,128)(2,1)} %bitcast.54, s32[8,2,24,128]{3,2,1,0:T(8,128)} %broadcast_in_dim.2.qs_ref, bf16[16,2,392,256]{3,2,1,0:T(8,128)(2,1)} %bitcast.55), custom_call_target="tpu_custom_call" | custom-call | flops 2717908992 | bytes 3932160 | tf_op jit(solution)/shard_map/pallas_call | solution.py:113
  104.8 4.4 %convolution_convert_fusion.1.after_ref = bf16[192,4096]{1,0:T(8,128)(2,1)} fusion(bf16[192,512]{1,0:T(8,128)(2,1)} %shard_map.55, bf16[512,4096]{1,0:T(8,128)(2,1)} %param.11), kind=kOutput, calls=%fused_computation.1 | convolution fusion | flops 806092800 | bytes 5963776 | tf_op jit(solution)/shard_map/dot_general | solution.py:208
  109.3 0.0 reduce-scatter.2.cloned.1.call-update
  109.3 6.5 %shard_map.56 = bf16[192,512]{1,0:T(8,128)(2,1)} custom-call(s32[8]{0:T(128)} %reshape.119.sc_ref, bf16[192,512]{1,0:T(8,128)(2,1)} %bitcast.60, bf16[16,2,392,256]{3,2,1,0:T(8,128)(2,1)} %bitcast.56, bf16[16,2,392,256]{3,2,1,0:T(8,128)(2,1)} %bitcast.57, s32[8,2,24,128]{3,2,1,0:T(8,128)} %broadcast_in_dim.2.qs_ref, ...), custom_call_target="tpu_custom_call" | custom-call | flops 2717908992 | bytes 3932160 | tf_op jit(solution)/shard_map/pallas_call | solution.py:113
  115.9 3.3 %convolution_convert_fusion = bf16[192,4096]{1,0:T(8,128)(2,1)S(1)} fusion(bf16[192,512]{1,0:T(8,128)(2,1)} %shard_map.56, bf16[512,4096]{1,0:T(8,128)(2,1)} %param.11), kind=kOutput, calls=%fused_computation | convolution fusion | flops 806092800 | bytes 5963776 | tf_op jit(solution)/shard_map/dot_general | solution.py:208
  119.2 0.1 dynamic-slice_bitcast_fusion
  119.2 0.1 collective-permute-start.1
  119.4 2.4 %collective-permute-done.1 = bf16[4,24,4096]{2,1,0:T(8,128)(2,1)} collective-permute-done((bf16[4,24,4096]{2,1,0:T(8,128)(2,1)S(1)}, bf16[4,24,4096]{2,1,0:T(8,128)(2,1)}, u32[]{:S(2)}, u32[]{:S(2)}) %collective-permute-start.1) | collective-permute-done | bytes 786464 | tf_op jit(solution)/shard_map/ppermute | solution.py:148
  121.8 1.3 convert_add_fusion
  123.1 41.3 %reduce-scatter.2.cloned.1.call-done = bf16[24,4096]{1,0:T(8,128)(2,1)} async-done(((bf16[192,4096]{1,0:T(8,128)(2,1)}), bf16[24,4096]{1,0:T(8,128)(2,1)}) %reduce-scatter.2.cloned.1.call-update) | async-done | bytes 196624 | tf_op jit(solution)/shard_map/reduce_scatter | solution.py:211
  164.4 0.1 fusion.3
  164.5 0.1 collective-permute-start.2
  164.6 0.1 collective-permute-start.4
  164.7 3.4 %collective-permute-start.3 = (bf16[24,4096]{1,0:T(8,128)(2,1)S(1)}, bf16[24,4096]{1,0:T(8,128)(2,1)S(1)}, u32[]{:S(2)}, u32[]{:S(2)}) collective-permute-start(bf16[24,4096]{1,0:T(8,128)(2,1)S(1)} %get-tuple-element.25), channel_id=1, source_target_pairs={{0,4},{1,5},{2,6},{3,7},{4,0},{5,1},{6,2},{7,3},{8,12},{9,13},{10,... | collective-permute-start | bytes 589832 | tf_op jit(solution)/shard_map/ppermute | solution.py:157
  168.0 7.4 %collective-permute-done.2 = bf16[24,4096]{1,0:T(8,128)(2,1)S(1)} collective-permute-done((bf16[24,4096]{1,0:T(8,128)(2,1)S(1)}, bf16[24,4096]{1,0:T(8,128)(2,1)S(1)}, u32[]{:S(2)}, u32[]{:S(2)}) %collective-permute-start.2) | collective-permute-done | bytes 196640 | tf_op jit(solution)/shard_map/ppermute | solution.py:157
  175.5 0.0 collective-permute-done.4
  175.5 7.9 %collective-permute-done.3 = bf16[24,4096]{1,0:T(8,128)(2,1)S(1)} collective-permute-done((bf16[24,4096]{1,0:T(8,128)(2,1)S(1)}, bf16[24,4096]{1,0:T(8,128)(2,1)S(1)}, u32[]{:S(2)}, u32[]{:S(2)}) %collective-permute-start.3) | collective-permute-done | bytes 196640 | tf_op jit(solution)/shard_map/ppermute | solution.py:157
  183.4 0.1 fusion.2
  183.5 1.7 pad_maximum_fusion.1
  (5 shorter events, 0.0 us)
Async XLA Ops:
  6.5 89.7 %copy-start = (s32[384]{0:T(512)S(1)}, s32[384]{0:T(512)}, u32[]{:S(2)}) copy-start(s32[384]{0:T(512)} %param.10) | copy-start | bytes 4612
  6.5 88.1 %all-gather.3.cloned.1.call-start = ((), (), s32[]{:S(2)}) async-start(), calls=%async_computation.2 | async-start | bytes 6823936 | tf_op jit(solution)/shard_map/all_gather | solution.py:177
  9.3 13.3 %collective-permute-start = (bf16[392,256]{1,0:T(8,128)(2,1)S(1)}, bf16[392,256]{1,0:T(8,128)(2,1)S(1)}, u32[]{:S(2)}, u32[]{:S(2)}) collective-permute-start(bf16[392,256]{1,0:T(8,128)(2,1)S(1)} %get-tuple-element.29), channel_id=1, source_target_pairs={{0,128},{128,0},{1,129},{129,1},{2,130},{130,2},{3,131},{131,3},{4... | collective-permute-start | bytes 602120 | tf_op jit(solution)/shard_map/ppermute | solution.py:175
  23.4 141.0 %reduce-scatter.2.cloned.1.call-start = ((), (), s32[]{:S(2)}) async-start(), calls=%async_computation.1 | async-start | bytes 1769472 | tf_op jit(solution)/shard_map/reduce_scatter | solution.py:211
  119.2 2.5 %collective-permute-start.1 = (bf16[4,24,4096]{2,1,0:T(8,128)(2,1)S(1)}, bf16[4,24,4096]{2,1,0:T(8,128)(2,1)}, u32[]{:S(2)}, u32[]{:S(2)}) collective-permute-start(bf16[4,24,4096]{2,1,0:T(8,128)(2,1)S(1)} %dynamic-slice_bitcast_fusion), channel_id=1, source_target_pairs={{0,1},{1,0},{2,3},{3,2},{4,5},{5,4},{6,7},{7,6},{8,9},{9,8},{10,11... | collective-permute-start | bytes 2359304 | tf_op jit(solution)/shard_map/ppermute | solution.py:148
  164.5 11.0 %collective-permute-start.2 = (bf16[24,4096]{1,0:T(8,128)(2,1)S(1)}, bf16[24,4096]{1,0:T(8,128)(2,1)S(1)}, u32[]{:S(2)}, u32[]{:S(2)}) collective-permute-start(bf16[24,4096]{1,0:T(8,128)(2,1)S(1)} %get-tuple-element.23), channel_id=1, source_target_pairs={{0,2},{1,3},{2,0},{3,1},{4,6},{5,7},{6,4},{7,5},{8,10},{9,11},{10,... | collective-permute-start | bytes 589832 | tf_op jit(solution)/shard_map/ppermute | solution.py:157
  164.6 10.9 %collective-permute-start.4 = (bf16[24,4096]{1,0:T(8,128)(2,1)S(1)}, bf16[24,4096]{1,0:T(8,128)(2,1)S(1)}, u32[]{:S(2)}, u32[]{:S(2)}) collective-permute-start(bf16[24,4096]{1,0:T(8,128)(2,1)S(1)} %get-tuple-element.24), channel_id=1, source_target_pairs={{0,6},{1,7},{2,4},{3,5},{4,2},{5,3},{6,0},{7,1},{8,14},{9,15},{10,... | collective-permute-start | bytes 589832 | tf_op jit(solution)/shard_map/ppermute | solution.py:157
  164.7 18.8 %collective-permute-start.3 = (bf16[24,4096]{1,0:T(8,128)(2,1)S(1)}, bf16[24,4096]{1,0:T(8,128)(2,1)S(1)}, u32[]{:S(2)}, u32[]{:S(2)}) collective-permute-start(bf16[24,4096]{1,0:T(8,128)(2,1)S(1)} %get-tuple-element.25), channel_id=1, source_target_pairs={{0,4},{1,5},{2,6},{3,7},{4,0},{5,1},{6,2},{7,3},{8,12},{9,13},{10,... | collective-permute-start | bytes 589832 | tf_op jit(solution)/shard_map/ppermute | solution.py:157
Sparse Core Ops, SparseCore 0:
  23.5 71.0 all-gather.2
  109.4 54.9 reduce-scatter.1

commit v11 on v4

--- a/solution.py
+++ b/solution.py
@@ -142,15 +142,16 @@
     keep = lax.dynamic_index_in_dim(held, core, axis=1, keepdims=False)
     send = lax.dynamic_index_in_dim(held, 1 - core, axis=1, keepdims=False)
     got = lax.ppermute(send, "head", perm=[(i, i ^ 1) for i in range(n_head)])
-    return keep.astype(jnp.float32) + got.astype(jnp.float32)
-
-
-def chip_step(held, n_head):
+    summed = keep.astype(jnp.float32) + got.astype(jnp.float32)
+    return summed, summed.astype(jnp.bfloat16)
+
+
+def chip_step(held, sent, n_head):
     chip = lax.axis_index("head") // 2
     total = lax.dynamic_index_in_dim(held, chip, axis=0, keepdims=False)
     for k in range(1, n_head // 2):
-        send = lax.dynamic_index_in_dim(held, chip ^ k, axis=0, keepdims=False)
-        got = lax.ppermute(send.astype(jnp.bfloat16), "head", perm=[(i, i ^ (2 * k)) for i in range(n_head)])
+        send = lax.dynamic_index_in_dim(sent, chip ^ k, axis=0, keepdims=False)
+        got = lax.ppermute(send, "head", perm=[(i, i ^ (2 * k)) for i in range(n_head)])
         total = total + got.astype(jnp.float32)
     return total.astype(jnp.bfloat16)
 
@@ -207,9 +208,9 @@
         if c < CHUNKS - 1:
             outs.append(lax.psum_scatter(projected, "head", scatter_dimension=0, tiled=True))
         else:
-            held = core_step(projected, n_head, piece)
-            *outs, held = lax.optimization_barrier((*outs, held))
-            outs.append(chip_step(held, n_head))
+            held, sent = core_step(projected, n_head, piece)
+            *outs, held, sent = lax.optimization_barrier((*outs, held, sent))
+            outs.append(chip_step(held, sent, n_head))
     return jnp.concatenate(outs, axis=0)
 
 

time: 195 us -> 195 us (level)
  Pallas kernels: 15.8 us -> 13.5 us
  waiting for transfers between devices: 133 us -> 135 us
    pallas_call x2, Pallas kernels: 15.8 us -> 13.5 us  [attention(): pl.pallas_call(kernel, out_shape=jax.ShapeDtypeStruct((rows, width), jnp....]
    convert_element_type x0 -> x1, other arithmetic: none -> 2.24 us  [core_step(): return (summed, summed.astype(jnp.bfloat16))]
  transfers between devices with their start and end apart: 7 -> 7, of which waited for: 6 -> 6; matrix products, arithmetic and copies ran while one was open for 3% -> 4% of each run, Pallas kernels for 4% -> 3%
where the time goes in v11:
time: 195 us; the launch traced here: 196 us
  waiting for transfers between devices  135 us (69%)
  between operations  13.6 us (7%)
  Pallas kernels  13.5 us (7%)
  starting transfers between devices  11 us (6%)
  other arithmetic  8.58 us (4%)
  matrix products  7.73 us (4%)
  local copies, waits for them, and re-layouts  6.53 us (3%)
    all_gather x1, waiting for transfers between devices, per_device(): gathered = lax.all_gather(pair, 'xy')  69.3 us
    reduce_scatter x1, waiting for transfers between devices, per_device(): lax.psum_scatter(projected, 'head', scatter_dimension=0, tiled=True)  41.5 us
    ppermute x3, waiting for transfers between devices, chip_step(): lax.ppermute(send, 'head', perm=[(i, i ^ 2 * k) for i in range(n_head)])  15.6 us
    pallas_call x2, Pallas kernels, attention(): pl.pallas_call(kernel, out_shape=jax.ShapeDtypeStruct((rows, width), jnp....  13.5 us
    dot_general x2, matrix products, per_device(): jnp.dot(attended, out_weight, preferred_element_type=jnp.float32)  7.73 us
    ppermute x1, starting transfers between devices, per_device(): partner = lax.ppermute(block, 'zh', perm=[(0, 1), (1, 0)])  7.28 us
    ppermute x1, waiting for transfers between devices, per_device(): partner = lax.ppermute(block, 'zh', perm=[(0, 1), (1, 0)])  6.02 us
  transfers between devices with their start and end apart: 7, of which 6 were waited for; matrix products, arithmetic and copies ran while one was open for 4% of the time, Pallas kernels for 3%

profile of v11, /device:TPU:2, one launch (start us, length us, event | category | flops | bytes accessed | tf_op | source)
XLA Modules:
  0.0 195.7 jit_solution(16207687278934605891)
XLA Ops:
  6.5 0.0 copy-start
  6.5 0.0 all-gather.3.cloned.1.call-start
  6.5 0.8 convert_convert_fusion
  7.3 1.0 copy.27
  8.3 0.9 fusion.4
  9.3 7.3 %collective-permute-start = (bf16[392,256]{1,0:T(8,128)(2,1)S(1)}, bf16[392,256]{1,0:T(8,128)(2,1)S(1)}, u32[]{:S(2)}, u32[]{:S(2)}) collective-permute-start(bf16[392,256]{1,0:T(8,128)(2,1)S(1)} %get-tuple-element.33), channel_id=1, source_target_pairs={{0,128},{128,0},{1,129},{129,1},{2,130},{130,2},{3,131},{131,3},{4... | collective-permute-start | bytes 602120 | tf_op jit(solution)/shard_map/ppermute | solution.py:172
  16.5 6.0 %collective-permute-done = bf16[392,256]{1,0:T(8,128)(2,1)S(1)} collective-permute-done((bf16[392,256]{1,0:T(8,128)(2,1)S(1)}, bf16[392,256]{1,0:T(8,128)(2,1)S(1)}, u32[]{:S(2)}, u32[]{:S(2)}) %collective-permute-start) | collective-permute-done | bytes 200736 | tf_op jit(solution)/shard_map/ppermute | solution.py:172
  22.6 0.8 pad_maximum_fusion
  23.3 0.0 all-gather.3.cloned.1.call-update
  23.4 0.0 reduce-scatter.2.cloned.1.call-start
  23.4 0.1 pad.9.clone
  23.5 1.8 fusion.6
  25.3 69.3 %all-gather.3.cloned.1.call-done = bf16[32,392,256]{2,1,0:T(8,128)(2,1)} async-done(((bf16[2,392,256]{2,1,0:T(8,128)(2,1)}), bf16[32,392,256]{2,1,0:T(8,128)(2,1)}) %all-gather.3.cloned.1.call-update) | async-done | bytes 6422544 | tf_op jit(solution)/shard_map/all_gather | solution.py:174
  94.6 0.9 slice_convert_fusion
  95.5 0.7 convert_reduce_fusion
  96.2 0.0 copy-done
  96.2 0.1 select_reduce_fusion
  96.3 0.1 convert_element_type.60
  96.4 0.1 and_reduce_fusion
  96.5 0.2 divide_reduce_fusion
  96.7 0.1 add_add_fusion.1
  96.8 0.1 copy.28
  96.9 0.6 reshape.126.sc_ref
  97.5 0.8 broadcast_in_dim.5.qp_ref
  98.3 0.8 broadcast_in_dim.4.qs_ref
  99.1 6.7 %shard_map.55 = bf16[192,512]{1,0:T(8,128)(2,1)} custom-call(s32[8]{0:T(128)} %reshape.126.sc_ref, bf16[192,512]{1,0:T(8,128)(2,1)} %bitcast.62, bf16[16,2,392,256]{3,2,1,0:T(8,128)(2,1)} %bitcast.54, bf16[16,2,392,256]{3,2,1,0:T(8,128)(2,1)} %bitcast.55, s32[8,2,24,128]{3,2,1,0:T(8,128)} %broadcast_in_dim.4.qs_ref, ...), custom_call_target="tpu_custom_call" | custom-call | flops 2717908992 | bytes 3932160 | tf_op jit(solution)/shard_map/pallas_call | solution.py:108
  105.9 4.4 %convolution_convert_fusion.1.after_ref = bf16[192,4096]{1,0:T(8,128)(2,1)} fusion(bf16[192,512]{1,0:T(8,128)(2,1)} %shard_map.55, bf16[512,4096]{1,0:T(8,128)(2,1)} %param.11), kind=kOutput, calls=%fused_computation.1 | convolution fusion | flops 806092800 | bytes 5963776 | tf_op jit(solution)/shard_map/dot_general | solution.py:206
  110.3 0.0 reduce-scatter.2.cloned.1.call-update
  110.3 6.7 %shard_map.56 = bf16[192,512]{1,0:T(8,128)(2,1)} custom-call(s32[8]{0:T(128)} %reshape.126.sc_ref, bf16[192,512]{1,0:T(8,128)(2,1)} %bitcast.61, bf16[16,2,392,256]{3,2,1,0:T(8,128)(2,1)} %bitcast.57, bf16[16,2,392,256]{3,2,1,0:T(8,128)(2,1)} %bitcast.58, s32[8,2,24,128]{3,2,1,0:T(8,128)} %broadcast_in_dim.4.qs_ref, ...), custom_call_target="tpu_custom_call" | custom-call | flops 2717908992 | bytes 3932160 | tf_op jit(solution)/shard_map/pallas_call | solution.py:108
  117.1 3.3 %convolution_convert_fusion = bf16[192,4096]{1,0:T(8,128)(2,1)S(1)} fusion(bf16[192,512]{1,0:T(8,128)(2,1)} %shard_map.56, bf16[512,4096]{1,0:T(8,128)(2,1)} %param.11), kind=kOutput, calls=%fused_computation | convolution fusion | flops 806092800 | bytes 5963776 | tf_op jit(solution)/shard_map/dot_general | solution.py:206
  120.4 0.1 dynamic-slice_bitcast_fusion
  120.5 0.1 collective-permute-start.1
  120.6 2.4 %collective-permute-done.1 = bf16[4,24,4096]{2,1,0:T(8,128)(2,1)} collective-permute-done((bf16[4,24,4096]{2,1,0:T(8,128)(2,1)S(1)}, bf16[4,24,4096]{2,1,0:T(8,128)(2,1)}, u32[]{:S(2)}, u32[]{:S(2)}) %collective-permute-start.1) | collective-permute-done | bytes 786464 | tf_op jit(solution)/shard_map/ppermute | solution.py:144
  123.0 2.2 %fusion.5 = (bf16[4,24,4096]{2,1,0:T(8,128)(2,1)}, f32[4,24,4096]{2,1,0:T(8,128)S(1)}) fusion(bf16[4,24,4096]{2,1,0:T(8,128)(2,1)} %collective-permute-done.1, bf16[4,2,24,4096]{3,2,1,0:T(8,128)(2,1)S(1)} %bitcast.60, s32[]{:T(128)S(6)} %select_n.46), kind=kLoop, calls=%fused_computation.28 | loop fusion | flops 1572864 | bytes 3932164 | tf_op jit(solution)/shard_map/convert_element_type | solution.py:146
  125.2 41.5 %reduce-scatter.2.cloned.1.call-done = bf16[24,4096]{1,0:T(8,128)(2,1)} async-done(((bf16[192,4096]{1,0:T(8,128)(2,1)}), bf16[24,4096]{1,0:T(8,128)(2,1)}) %reduce-scatter.2.cloned.1.call-update) | async-done | bytes 196624 | tf_op jit(solution)/shard_map/reduce_scatter | solution.py:209
  166.7 1.2 dynamic-slice_bitcast_fusion.3
  167.8 0.1 collective-permute-start.2
  167.9 0.1 collective-permute-start.4
  168.0 3.4 %collective-permute-start.3 = (bf16[24,4096]{1,0:T(8,128)(2,1)S(1)}, bf16[24,4096]{1,0:T(8,128)(2,1)S(1)}, u32[]{:S(2)}, u32[]{:S(2)}) collective-permute-start(bf16[24,4096]{1,0:T(8,128)(2,1)S(1)} %get-tuple-element.29), channel_id=1, source_target_pairs={{0,4},{1,5},{2,6},{3,7},{4,0},{5,1},{6,2},{7,3},{8,12},{9,13},{10,... | collective-permute-start | bytes 589832 | tf_op jit(solution)/shard_map/ppermute | solution.py:154
  171.4 7.2 %collective-permute-done.2 = bf16[24,4096]{1,0:T(8,128)(2,1)S(1)} collective-permute-done((bf16[24,4096]{1,0:T(8,128)(2,1)S(1)}, bf16[24,4096]{1,0:T(8,128)(2,1)S(1)}, u32[]{:S(2)}, u32[]{:S(2)}) %collective-permute-start.2) | collective-permute-done | bytes 196640 | tf_op jit(solution)/shard_map/ppermute | solution.py:154
  178.6 0.0 collective-permute-done.4
  178.6 8.4 %collective-permute-done.3 = bf16[24,4096]{1,0:T(8,128)(2,1)S(1)} collective-permute-done((bf16[24,4096]{1,0:T(8,128)(2,1)S(1)}, bf16[24,4096]{1,0:T(8,128)(2,1)S(1)}, u32[]{:S(2)}, u32[]{:S(2)}) %collective-permute-start.3) | collective-permute-done | bytes 196640 | tf_op jit(solution)/shard_map/ppermute | solution.py:154
  187.0 0.1 fusion.2
  187.1 1.7 pad_maximum_fusion.1
  (6 shorter events, 0.0 us)
Async XLA Ops:
  6.5 89.7 %copy-start = (s32[384]{0:T(512)S(1)}, s32[384]{0:T(512)}, u32[]{:S(2)}) copy-start(s32[384]{0:T(512)} %param.10) | copy-start | bytes 4612
  6.5 88.1 %all-gather.3.cloned.1.call-start = ((), (), s32[]{:S(2)}) async-start(), calls=%async_computation.2 | async-start | bytes 6823936 | tf_op jit(solution)/shard_map/all_gather | solution.py:174
  9.3 13.3 %collective-permute-start = (bf16[392,256]{1,0:T(8,128)(2,1)S(1)}, bf16[392,256]{1,0:T(8,128)(2,1)S(1)}, u32[]{:S(2)}, u32[]{:S(2)}) collective-permute-start(bf16[392,256]{1,0:T(8,128)(2,1)S(1)} %get-tuple-element.33), channel_id=1, source_target_pairs={{0,128},{128,0},{1,129},{129,1},{2,130},{130,2},{3,131},{131,3},{4... | collective-permute-start | bytes 602120 | tf_op jit(solution)/shard_map/ppermute | solution.py:172
  23.4 143.3 %reduce-scatter.2.cloned.1.call-start = ((), (), s32[]{:S(2)}) async-start(), calls=%async_computation.1 | async-start | bytes 1769472 | tf_op jit(solution)/shard_map/reduce_scatter | solution.py:209
  120.5 2.5 %collective-permute-start.1 = (bf16[4,24,4096]{2,1,0:T(8,128)(2,1)S(1)}, bf16[4,24,4096]{2,1,0:T(8,128)(2,1)}, u32[]{:S(2)}, u32[]{:S(2)}) collective-permute-start(bf16[4,24,4096]{2,1,0:T(8,128)(2,1)S(1)} %dynamic-slice_bitcast_fusion), channel_id=1, source_target_pairs={{0,1},{1,0},{2,3},{3,2},{4,5},{5,4},{6,7},{7,6},{8,9},{9,8},{10,11... | collective-permute-start | bytes 2359304 | tf_op jit(solution)/shard_map/ppermute | solution.py:144
  167.8 10.8 %collective-permute-start.2 = (bf16[24,4096]{1,0:T(8,128)(2,1)S(1)}, bf16[24,4096]{1,0:T(8,128)(2,1)S(1)}, u32[]{:S(2)}, u32[]{:S(2)}) collective-permute-start(bf16[24,4096]{1,0:T(8,128)(2,1)S(1)} %get-tuple-element.27), channel_id=1, source_target_pairs={{0,2},{1,3},{2,0},{3,1},{4,6},{5,7},{6,4},{7,5},{8,10},{9,11},{10,... | collective-permute-start | bytes 589832 | tf_op jit(solution)/shard_map/ppermute | solution.py:154
  167.9 10.7 %collective-permute-start.4 = (bf16[24,4096]{1,0:T(8,128)(2,1)S(1)}, bf16[24,4096]{1,0:T(8,128)(2,1)S(1)}, u32[]{:S(2)}, u32[]{:S(2)}) collective-permute-start(bf16[24,4096]{1,0:T(8,128)(2,1)S(1)} %get-tuple-element.28), channel_id=1, source_target_pairs={{0,6},{1,7},{2,4},{3,5},{4,2},{5,3},{6,0},{7,1},{8,14},{9,15},{10,... | collective-permute-start | bytes 589832 | tf_op jit(solution)/shard_map/ppermute | solution.py:154
  168.0 19.0 %collective-permute-start.3 = (bf16[24,4096]{1,0:T(8,128)(2,1)S(1)}, bf16[24,4096]{1,0:T(8,128)(2,1)S(1)}, u32[]{:S(2)}, u32[]{:S(2)}) collective-permute-start(bf16[24,4096]{1,0:T(8,128)(2,1)S(1)} %get-tuple-element.29), channel_id=1, source_target_pairs={{0,4},{1,5},{2,6},{3,7},{4,0},{5,1},{6,2},{7,3},{8,12},{9,13},{10,... | collective-permute-start | bytes 589832 | tf_op jit(solution)/shard_map/ppermute | solution.py:154
Sparse Core Ops, SparseCore 0:
  23.5 71.0 all-gather.2
  110.4 56.1 reduce-scatter.1
